TPU v7x, 256 devices: a whole 4x4x8 slice. The times are simulated.
256 devices in a mesh: corpus: 32 (over z, x), group: 8 (over y, core).
Axes of the slice: x: 4, y: 4, z: 8, core: 2. Of those that a mesh axis runs over, the one named last changes fastest.
Arguments:
- embeddings: float32 [196608, 768], P(('corpus', 'group')), may hold values from -150 to 150
- labels: int32 [196608, 1], P(('corpus', 'group')), may hold values from 0 to 255, as said below
- neighbours: int32 [256], replicated, may hold values from 0 to 255, as said below
Outputs:
- dup_score: float32 [196608], P(('corpus', 'group'))
- typical: float32 [196608], P(('corpus', 'group'))
Inputs may be any that keep to these rules, and one draw needn't show every extreme that they name: `labels`: in the rows of one device no cluster is named by more than 6 rows, and some cluster by exactly 6; every cluster is named by some row. `neighbours`: each cluster is the neighbour of exactly one cluster, and never its own.
All inputs are finite; a program needn't handle non-finite values.
Results may differ from a plain program's by a relative error of at most 0.0013.
Values may be sent and summed in bfloat16 or wider, within the bound.
No kernel may reach another device: no remote copies, remote signals or barrier semaphores. Data moves between devices by JAX's collectives and lax.ppermute only.
A program may use at most 128 MiB of HBM per device.

v0:
```python
import math

import jax
import jax.numpy as jnp
from jax import lax
from jax.sharding import PartitionSpec as P

MOST = 6


SHARPNESS = 16.0
TYPICAL_SCALE = 8.0
EPSILON = 1e-06


def normalize(values):
    return values * lax.rsqrt(jnp.sum(values * values, axis=-1, keepdims=True) + EPSILON)


def lookup(lookup_table, positions):
    table_ids = jnp.arange(lookup_table.shape[0], dtype=jnp.int32)
    matches = positions[:, None] == table_ids[None, :]
    return jnp.sum(
        jnp.where(matches, lookup_table[None, :], jnp.zeros_like(lookup_table)[None, :]), axis=1
    )


def fill_slots(unit_embed, positions, slot_total):
    row_ids = jnp.arange(unit_embed.shape[0], dtype=jnp.int32)
    source = jnp.full((slot_total,), -1, jnp.int32).at[positions].set(row_ids)
    present = source >= 0
    picked = jnp.take(unit_embed, jnp.maximum(source, 0), axis=0)
    picked = jnp.where(present[:, None], picked, jnp.zeros_like(picked))
    return (picked, present.astype(jnp.bfloat16))


def pair_sums(block_rows, col_rows, col_mask, distinct):
    similarity = lax.dot_general(
        block_rows, col_rows, (((1,), (1,)), ((), ())), preferred_element_type=jnp.float32
    )
    weights = jnp.exp(SHARPNESS * similarity) * col_mask.astype(jnp.float32)[None, :]
    if distinct is not None:
        weights = jnp.where(distinct, weights, 0.0)
    return jnp.sum(weights, axis=1)


def body(embeddings, labels, neighbours):
    corpus_size = lax.axis_size("corpus")
    group_size = lax.axis_size("group")
    row_count, feature_width = embeddings.shape
    clusters = neighbours.shape[0]
    per_owner = clusters // corpus_size
    per_device = clusters // (corpus_size * group_size)
    slot_total = clusters * MOST
    unit_embed = normalize(embeddings).astype(jnp.bfloat16)
    row_label = labels[:, 0]
    cluster_ids = jnp.arange(clusters, dtype=jnp.int32)
    previous = jnp.sum(
        jnp.where(neighbours[None, :] == cluster_ids[:, None], cluster_ids[None, :], 0), axis=1
    )
    row_ids = jnp.arange(row_count, dtype=jnp.int32)
    before = (row_label[None, :] == row_label[:, None]) & (row_ids[None, :] < row_ids[:, None])
    row_slot = jnp.sum(before.astype(jnp.int32), axis=1)
    near_label = lookup(previous, row_label)
    own_owner = row_label // per_owner
    own_rank = row_label % per_owner
    near_owner = near_label // per_owner
    near_rank = near_label % per_owner
    corpus_at = lax.axis_index("corpus")
    group_at = lax.axis_index("group")
    member_hot = (row_label[:, None] == cluster_ids[None, :]).astype(jnp.bfloat16)
    cluster_sums = lax.dot_general(
        member_hot, unit_embed, (((0,), (0,)), ((), ())), preferred_element_type=jnp.float32
    )
    local_counts = jnp.sum(member_hot, axis=0, dtype=jnp.float32)
    cluster_sums, counts = lax.psum((cluster_sums, local_counts), ("corpus", "group"))
    centroid = normalize(cluster_sums)
    typical_rows = TYPICAL_SCALE * jnp.sum(
        unit_embed * jnp.take(centroid, row_label, axis=0), axis=1
    )

    def slot_of(owner_at, rank_at):
        return (
            (owner_at * group_size + rank_at % group_size) * per_device + rank_at // group_size
        ) * MOST + row_slot

    member_buf, member_mask = fill_slots(unit_embed, slot_of(own_owner, own_rank), slot_total)
    near_buf, near_mask = fill_slots(unit_embed, slot_of(near_owner, near_rank), slot_total)
    shape_rows = (corpus_size, group_size, per_device, MOST, feature_width)
    shape_mask = (corpus_size, group_size, per_device, MOST)
    arrived = (
        lax.all_to_all(
            lax.all_to_all(
                member_buf.reshape(shape_rows), "corpus", split_axis=0, concat_axis=3, tiled=True
            ),
            "group",
            split_axis=1,
            concat_axis=3,
            tiled=True,
        ),
        lax.all_to_all(
            lax.all_to_all(
                near_buf.reshape(shape_rows), "corpus", split_axis=0, concat_axis=3, tiled=True
            ),
            "group",
            split_axis=1,
            concat_axis=3,
            tiled=True,
        ),
        lax.all_to_all(
            lax.all_to_all(
                member_mask.reshape(shape_mask), "corpus", split_axis=0, concat_axis=3, tiled=True
            ),
            "group",
            split_axis=1,
            concat_axis=3,
            tiled=True,
        ),
        lax.all_to_all(
            lax.all_to_all(
                near_mask.reshape(shape_mask), "corpus", split_axis=0, concat_axis=3, tiled=True
            ),
            "group",
            split_axis=1,
            concat_axis=3,
            tiled=True,
        ),
    )
    cluster_span = group_size * corpus_size * MOST
    member_rows = arrived[0].reshape(per_device, cluster_span, feature_width)
    other_rows = arrived[1].reshape(per_device, cluster_span, feature_width)
    member_valid = arrived[2].reshape(per_device, cluster_span)
    other_valid = arrived[3].reshape(per_device, cluster_span)
    mine = corpus_at * per_owner + jnp.arange(per_device, dtype=jnp.int32) * group_size + group_at
    own_count = lookup(counts, mine)
    near_count = lookup(counts, lookup(neighbours, mine))
    block_size = math.gcd(cluster_span, 1024)
    col_ids = jnp.arange(cluster_span, dtype=jnp.int32)

    def one_cluster(cluster_item):
        members, others, member_flags, other_flags, count_own, count_near = cluster_item

        def one_block(first_row):
            block_rows = lax.dynamic_slice_in_dim(members, first_row, block_size, 0)
            distinct = (first_row + jnp.arange(block_size, dtype=jnp.int32))[:, None] != col_ids[
                None, :
            ]
            return (
                pair_sums(block_rows, members, member_flags, distinct),
                pair_sums(block_rows, others, other_flags, None),
            )

        own_sum, near_sum = lax.map(
            one_block, jnp.arange(cluster_span // block_size, dtype=jnp.int32) * block_size
        )
        return jnp.log(
            1.0
            + own_sum.reshape(cluster_span) / count_own
            + near_sum.reshape(cluster_span) / count_near
        )

    scores = lax.map(
        one_cluster, (member_rows, other_rows, member_valid, other_valid, own_count, near_count)
    )
    payload = scores[None]
    layers = payload.shape[0]
    payload = payload.reshape(layers, 1, per_device, group_size, corpus_size, MOST)
    returned = lax.all_to_all(
        lax.all_to_all(payload, "corpus", split_axis=4, concat_axis=1, tiled=True),
        "group",
        split_axis=3,
        concat_axis=4,
        tiled=True,
    )
    returned = returned.reshape(layers, slot_total)
    home_slot = (
        (own_owner * per_device + own_rank // group_size) * group_size + own_rank % group_size
    ) * MOST + row_slot
    dup_score = jnp.take(returned[0], home_slot)
    return (dup_score, typical_rows)


def solution(mesh):
    placed = (P(("corpus", "group"), None), P(("corpus", "group"), None), P())
    return jax.shard_map(
        body,
        mesh=mesh,
        in_specs=placed,
        out_specs=(P(("corpus", "group")), P(("corpus", "group"))),
        check_vma=False,
    )
```

profile of v0, /device:TPU:1, one launch (start us, length us, event | category | flops | bytes accessed | tf_op | source)
XLA Modules:
  0.0 593.5 jit_solution(3198293003437910147)
XLA Ops:
  10.1 1.9 fusion.28
  12.7 3.4 scatter_custom_fusion.1
  17.5 12.0 %all-to-all-start.6 = ((bf16[32,8,1,6]{3,1,2,0:T(8,128)(2,1)}), bf16[32,8,1,6]{3,1,2,0:T(8,128)(2,1)}, u32[]{:S(2)}, u32[]{:S(2)}) async-start(bf16[32,8,1,6]{3,1,2,0:T(8,128)(2,1)} %bitcast.11), calls=%async_computation.6 | async-start | bytes 131072 | tf_op jit(solution)/shard_map/all_to_all | solution.py:120
  29.5 1.9 multiply_reduce_fusion.1
  32.2 3.5 scatter_custom_fusion
  36.3 1.5 reshape.324
  38.3 8.8 %all-to-all-start.2 = ((bf16[32,8,1,6]{3,1,2,0:T(8,128)(2,1)}), bf16[32,8,1,6]{3,1,2,0:T(8,128)(2,1)}, u32[]{:S(2)}, u32[]{:S(2)}) async-start(bf16[32,8,1,6]{3,1,2,0:T(8,128)(2,1)} %bitcast.58), calls=%async_computation.2 | async-start | bytes 131072 | tf_op jit(solution)/shard_map/all_to_all | solution.py:111
  48.3 1.6 copy.45
  51.4 1.6 all_to_all.126
  52.9 2.9 all-to-all-done.2
  55.9 7.1 %all-to-all-start.7 = ((bf16[1,8,1,192]{3,2,0,1:T(2,128)(2,1)}), bf16[1,8,1,192]{3,2,0,1:T(2,128)(2,1)}, u32[]{:S(2)}, u32[]{:S(2)}) async-start(bf16[1,8,1,192]{3,2,0,1:T(2,128)(2,1)} %all_to_all.126), calls=%async_computation.7 | async-start | bytes 16384 | tf_op jit(solution)/shard_map/all_to_all | solution.py:119
  64.3 5.7 gather_fusion.3
  70.0 1.6 copy.39
  73.1 1.6 all_to_all.125
  74.6 4.8 all-to-all-start.3
  79.4 3.4 select_select_fusion
  82.8 5.0 reshape.320
  87.8 3.9 copy.42
  91.7 5.5 all-to-all-start.4
  97.2 5.7 gather_fusion.2
  103.0 3.4 select_select_fusion.1
  106.3 5.0 reshape.317
  111.4 3.9 copy.36
  115.3 35.8 %all-to-all-done.4 = bf16[32,8,1,6,768]{4,1,3,2,0:T(8,128)(2,1)} async-done(((bf16[32,8,1,6,768]{4,1,3,2,0:T(8,128)(2,1)}), bf16[32,8,1,6,768]{4,1,3,2,0:T(8,128)(2,1)}, u32[]{:S(2)}, u32[]{:S(2)}) %all-to-all-start.4) | async-done | bytes 2359328 | tf_op jit(solution)/shard_map/all_to_all | solution.py:102
  151.2 7.6 %all-to-all-start = ((bf16[32,8,1,6,768]{4,1,3,2,0:T(8,128)(2,1)}), bf16[32,8,1,6,768]{4,1,3,2,0:T(8,128)(2,1)}, u32[]{:S(2)}, u32[]{:S(2)}) async-start(bf16[32,8,1,6,768]{4,1,3,2,0:T(8,128)(2,1)} %copy.36), calls=%async_computation | async-start | bytes 4718592 | tf_op jit(solution)/shard_map/all_to_all | solution.py:93
  158.7 3.5 copy.43
  162.2 50.3 %all-to-all-done = bf16[32,8,1,6,768]{4,1,3,2,0:T(8,128)(2,1)} async-done(((bf16[32,8,1,6,768]{4,1,3,2,0:T(8,128)(2,1)}), bf16[32,8,1,6,768]{4,1,3,2,0:T(8,128)(2,1)}, u32[]{:S(2)}, u32[]{:S(2)}) %all-to-all-start) | async-done | bytes 2359328 | tf_op jit(solution)/shard_map/all_to_all | solution.py:93
  212.5 7.1 %all-to-all-start.5 = ((bf16[1,8,1,192,768]{4,3,2,0,1:T(8,128)(2,1)}), bf16[1,8,1,192,768]{4,3,2,0,1:T(8,128)(2,1)}, u32[]{:S(2)}, u32[]{:S(2)}) async-start(bf16[1,8,1,192,768]{4,3,2,0,1:T(8,128)(2,1)} %copy.43), calls=%async_computation.5 | async-start | bytes 4718592 | tf_op jit(solution)/shard_map/all_to_all | solution.py:101
  219.6 3.5 copy.37
  223.1 25.8 %all-to-all-done.5 = bf16[1,8,1,192,768]{4,3,2,0,1:T(8,128)(2,1)} async-done(((bf16[1,8,1,192,768]{4,3,2,0,1:T(8,128)(2,1)}), bf16[1,8,1,192,768]{4,3,2,0,1:T(8,128)(2,1)}, u32[]{:S(2)}, u32[]{:S(2)}) %all-to-all-start.5) | async-done | bytes 2359328 | tf_op jit(solution)/shard_map/all_to_all | solution.py:101
  248.9 5.1 all-to-all-start.1
  254.0 1.6 fusion.14
  258.5 91.5 %psum.14 = f32[256]{0:T(256)S(1)} all-reduce(f32[256]{0:T(256)S(1)} %convert_reduce_fusion.1), channel_id=1, replica_groups=mesh['corpus'=32,'group'=8] {'corpus','group'}, use_global_device_ids=true, to_apply=%region_11.13 | all-reduce | flops 256 | bytes 2048 | tf_op jit(solution)/shard_map/psum | solution.py:76
  353.7 161.5 %all-reduce.2.cloned.1.call-done = f32[256,768]{1,0:T(8,128)} async-done(((f32[256,768]{1,0:T(8,128)}), f32[256,768]{1,0:T(8,128)}) %all-reduce.2.cloned.1.call-update) | async-done | bytes 786448 | tf_op jit(solution)/shard_map/psum | solution.py:76
  516.5 31.4 %while.21 = (s32[]{:T(128)}, f32[3,512]{1,0:T(4,128)S(1)}, f32[3,512]{1,0:T(4,128)S(1)}, s32[3]{0:T(128)S(1)}, bf16[1536,768]{1,0:T(8,128)(2,1)}, /*index=5*/bf1...) while((s32[]{:T(128)}, f32[3,512]{1,0:T(4,128)S(1)}, ...), condition=%wide.region_9.11_spmd.clone, body=%wide.region_6.10_spmd.clone.sunk | while | flops 2422213120 | bytes 6338743 | solution.py:153
  519.7 3.5 fusion.45
  523.2 3.6 fusion.44
  530.1 3.5 fusion.45
  533.7 3.6 fusion.44
  540.6 3.5 fusion.45
  544.2 3.6 fusion.44
  550.1 9.5 %all-to-all-start.8 = ((f32[1,1,1,8,32,6]{3,2,5,1,0,4:T(1,128)}), f32[1,1,1,8,32,6]{3,2,5,1,0,4:T(1,128)S(1)}, u32[]{:S(2)}, u32[]{:S(2)}) async-start(f32[1,1,1,8,32,6]{3,2,5,1,0,4:T(1,128)} %copy.48), calls=%async_computation.8 | async-start | bytes 196608 | tf_op jit(solution)/shard_map/all_to_all | solution.py:169
  560.8 3.5 gather_fusion.1
  564.3 4.4 all-to-all-done.8
  570.7 5.3 all-to-all-start.9
  576.0 2.2 multiply_reduce_fusion
  578.2 2.4 all-to-all-done.9
  581.6 4.5 gather_fusion
  (77 shorter events, 31.3 us)
Async XLA Ops:
  7.2 24.2 %copy-start = (f32[768,768]{1,0:T(8,128)S(1)}, f32[768,768]{1,0:T(8,128)}, u32[]{:S(2)}) copy-start(f32[768,768]{1,0:T(8,128)} %param.7) | copy-start | bytes 7077892
  16.1 15.3 %copy-start.1 = (s32[1536]{0:T(1024)}, s32[1536]{0:T(1024)S(1)}, u32[]{:S(2)}) copy-start(s32[1536]{0:T(1024)S(1)} %scatter_custom_fusion.1) | copy-start | bytes 18436
  17.5 20.8 %all-to-all-start.6 = ((bf16[32,8,1,6]{3,1,2,0:T(8,128)(2,1)}), bf16[32,8,1,6]{3,1,2,0:T(8,128)(2,1)}, u32[]{:S(2)}, u32[]{:S(2)}) async-start(bf16[32,8,1,6]{3,1,2,0:T(8,128)(2,1)} %bitcast.11), calls=%async_computation.6 | async-start | bytes 131072 | tf_op jit(solution)/shard_map/all_to_all | solution.py:120
  38.3 17.6 %all-to-all-start.2 = ((bf16[32,8,1,6]{3,1,2,0:T(8,128)(2,1)}), bf16[32,8,1,6]{3,1,2,0:T(8,128)(2,1)}, u32[]{:S(2)}, u32[]{:S(2)}) async-start(bf16[32,8,1,6]{3,1,2,0:T(8,128)(2,1)} %bitcast.58), calls=%async_computation.2 | async-start | bytes 131072 | tf_op jit(solution)/shard_map/all_to_all | solution.py:111
  55.9 18.8 %all-to-all-start.7 = ((bf16[1,8,1,192]{3,2,0,1:T(2,128)(2,1)}), bf16[1,8,1,192]{3,2,0,1:T(2,128)(2,1)}, u32[]{:S(2)}, u32[]{:S(2)}) async-start(bf16[1,8,1,192]{3,2,0,1:T(2,128)(2,1)} %all_to_all.126), calls=%async_computation.7 | async-start | bytes 16384 | tf_op jit(solution)/shard_map/all_to_all | solution.py:119
  74.6 17.1 %all-to-all-start.3 = ((bf16[1,8,1,192]{3,2,0,1:T(2,128)(2,1)}), bf16[1,8,1,192]{3,2,0,1:T(2,128)(2,1)}, u32[]{:S(2)}, u32[]{:S(2)}) async-start(bf16[1,8,1,192]{3,2,0,1:T(2,128)(2,1)} %all_to_all.125), calls=%async_computation.3 | async-start | bytes 16384 | tf_op jit(solution)/shard_map/all_to_all | solution.py:110
  91.7 59.4 %all-to-all-start.4 = ((bf16[32,8,1,6,768]{4,1,3,2,0:T(8,128)(2,1)}), bf16[32,8,1,6,768]{4,1,3,2,0:T(8,128)(2,1)}, u32[]{:S(2)}, u32[]{:S(2)}) async-start(bf16[32,8,1,6,768]{4,1,3,2,0:T(8,128)(2,1)} %copy.42), calls=%async_computation.4 | async-start | bytes 4718592 | tf_op jit(solution)/shard_map/all_to_all | solution.py:102
  151.2 61.4 %all-to-all-start = ((bf16[32,8,1,6,768]{4,1,3,2,0:T(8,128)(2,1)}), bf16[32,8,1,6,768]{4,1,3,2,0:T(8,128)(2,1)}, u32[]{:S(2)}, u32[]{:S(2)}) async-start(bf16[32,8,1,6,768]{4,1,3,2,0:T(8,128)(2,1)} %copy.36), calls=%async_computation | async-start | bytes 4718592 | tf_op jit(solution)/shard_map/all_to_all | solution.py:93
  212.5 36.4 %all-to-all-start.5 = ((bf16[1,8,1,192,768]{4,3,2,0,1:T(8,128)(2,1)}), bf16[1,8,1,192,768]{4,3,2,0,1:T(8,128)(2,1)}, u32[]{:S(2)}, u32[]{:S(2)}) async-start(bf16[1,8,1,192,768]{4,3,2,0,1:T(8,128)(2,1)} %copy.43), calls=%async_computation.5 | async-start | bytes 4718592 | tf_op jit(solution)/shard_map/all_to_all | solution.py:101
  248.9 267.6 %all-to-all-start.1 = ((bf16[1,8,1,192,768]{4,3,2,0,1:T(8,128)(2,1)}), bf16[1,8,1,192,768]{4,3,2,0,1:T(8,128)(2,1)}, u32[]{:S(2)}, u32[]{:S(2)}) async-start(bf16[1,8,1,192,768]{4,3,2,0,1:T(8,128)(2,1)} %copy.37), calls=%async_computation.1 | async-start | bytes 4718592 | tf_op jit(solution)/shard_map/all_to_all | solution.py:92
  254.0 98.0 %copy-start.2 = (s32[768,1]{0,1:T(1,128)S(1)}, s32[768,1]{0,1:T(1,128)}, u32[]{:S(2)}) copy-start(s32[768,1]{0,1:T(1,128)} %param.8) | copy-start | bytes 9220
  254.0 261.2 %all-reduce.2.cloned.1.call-start = ((), (), s32[]{:S(2)}) async-start(), calls=%async_computation.10 | async-start | bytes 1572864 | tf_op jit(solution)/shard_map/psum | solution.py:76
  550.1 18.6 %all-to-all-start.8 = ((f32[1,1,1,8,32,6]{3,2,5,1,0,4:T(1,128)}), f32[1,1,1,8,32,6]{3,2,5,1,0,4:T(1,128)S(1)}, u32[]{:S(2)}, u32[]{:S(2)}) async-start(f32[1,1,1,8,32,6]{3,2,5,1,0,4:T(1,128)} %copy.48), calls=%async_computation.8 | async-start | bytes 196608 | tf_op jit(solution)/shard_map/all_to_all | solution.py:169
  570.7 9.9 %all-to-all-start.9 = ((f32[8,1,192]{2,1,0:T(1,128)}), f32[8,1,192]{2,1,0:T(1,128)S(1)}, u32[]{:S(2)}, u32[]{:S(2)}) async-start(f32[8,1,192]{2,1,0:T(1,128)} %reshape.394), calls=%async_computation.9 | async-start | bytes 16384 | tf_op jit(solution)/shard_map/all_to_all | solution.py:168
Sparse Core Ops, SparseCore 0:
  260.3 254.8 all-reduce.1
where the time goes:
time: 596 us; the launch traced here: 594 us
  waiting for transfers between devices  284 us (48%)
  blocking collectives  91.5 us (15%)
  starting transfers between devices  72.7 us (12%)
  local copies, waits for them, and re-layouts  68.2 us (11%)
  other arithmetic  34.3 us (6%)
  matrix products  23 us (4%)
  between operations  14.3 us (2%)
  loops' own time  5.96 us (1%)
    psum x1, waiting for transfers between devices, body(): lax.psum((cluster_sums, local_counts), ('corpus', 'group'))  161 us
    psum x1, blocking collectives, body(): lax.psum((cluster_sums, local_counts), ('corpus', 'group'))  91.5 us
    all_to_all x1, waiting for transfers between devices, body(): lax.all_to_all(member_buf.reshape(shape_rows), 'corpus', split_axis=0, co...  50.3 us
    all_to_all x1, waiting for transfers between devices, body(): lax.all_to_all(near_buf.reshape(shape_rows), 'corpus', split_axis=0, conc...  35.8 us
    all_to_all x1, waiting for transfers between devices, body(): lax.all_to_all(lax.all_to_all(near_buf.reshape(shape_rows), 'corpus', spl...  25.8 us
    dot_general x6, matrix products, pair_sums(): lax.dot_general(block_rows, col_rows, (((1,), (1,)), ((), ())), preferred...  21.4 us
    all_to_all x1, starting transfers between devices, body(): lax.all_to_all(near_mask.reshape(shape_mask), 'corpus', split_axis=0, con...  12 us
  transfers between devices with their start and end apart: 11, of which 8 were waited for; matrix products, arithmetic and copies ran while one was open for 13% of the time, Pallas kernels for 0%

commit v1 on v0

v1 whole, which is shorter than its diff:
```python
import jax
import jax.numpy as jnp
from jax import lax
from jax.sharding import PartitionSpec as P

MOST = 6


SHARPNESS = 16.0
TYPICAL_SCALE = 8.0
EPSILON = 1e-06
EMPTY = 2.0


def normalize(values):
    return values * lax.rsqrt(jnp.sum(values * values, axis=-1, keepdims=True) + EPSILON)


def body(embeddings, labels, neighbours):
    axes = ("corpus", "group")
    devices = lax.axis_size("corpus") * lax.axis_size("group")
    row_count, feature_width = embeddings.shape
    clusters = neighbours.shape[0]
    per_device = clusters // devices
    slots = 2 * MOST
    unit_embed = normalize(embeddings).astype(jnp.bfloat16)
    row_label = labels[:, 0]
    cluster_ids = jnp.arange(clusters, dtype=jnp.int32)
    previous = jnp.sum(
        jnp.where(neighbours[None, :] == cluster_ids[:, None], cluster_ids[None, :], 0), axis=1
    )
    row_ids = jnp.arange(row_count, dtype=jnp.int32)
    before = (row_label[None, :] == row_label[:, None]) & (row_ids[None, :] < row_ids[:, None])
    row_slot = jnp.sum(before.astype(jnp.int32), axis=1)
    near_label = jnp.take(previous, row_label)

    member_pos = row_label * slots + row_slot
    near_pos = near_label * slots + MOST + row_slot
    slot_total = clusters * slots
    source = jnp.full((slot_total,), -1, jnp.int32)
    source = source.at[member_pos].set(row_ids).at[near_pos].set(row_ids)
    present = source >= 0
    picked = jnp.take(unit_embed, jnp.maximum(source, 0), axis=0)
    send = jnp.where(present[:, None], picked, jnp.asarray(EMPTY, jnp.bfloat16))
    send = send.reshape(devices, per_device * slots, feature_width)
    arrived = lax.all_to_all(send, axes, split_axis=0, concat_axis=0, tiled=True)
    arrived = arrived.reshape(devices, per_device, slots, feature_width)
    cluster_span = devices * MOST

    def one_cluster(rows):
        members = rows[:, :MOST].reshape(cluster_span, feature_width)
        others = rows[:, MOST:].reshape(cluster_span, feature_width)
        member_ok = members[:, 0] < 1.5
        other_ok = others[:, 0] < 1.5
        members = jnp.where(member_ok[:, None], members, jnp.zeros_like(members))
        others = jnp.where(other_ok[:, None], others, jnp.zeros_like(others))
        count_own = jnp.sum(member_ok.astype(jnp.float32))
        count_near = jnp.sum(other_ok.astype(jnp.float32))
        members_f = members.astype(jnp.float32)
        sums = jnp.sum(members_f, axis=0)
        centroid = normalize(sums)
        typical = TYPICAL_SCALE * jnp.sum(members_f * centroid[None, :], axis=1)
        g_own = lax.dot_general(
            members, members, (((1,), (1,)), ((), ())), preferred_element_type=jnp.float32
        )
        g_near = lax.dot_general(
            members, others, (((1,), (1,)), ((), ())), preferred_element_type=jnp.float32
        )
        ids = jnp.arange(cluster_span, dtype=jnp.int32)
        distinct = ids[:, None] != ids[None, :]
        w_own = jnp.where(distinct & member_ok[None, :], jnp.exp(SHARPNESS * g_own), 0.0)
        w_near = jnp.where(other_ok[None, :], jnp.exp(SHARPNESS * g_near), 0.0)
        own_sum = jnp.sum(w_own, axis=1)
        near_sum = jnp.sum(w_near, axis=1)
        score = jnp.log(1.0 + own_sum / count_own + near_sum / count_near)
        return jnp.stack(
            [score.reshape(devices, MOST), typical.reshape(devices, MOST)], axis=1
        )

    results = lax.map(one_cluster, jnp.moveaxis(arrived, 1, 0))
    payload = jnp.moveaxis(results, 1, 0).reshape(devices, per_device * 2 * MOST)
    returned = lax.all_to_all(payload, axes, split_axis=0, concat_axis=0, tiled=True)
    returned = returned.reshape(clusters, 2, MOST)
    dup_score = returned[row_label, 0, row_slot]
    typical_rows = returned[row_label, 1, row_slot]
    return (dup_score, typical_rows)


def solution(mesh):
    placed = (P(("corpus", "group"), None), P(("corpus", "group"), None), P())
    return jax.shard_map(
        body,
        mesh=mesh,
        in_specs=placed,
        out_specs=(P(("corpus", "group")), P(("corpus", "group"))),
        check_vma=False,
    )
```

time: 596 us -> 280 us (0.47)
  waiting for transfers between devices: 284 us -> 0 us
  blocking collectives: 91.5 us -> 178 us
  starting transfers between devices: 72.7 us -> 0 us
  other arithmetic: 34.3 us -> 21.2 us
  matrix products: 23 us -> 10 us
  between operations: 14.3 us -> 1.56 us
  loops' own time: 5.96 us -> 0 us
    all_to_all x0 -> x2, blocking collectives: none -> 178 us  [the longest x1 158 us: body(): lax.all_to_all(send, axes, split_axis=0, concat_axis=0, tiled=True)]
    psum x1 -> x0, waiting for transfers between devices: 161 us -> none  [body(): lax.psum((cluster_sums, local_counts), ('corpus', 'group'))]
    all_to_all x10 -> x0, waiting for transfers between devices: 122 us -> none  [the longest x1 50.3 us: body(): lax.all_to_all(member_buf.reshape(shape_rows), 'corpus', split_axis=0, co...]
    psum x1 -> x0, blocking collectives: 91.5 us -> none  [body(): lax.psum((cluster_sums, local_counts), ('corpus', 'group'))]
    all_to_all x10 -> x0, starting transfers between devices: 72.7 us -> none  [the longest x1 12 us: body(): lax.all_to_all(near_mask.reshape(shape_mask), 'corpus', split_axis=0, con...]
    gather x4 -> x5, local copies, waits for them, and re-layouts: 19.4 us -> 43.1 us  [the longest x2 22.9 us: body(): picked = jnp.take(unit_embed, jnp.maximum(source, 0), axis=0)]
    all_to_all x10 -> x3, local copies, waits for them, and re-layouts: 16.4 us -> 0.2 us  [body(): lax.all_to_all(payload, axes, split_axis=0, concat_axis=0, tiled=True)]
    dot_general x7 -> x2, matrix products: 23 us -> 10 us  [the longest x1 5.63 us: one_cluster(): lax.dot_general(members, members, (((1,), (1,)), ((), ())), preferred_ele...]
  transfers between devices with their start and end apart: 11 -> 0, of which waited for: 8 -> 0; matrix products, arithmetic and copies ran while one was open for 13% -> 0% of each run, Pallas kernels for 0% -> 0%
where the time goes in v1:
time: 280 us; the launch traced here: 279 us
  blocking collectives  178 us (64%)
  local copies, waits for them, and re-layouts  68.6 us (24%)
  other arithmetic  21.2 us (8%)
  matrix products  10 us (4%)
    all_to_all x1, blocking collectives, body(): lax.all_to_all(send, axes, split_axis=0, concat_axis=0, tiled=True)  158 us
    gather x2, local copies, waits for them, and re-layouts, body(): picked = jnp.take(unit_embed, jnp.maximum(source, 0), axis=0)  22.9 us
    all_to_all x1, blocking collectives, body(): lax.all_to_all(payload, axes, split_axis=0, concat_axis=0, tiled=True)  19.9 us
    gather x1, local copies, waits for them, and re-layouts, body(): typical_rows = returned[row_label, 1, row_slot]  7.63 us
    gather x1, local copies, waits for them, and re-layouts, body(): dup_score = returned[row_label, 0, row_slot]  7.61 us
    scatter x2, local copies, waits for them, and re-layouts, body(): source = source.at[member_pos].set(row_ids).at[near_pos].set(row_ids)  6.8 us
    dot_general x1, matrix products, one_cluster(): lax.dot_general(members, members, (((1,), (1,)), ((), ())), preferred_ele...  5.63 us
    select_n x1, other arithmetic, one_cluster(): others = jnp.where(other_ok[:, None], others, jnp.zeros_like(others))  5.61 us

profile of v1, /device:TPU:1, one launch (start us, length us, event | category | flops | bytes accessed | tf_op | source)
XLA Modules:
  0.0 279.0 jit_solution(18382362444739946032)
XLA Ops:
  0.6 0.0 copy-start.6
  0.6 0.8 select_reduce_fusion.2
  1.4 0.7 fusion.9
  2.2 0.4 convert_reduce_fusion.1
  2.5 5.0 %gather_fusion = s32[768]{0:T(1024)S(1)} fusion(s32[256]{0:T(256)S(1)} %select_reduce_fusion.2, s32[1024]{0:T(1024)S(1)} %pad_clamp_fusion), kind=kCustom, calls=%fused_computation | custom fusion | bytes 9216 | tf_op jit(solution)/shard_map/jit(_take)/gather | solution.py:35
  7.5 0.0 copy-done.6
  7.6 0.1 or_reduce_fusion
  7.6 3.4 %scatter_custom_fusion = s32[3072]{0:T(1024)S(1)} fusion(s32[768]{0:T(1024)S(1)} %get-tuple-element.14, s32[768]{0:T(1024)S(1)} %iota.26, s32[]{:T(128)} %constant.38.clone.1), kind=kCustom, calls=%fused_computation.40 | custom fusion | bytes 12292 | tf_op jit(solution)/shard_map/scatter | solution.py:41
  11.0 0.0 copy-start.1
  11.1 3.4 %scatter_fusion = s32[3072]{0:T(1024)S(1)} fusion(s32[3072]{0:T(1024)S(1)} %scatter_custom_fusion, s32[768]{0:T(1024)S(1)} %get-tuple-element.12, s32[768]{0:T(1024)S(1)} %iota.27), kind=kCustom, calls=%fused_computation.5 | custom fusion | bytes 12288 | tf_op jit(solution)/shard_map/scatter | solution.py:41
  14.5 0.6 maximum_clamp_fusion
  15.1 0.0 copy-done.1
  15.1 0.2 multiply_reduce_fusion
  15.3 0.8 broadcast_in_dim.131
  16.1 0.8 broadcast_in_dim.133
  16.9 0.2 multiply_convert_fusion
  17.1 14.6 %gather_fusion.1 = bf16[3072,768]{1,0:T(8,128)(2,1)} fusion(bf16[768,768]{1,0:T(8,128)(2,1)S(1)} %multiply_convert_fusion, s32[3072]{0:T(1024)} %maximum_clamp_fusion), kind=kCustom, calls=%fused_computation.1 | custom fusion | bytes 9449472 | tf_op jit(solution)/shard_map/jit(_take)/gather | solution.py:43
  31.6 8.3 %gather.21 = bf16[256,12,768]{2,1,0:T(8,128)(2,1)} reshape(bf16[3072,768]{1,0:T(8,128)(2,1)} %gather_fusion.1) | data formatting | bytes 9437184 | tf_op jit(solution)/shard_map/jit(_take)/gather | solution.py:43
  39.9 0.0 copy-done.5
  39.9 4.1 %select_select_fusion = bf16[256,12,768]{2,1,0:T(8,128)(2,1)S(1)} fusion(bf16[256,12,768]{2,1,0:T(8,128)(2,1)} %gather.21, pred[256,12]{1,0:T(8,128)(4,1)S(1)} %copy-done.5, pred[256,12]{1,0:T(8,128)(4,1)S(1)} %copy-done.4), kind=kLoop, calls=%fused_computation.15 | loop fusion | flops 4718592 | bytes 9443328 | tf_op jit(solution)/shard_map/jit(_where)/select_n | solution.py:44
  44.1 157.8 %all_to_all.14 = bf16[256,12,768]{2,1,0:T(8,128)(2,1)S(1)} all-to-all(bf16[256,12,768]{2,1,0:T(8,128)(2,1)S(1)} %select_select_fusion), channel_id=1, replica_groups=mesh['corpus'=32,'group'=8] {'corpus','group'}, dimensions={0} | all-to-all | bytes 9437184 | tf_op jit(solution)/shard_map/all_to_all | solution.py:46
  201.9 2.7 copy-done
  204.5 0.9 slice.32
  205.4 2.3 reshape.181
  207.7 1.3 compare_reduce_fusion
  209.0 0.2 broadcast_in_dim.142
  209.2 5.6 %broadcast_select_fusion = (bf16[256,6,768]{2,1,0:T(8,128)(2,1)S(1)}, bf16[256,6,768]{2,1,0:T(8,128)(2,1)}) fusion(pred[256,6]{1,0:T(8,128)(4,1)S(1)} %broadcast_in_dim.142, bf16[256,12,768]{2,1,0:T(8,128)(2,1)} %copy-done), kind=kLoop, calls=%fused_computation.16 | loop fusion | flops 1179648 | bytes 9438720 | tf_op jit(solution)/shard_map/while/body/eval_jaxpr/jit(_where)/select_n | solution.py:56
  214.8 5.1 %reshape.180 = bf16[1536,768]{1,0:T(8,128)(2,1)} reshape(bf16[256,6,768]{2,1,0:T(8,128)(2,1)} %get-tuple-element.20) | data formatting | bytes 4718592 | tf_op jit(solution)/shard_map/while/body/eval_jaxpr/reshape | solution.py:51
  219.9 1.3 compare_reduce_fusion.1
  221.2 0.6 convert_reduce_fusion.2
  221.8 0.2 broadcast_in_dim.138
  222.0 2.3 select_n.90
  224.3 2.6 convert_reduce_fusion
  226.9 0.6 multiply_reduce_fusion.1
  228.2 2.3 select_n.87
  230.4 0.9 fusion.1
  231.3 0.8 copy-done.3
  232.1 5.6 %select_reduce_fusion.1 = f32[1536]{0:T(1024)S(1)} fusion(bf16[1536,768]{1,0:T(8,128)(2,1)S(1)} %copy-done.3, pred[1536]{0:T(1024)(128)(4,1)S(1)} %compare_reduce_fusion.1), kind=kOutput, calls=%fused_computation.9 | convolution fusion | flops 3635673600 | bytes 2366976 | tf_op jit(solution)/shard_map/while/body/eval_jaxpr/dot_general | solution.py:63
  237.7 0.0 copy-done.2
  237.7 4.4 %select_reduce_fusion = f32[1536]{0:T(1024)S(1)} fusion(bf16[1536,768]{1,0:T(8,128)(2,1)S(1)} %copy-done.3, bf16[1536,768]{1,0:T(8,128)(2,1)S(1)} %copy-done.2, pred[1536]{0:T(1024)(128)(4,1)S(1)} %compare_reduce_fusion), kind=kOutput, calls=%fused_computation.8 | convolution fusion | flops 3630955008 | bytes 4726272 | tf_op jit(solution)/shard_map/while/body/eval_jaxpr/dot_general | solution.py:66
  242.1 1.3 add_log_fusion
  243.4 0.1 log.15
  243.6 0.1 copy.18
  243.7 0.1 copy.19
  243.8 19.9 %all_to_all.15 = f32[256,1,12]{2,1,0:T(1,128)S(1)} all-to-all(f32[256,1,12]{2,1,0:T(1,128)S(1)} %copy.19), channel_id=1, replica_groups=mesh['corpus'=32,'group'=8] {'corpus','group'}, dimensions={0} | all-to-all | bytes 24576 | tf_op jit(solution)/shard_map/all_to_all | solution.py:82
  263.7 0.1 copy.20
  263.8 7.6 %gather_fusion.3 = f32[768]{0:T(1024)} fusion(f32[256,2,6]{0,2,1:T(8,128)S(1)} %reshape.182, s32[768]{0:T(1024)S(1)} %get-tuple-element.8), kind=kCustom, calls=%fused_computation.3 | custom fusion | bytes 15360 | tf_op jit(solution)/shard_map/gather | solution.py:85
  271.4 7.6 %gather_fusion.2 = f32[768]{0:T(1024)} fusion(f32[256,2,6]{0,2,1:T(8,128)S(1)} %reshape.182, s32[768]{0:T(1024)S(1)} %get-tuple-element.13), kind=kCustom, calls=%fused_computation.2 | custom fusion | bytes 15360 | tf_op jit(solution)/shard_map/gather | solution.py:84
  (16 shorter events, 0.1 us)
Async XLA Ops:
  0.6 6.9 %copy-start.6 = (s32[768,1]{0,1:T(1,128)S(1)}, s32[768,1]{0,1:T(1,128)}, u32[]{:S(2)}) copy-start(s32[768,1]{0,1:T(1,128)} %param.4) | copy-start | bytes 9220
  11.0 4.0 %copy-start.1 = (f32[768,768]{1,0:T(8,128)S(1)}, f32[768,768]{1,0:T(8,128)}, u32[]{:S(2)}) copy-start(f32[768,768]{1,0:T(8,128)} %param.3) | copy-start | bytes 7077892
  31.6 8.3 %copy-start.4 = (pred[256,12]{1,0:T(8,128)(4,1)S(1)}, pred[256,12]{1,0:T(8,128)(4,1)}, u32[]{:S(2)}) copy-start(pred[256,12]{1,0:T(8,128)(4,1)} %broadcast_in_dim.131) | copy-start | bytes 9220
  31.6 8.3 %copy-start.5 = (pred[256,12]{1,0:T(8,128)(4,1)S(1)}, pred[256,12]{1,0:T(8,128)(4,1)}, u32[]{:S(2)}) copy-start(pred[256,12]{1,0:T(8,128)(4,1)} %broadcast_in_dim.133) | copy-start | bytes 9220
  201.9 2.7 copy-start
  230.4 1.7 copy-start.3
  232.1 5.6 %copy-start.2 = (bf16[1536,768]{1,0:T(8,128)(2,1)S(1)}, bf16[1536,768]{1,0:T(8,128)(2,1)}, u32[]{:S(2)}) copy-start(bf16[1536,768]{1,0:T(8,128)(2,1)} %select_n.90) | copy-start | bytes 7077892

commit v2 on v1

v2 whole, which is shorter than its diff:
```python
import jax
import jax.numpy as jnp
from jax import lax
from jax.sharding import PartitionSpec as P

MOST = 6


SHARPNESS = 16.0
TYPICAL_SCALE = 8.0
EPSILON = 1e-06
EMPTY = 2.0
PIECE = 3


def normalize(values):
    return values * lax.rsqrt(jnp.sum(values * values, axis=-1, keepdims=True) + EPSILON)


def body(embeddings, labels, neighbours):
    axes = ("corpus", "group")
    devices = lax.axis_size("corpus") * lax.axis_size("group")
    row_count, feature_width = embeddings.shape
    clusters = neighbours.shape[0]
    assert clusters == devices
    halves = MOST // PIECE
    pieces = 2 * halves
    piece_rows = clusters * PIECE
    unit_embed = normalize(embeddings).astype(jnp.bfloat16)
    row_label = labels[:, 0]
    cluster_ids = jnp.arange(clusters, dtype=jnp.int32)
    previous = jnp.sum(
        jnp.where(neighbours[None, :] == cluster_ids[:, None], cluster_ids[None, :], 0), axis=1
    )
    row_ids = jnp.arange(row_count, dtype=jnp.int32)
    before = (row_label[None, :] == row_label[:, None]) & (row_ids[None, :] < row_ids[:, None])
    row_slot = jnp.sum(before.astype(jnp.int32), axis=1)
    near_label = jnp.take(previous, row_label)

    within = row_slot % PIECE
    member_pos = (row_slot // PIECE) * piece_rows + row_label * PIECE + within
    near_pos = (halves + row_slot // PIECE) * piece_rows + near_label * PIECE + within
    slot_ids = jnp.arange(pieces * piece_rows, dtype=jnp.int32)
    chosen = (member_pos[None, :] == slot_ids[:, None]) | (near_pos[None, :] == slot_ids[:, None])
    present = jnp.any(chosen, axis=1)
    picked = lax.dot_general(
        chosen.astype(jnp.bfloat16),
        unit_embed,
        (((1,), (0,)), ((), ())),
        preferred_element_type=jnp.float32,
    )
    first = jnp.arange(feature_width, dtype=jnp.int32)[None, :] == 0
    send = jnp.where(first & ~present[:, None], EMPTY, picked).astype(jnp.bfloat16)
    send = send.reshape(pieces, piece_rows, feature_width)
    arrived = lax.all_to_all(send, axes, split_axis=1, concat_axis=1, tiled=True)
    cluster_span = halves * piece_rows
    members = arrived[:halves].reshape(cluster_span, feature_width)
    others = arrived[halves:].reshape(cluster_span, feature_width)
    member_ok = members[:, 0] < 1.5
    other_ok = others[:, 0] < 1.5
    count_own = jnp.sum(member_ok.astype(jnp.float32))
    count_near = jnp.sum(other_ok.astype(jnp.float32))
    sums = lax.dot_general(
        member_ok.astype(jnp.bfloat16)[None, :],
        members,
        (((1,), (0,)), ((), ())),
        preferred_element_type=jnp.float32,
    )
    centroid = normalize(sums)
    typical = TYPICAL_SCALE * jnp.sum(members.astype(jnp.float32) * centroid, axis=1)
    g_own = lax.dot_general(
        members, members, (((1,), (1,)), ((), ())), preferred_element_type=jnp.float32
    )
    g_near = lax.dot_general(
        members, others, (((1,), (1,)), ((), ())), preferred_element_type=jnp.float32
    )
    ids = jnp.arange(cluster_span, dtype=jnp.int32)
    distinct = ids[:, None] != ids[None, :]
    w_own = jnp.where(distinct & member_ok[None, :], jnp.exp(SHARPNESS * g_own), 0.0)
    w_near = jnp.where(other_ok[None, :], jnp.exp(SHARPNESS * g_near), 0.0)
    own_sum = jnp.sum(w_own, axis=1)
    near_sum = jnp.sum(w_near, axis=1)
    score = jnp.log(1.0 + own_sum / count_own + near_sum / count_near)
    payload = jnp.stack([score, typical]).reshape(2 * halves, piece_rows)
    returned = lax.all_to_all(payload, axes, split_axis=1, concat_axis=1, tiled=True)
    returned = returned.reshape(2, cluster_span)
    home = member_pos[:, None] == ids[None, :]
    dup_score = jnp.sum(jnp.where(home, returned[0][None, :], 0.0), axis=1)
    typical_rows = jnp.sum(jnp.where(home, returned[1][None, :], 0.0), axis=1)
    return (dup_score, typical_rows)


def solution(mesh):
    placed = (P(("corpus", "group"), None), P(("corpus", "group"), None), P())
    return jax.shard_map(
        body,
        mesh=mesh,
        in_specs=placed,
        out_specs=(P(("corpus", "group")), P(("corpus", "group"))),
        check_vma=False,
    )
```

time: 280 us -> 199 us (0.71)
  local copies, waits for them, and re-layouts: 68.6 us -> 16.9 us
  blocking collectives: 178 us -> 151 us
  other arithmetic: 21.2 us -> 12.9 us
  matrix products: 10 us -> 16.4 us
    gather x4 -> x0, local copies, waits for them, and re-layouts: 38.1 us -> none  [the longest x2 22.9 us: body(): picked = jnp.take(unit_embed, jnp.maximum(source, 0), axis=0)]
    all_to_all x2, blocking collectives: 178 us -> 151 us  [the longest x1 124 us: body(): lax.all_to_all(send, axes, split_axis=1, concat_axis=1, tiled=True)]
    select_n x3 -> x0, other arithmetic: 10.4 us -> none  [the longest x1 5.61 us: one_cluster(): others = jnp.where(other_ok[:, None], others, jnp.zeros_like(others))]
    scatter x2 -> x0, local copies, waits for them, and re-layouts: 6.8 us -> none  [body(): source = source.at[member_pos].set(row_ids).at[near_pos].set(row_ids)]
    dot_general x2 -> x4, matrix products: 10 us -> 16.4 us  [the longest x1 5.97 us: body(): lax.dot_general(chosen.astype(jnp.bfloat16), unit_embed, (((1,), (0,)), (...]
    select_n x2 -> x0, local copies, waits for them, and re-layouts: 4.58 us -> none  [the longest x1 2.31 us: one_cluster(): others = jnp.where(other_ok[:, None], others, jnp.zeros_like(others))]
    slice x1 -> x4, local copies, waits for them, and re-layouts: 0.92 us -> 4.92 us  [the longest x1 4.67 us: body(): others = arrived[halves:].reshape(cluster_span, feature_width)]
    reshape x3 -> x1, local copies, waits for them, and re-layouts: 7.39 us -> 3.64 us  [body(): send = send.reshape(pieces, piece_rows, feature_width)]
where the time goes in v2:
time: 199 us
  blocking collectives  151 us (76%)
  local copies, waits for them, and re-layouts  16.9 us (8%)
  matrix products  16.4 us (8%)
  other arithmetic  12.9 us (6%)
    all_to_all x1, blocking collectives, body(): lax.all_to_all(send, axes, split_axis=1, concat_axis=1, tiled=True)  124 us
    all_to_all x1, blocking collectives, body(): lax.all_to_all(payload, axes, split_axis=1, concat_axis=1, tiled=True)  26.6 us
    dot_general x1, matrix products, body(): lax.dot_general(chosen.astype(jnp.bfloat16), unit_embed, (((1,), (0,)), (...  5.97 us
    dot_general x1, matrix products, body(): lax.dot_general(members, members, (((1,), (1,)), ((), ())), preferred_ele...  5.64 us
    gather x1, local copies, waits for them, and re-layouts, body(): near_label = jnp.take(previous, row_label)  4.98 us
    slice x1, local copies, waits for them, and re-layouts, body(): others = arrived[halves:].reshape(cluster_span, feature_width)  4.67 us
    dot_general x1, matrix products, body(): lax.dot_general(members, others, (((1,), (1,)), ((), ())), preferred_elem...  4.34 us

profile of v2, /device:TPU:1, one launch (start us, length us, event | category | flops | bytes accessed | tf_op | source)
XLA Modules:
  0.0 198.7 jit_solution(4546644548448086711)
XLA Ops:
  0.6 0.0 copy-start.1
  0.7 0.8 select_reduce_fusion.4
  1.5 0.7 and_reduce_fusion
  2.2 0.7 reduce.3
  2.9 0.4 convert_reduce_fusion
  3.2 1.9 multiply_reduce_fusion.1
  5.1 0.0 copy-start
  5.2 0.0 copy-done.1
  5.2 5.0 %gather_fusion = s32[768]{0:T(1024)S(1)} fusion(s32[256]{0:T(256)S(1)} %select_reduce_fusion.4, s32[1024]{0:T(1024)S(1)} %pad_clamp_fusion), kind=kCustom, calls=%fused_computation | custom fusion | bytes 9216 | tf_op jit(solution)/shard_map/jit(_take)/gather | solution.py:38
  10.2 2.3 %fusion.4 = pred[3072]{0:T(1024)(128)(4,1)S(1)} fusion(s32[768]{0:T(1024)S(1)} %add_add_fusion, s32[768]{0:T(1024)S(1)} %get-tuple-element.6), kind=kLoop, calls=%fused_computation.12 | loop fusion | flops 9434112 | bytes 9216 | tf_op jit(solution)/shard_map/reduce_or | solution.py:45
  12.6 0.0 copy-done
  12.6 6.0 %select_convert_fusion = bf16[3072,768]{1,0:T(8,128)(2,1)S(1)} fusion(pred[768]{0:T(1024)(128)(4,1)S(1)} %iota_compare_fusion.6, pred[3072]{0:T(1024)(128)(4,1)S(1)} %not.8, s32[768]{0:T(1024)S(1)} %add_add_fusion, s32[768]{0:T(1024)S(1)} %get-tuple-element.6, f32[768,768]{1,0:T(8,128)S(1)} %copy-done, f32[768]{0:T(1024)S(1)} %add_rsqrt_fusion), kind=kOutput, calls=%fused_computation.5 | convolution fusion | flops 3639214080 | bytes 7090944 | tf_op jit(solution)/shard_map/dot_general | solution.py:46
  18.6 3.6 %copy.17 = bf16[4,768,768]{2,0,1:T(4,128)(2,1)S(1)} copy(bf16[4,768,768]{2,1,0:T(8,128)(2,1)S(1)} %bitcast.17) | data formatting | bytes 9437184 | tf_op jit(solution)/shard_map/reshape | solution.py:54
  22.2 124.4 %all_to_all.14 = bf16[4,768,768]{2,0,1:T(4,128)(2,1)S(1)} all-to-all(bf16[4,768,768]{2,0,1:T(4,128)(2,1)S(1)} %copy.17), channel_id=1, replica_groups=mesh['corpus'=32,'group'=8] {'corpus','group'}, dimensions={1} | all-to-all | bytes 9437184 | tf_op jit(solution)/shard_map/all_to_all | solution.py:55
  146.6 4.7 %fusion.14 = (bf16[2,768,768]{2,0,1:T(2,128)(2,1)}, bf16[2,768,768]{2,0,1:T(2,128)(2,1)S(1)}) fusion(bf16[4,768,768]{2,0,1:T(4,128)(2,1)S(1)} %all_to_all.14), kind=kLoop, calls=%fused_computation.54 | loop fusion | bytes 9437184 | tf_op jit(solution)/shard_map/slice | solution.py:58
  151.2 2.0 copy.24
  153.2 0.3 compare_reduce_fusion
  153.5 0.3 copy.23
  153.8 0.3 compare_reduce_fusion.1
  154.1 4.3 %select_reduce_fusion = f32[1536]{0:T(1024)S(1)} fusion(bf16[1536,768]{1,0:T(8,128)(2,1)S(1)} %bitcast.14, bf16[1536,768]{1,0:T(8,128)(2,1)S(1)} %bitcast.19, pred[1536]{0:T(1024)(128)(4,1)S(1)} %compare_reduce_fusion), kind=kOutput, calls=%fused_computation.3 | convolution fusion | flops 3630955008 | bytes 4726272 | tf_op jit(solution)/shard_map/dot_general | solution.py:74
  158.4 0.7 convert_reduce_fusion.1
  159.1 5.6 %select_reduce_fusion.1 = f32[1536]{0:T(1024)S(1)} fusion(bf16[1536,768]{1,0:T(8,128)(2,1)S(1)} %bitcast.15, pred[1536]{0:T(1024)(128)(4,1)S(1)} %compare_reduce_fusion.1), kind=kOutput, calls=%fused_computation.4 | convolution fusion | flops 3635673600 | bytes 2366976 | tf_op jit(solution)/shard_map/dot_general | solution.py:71
  164.8 0.4 convolution_reduce_fusion
  165.2 0.6 multiply_reduce_fusion.2
  166.5 1.3 add_log_fusion
  167.9 0.5 multiply_reduce_fusion
  168.5 0.4 all_to_all.10
  168.8 0.3 copy.20
  169.2 26.6 %all_to_all.15 = f32[4,256,3]{2,0,1:T(4,128)S(1)} all-to-all(f32[4,256,3]{2,0,1:T(4,128)S(1)} %copy.20), channel_id=1, replica_groups=mesh['corpus'=32,'group'=8] {'corpus','group'}, dimensions={1} | all-to-all | bytes 24576 | tf_op jit(solution)/shard_map/all_to_all | solution.py:85
  195.8 0.2 fusion.15
  196.0 0.2 broadcast_in_dim.84
  196.2 0.2 broadcast_in_dim.87
  196.4 2.2 %select_reduce_fusion.2 = (f32[768]{0:T(1024)}, f32[768]{0:T(1024)}) fusion(f32[1536]{0:T(1024)S(1)} %broadcast_in_dim.87, s32[768]{0:T(1024)S(1)} %get-tuple-element.4, f32[1536]{0:T(1024)S(1)} %broadcast_in_dim.84), kind=kLoop, calls=%fused_computation.13 | loop fusion | flops 5896704 | bytes 21504 | tf_op jit(solution)/shard_map/reduce_sum | solution.py:89
  (15 shorter events, 0.2 us)
Async XLA Ops:
  0.6 4.5 %copy-start.1 = (s32[768,1]{0,1:T(1,128)S(1)}, s32[768,1]{0,1:T(1,128)}, u32[]{:S(2)}) copy-start(s32[768,1]{0,1:T(1,128)} %param.4) | copy-start | bytes 9220
  5.1 7.5 %copy-start = (f32[768,768]{1,0:T(8,128)S(1)}, f32[768,768]{1,0:T(8,128)}, u32[]{:S(2)}) copy-start(f32[768,768]{1,0:T(8,128)} %param.3) | copy-start | bytes 7077892

commit v3 on v2

--- a/solution.py
+++ b/solution.py
@@ -35,14 +35,24 @@
     row_ids = jnp.arange(row_count, dtype=jnp.int32)
     before = (row_label[None, :] == row_label[:, None]) & (row_ids[None, :] < row_ids[:, None])
     row_slot = jnp.sum(before.astype(jnp.int32), axis=1)
-    near_label = jnp.take(previous, row_label)
+    label_hot = row_label[:, None] == cluster_ids[None, :]
+    near_label = jnp.sum(jnp.where(label_hot, previous[None, :], 0), axis=1)
+    local_count = jnp.sum(label_hot.astype(jnp.int32), axis=0)
+    near_count = jnp.sum(
+        jnp.where(neighbours[:, None] == cluster_ids[None, :], local_count[None, :], 0), axis=1
+    )
 
     within = row_slot % PIECE
-    member_pos = (row_slot // PIECE) * piece_rows + row_label * PIECE + within
-    near_pos = (halves + row_slot // PIECE) * piece_rows + near_label * PIECE + within
+    half = row_slot // PIECE
+    member_pos = (row_label * PIECE + within) * pieces + half
+    near_pos = (near_label * PIECE + within) * pieces + halves + half
     slot_ids = jnp.arange(pieces * piece_rows, dtype=jnp.int32)
     chosen = (member_pos[None, :] == slot_ids[:, None]) | (near_pos[None, :] == slot_ids[:, None])
-    present = jnp.any(chosen, axis=1)
+    slot_piece = slot_ids % pieces
+    slot_rank = (slot_piece % halves) * PIECE + (slot_ids // pieces) % PIECE
+    slot_cluster = slot_ids // (pieces * PIECE)
+    have = jnp.where(slot_piece < halves, local_count[slot_cluster], near_count[slot_cluster])
+    present = have > slot_rank
     picked = lax.dot_general(
         chosen.astype(jnp.bfloat16),
         unit_embed,
@@ -51,7 +61,7 @@
     )
     first = jnp.arange(feature_width, dtype=jnp.int32)[None, :] == 0
     send = jnp.where(first & ~present[:, None], EMPTY, picked).astype(jnp.bfloat16)
-    send = send.reshape(pieces, piece_rows, feature_width)
+    send = send.reshape(piece_rows, pieces, feature_width).transpose(1, 0, 2)
     arrived = lax.all_to_all(send, axes, split_axis=1, concat_axis=1, tiled=True)
     cluster_span = halves * piece_rows
     members = arrived[:halves].reshape(cluster_span, feature_width)
@@ -81,12 +91,16 @@
     own_sum = jnp.sum(w_own, axis=1)
     near_sum = jnp.sum(w_near, axis=1)
     score = jnp.log(1.0 + own_sum / count_own + near_sum / count_near)
-    payload = jnp.stack([score, typical]).reshape(2 * halves, piece_rows)
-    returned = lax.all_to_all(payload, axes, split_axis=1, concat_axis=1, tiled=True)
-    returned = returned.reshape(2, cluster_span)
-    home = member_pos[:, None] == ids[None, :]
-    dup_score = jnp.sum(jnp.where(home, returned[0][None, :], 0.0), axis=1)
-    typical_rows = jnp.sum(jnp.where(home, returned[1][None, :], 0.0), axis=1)
+
+    def by_source(values):
+        return values.reshape(halves, clusters, PIECE).transpose(1, 0, 2).reshape(clusters, MOST)
+
+    payload = jnp.stack([by_source(score), by_source(typical)], axis=1).reshape(clusters, 2 * MOST)
+    returned = lax.all_to_all(payload, axes, split_axis=0, concat_axis=0, tiled=True)
+    returned = returned.reshape(clusters, 2, MOST)
+    home = (row_label * MOST + row_slot)[:, None] == ids[None, :]
+    dup_score = jnp.sum(jnp.where(home, returned[:, 0].reshape(-1)[None, :], 0.0), axis=1)
+    typical_rows = jnp.sum(jnp.where(home, returned[:, 1].reshape(-1)[None, :], 0.0), axis=1)
     return (dup_score, typical_rows)
 
 

time: 199 us -> 231 us (1.16)
  local copies, waits for them, and re-layouts: 16.9 us -> 56.9 us
  blocking collectives: 151 us -> 125 us
  waiting for transfers between devices: 0 us -> 12.9 us
  starting transfers between devices: 0 us -> 6.79 us
  other arithmetic: 12.9 us -> 10.3 us
    gather x1 -> x2, local copies, waits for them, and re-layouts: 4.98 us -> 38.9 us  [the longest x1 19.4 us: body(): local_count[slot_cluster]]
    all_to_all x1 -> x0, blocking collectives: 26.6 us -> none  [body(): lax.all_to_all(payload, axes, split_axis=1, concat_axis=1, tiled=True)]
    all_to_all x0 -> x1, waiting for transfers between devices: none -> 12.9 us  [body(): lax.all_to_all(payload, axes, split_axis=0, concat_axis=0, tiled=True)]
    all_to_all x0 -> x1, starting transfers between devices: none -> 6.79 us  [body(): lax.all_to_all(payload, axes, split_axis=0, concat_axis=0, tiled=True)]
    reshape x1 -> x2, local copies, waits for them, and re-layouts: 3.64 us -> 8.98 us  [the longest x1 8.97 us: body(): send = send.reshape(piece_rows, pieces, feature_width).transpose(1, 0, 2)]
  transfers between devices with their start and end apart: 0 -> 1, of which waited for: 0 -> 1; matrix products, arithmetic and copies ran while one was open for 0% -> 0% of each run, Pallas kernels for 0% -> 0%
where the time goes in v3:
time: 231 us; the launch traced here: 230 us
  blocking collectives  125 us (54%)
  local copies, waits for them, and re-layouts  56.9 us (25%)
  matrix products  17.3 us (7%)
  waiting for transfers between devices  12.9 us (6%)
  other arithmetic  10.3 us (4%)
  starting transfers between devices  6.79 us (3%)
    all_to_all x1, blocking collectives, body(): lax.all_to_all(send, axes, split_axis=1, concat_axis=1, tiled=True)  125 us
    gather x1, local copies, waits for them, and re-layouts, body(): local_count[slot_cluster]  19.4 us
    gather x1, local copies, waits for them, and re-layouts, body(): near_count[slot_cluster]  19.4 us
    all_to_all x1, waiting for transfers between devices, body(): lax.all_to_all(payload, axes, split_axis=0, concat_axis=0, tiled=True)  12.9 us
    reshape x1, local copies, waits for them, and re-layouts, body(): send = send.reshape(piece_rows, pieces, feature_width).transpose(1, 0, 2)  8.97 us
    dot_general x1, matrix products, body(): lax.dot_general(chosen.astype(jnp.bfloat16), unit_embed, (((1,), (0,)), (...  6.9 us
    all_to_all x1, starting transfers between devices, body(): lax.all_to_all(payload, axes, split_axis=0, concat_axis=0, tiled=True)  6.79 us
    dot_general x1, matrix products, body(): lax.dot_general(members, members, (((1,), (1,)), ((), ())), preferred_ele...  5.64 us
  transfers between devices with their start and end apart: 1, of which 1 were waited for; matrix products, arithmetic and copies ran while one was open for 0% of the time, Pallas kernels for 0%

profile of v3, /device:TPU:1, one launch (start us, length us, event | category | flops | bytes accessed | tf_op | source)
XLA Modules:
  0.0 230.4 jit_solution(10316357403071979209)
XLA Ops:
  0.6 0.0 copy-start.2
  0.7 0.8 select_reduce_fusion.5
  1.5 0.7 reduce.3
  2.2 0.4 convert_reduce_fusion
  2.6 1.9 multiply_reduce_fusion.1
  4.5 0.3 select_reduce_fusion.4
  4.8 0.0 copy-done.2
  4.8 0.2 select_reduce_fusion.6
  5.0 19.4 %gather_fusion = s32[3072]{0:T(1024)S(1)} fusion(s32[256]{0:T(256)S(1)} %get-tuple-element.5, s32[3072]{0:T(1024)S(1)} %broadcast_clamp_fusion), kind=kCustom, calls=%fused_computation | custom fusion | bytes 36864 | tf_op jit(solution)/shard_map/gather | solution.py:54
  24.4 0.0 copy-start
  24.5 19.4 %gather_fusion.1 = s32[3072]{0:T(1024)S(1)} fusion(s32[256]{0:T(256)S(1)} %select_reduce_fusion.6, s32[3072]{0:T(1024)S(1)} %broadcast_clamp_fusion), kind=kCustom, calls=%fused_computation.1 | custom fusion | bytes 36864 | tf_op jit(solution)/shard_map/gather | solution.py:54
  43.9 0.0 copy-done
  44.0 6.9 %select_convert_fusion = bf16[3072,768]{1,0:T(8,128)(2,1)} fusion(pred[768]{0:T(1024)(128)(4,1)S(1)} %iota_compare_fusion.9, pred[3072]{0:T(1024)(128)(4,1)S(1)} %fusion.23, s32[768]{0:T(1024)S(1)} %get-tuple-element.11, s32[768]{0:T(1024)S(1)} %get-tuple-element.10, f32[768,768]{1,0:T(8,128)S(1)} %copy-done, f32[768]{0:T(1024)S(1)} %add_rsqrt_fusion), kind=kOutput, calls=%fused_computation.6 | convolution fusion | flops 3639214080 | bytes 7090944 | tf_op jit(solution)/shard_map/dot_general | solution.py:56
  50.9 9.0 %reshape.212 = bf16[768,4,768]{2,1,0:T(4,128)(2,1)} reshape(bf16[3072,768]{1,0:T(8,128)(2,1)} %select_convert_fusion) | data formatting | bytes 9437184 | tf_op jit(solution)/shard_map/reshape | solution.py:64
  59.8 124.6 %all_to_all.14 = bf16[4,768,768]{2,0,1:T(4,128)(2,1)S(1)} all-to-all(bf16[4,768,768]{2,0,1:T(4,128)(2,1)} %bitcast.24), channel_id=1, replica_groups=mesh['corpus'=32,'group'=8] {'corpus','group'}, dimensions={1} | all-to-all | bytes 9437184 | tf_op jit(solution)/shard_map/all_to_all | solution.py:65
  184.4 4.7 %fusion.25 = (bf16[2,768,768]{2,0,1:T(2,128)(2,1)}, bf16[2,768,768]{2,0,1:T(2,128)(2,1)S(1)}) fusion(bf16[4,768,768]{2,0,1:T(4,128)(2,1)S(1)} %all_to_all.14), kind=kLoop, calls=%fused_computation.80 | loop fusion | bytes 9437184 | tf_op jit(solution)/shard_map/slice | solution.py:68
  189.1 2.0 copy.27
  191.0 0.3 compare_reduce_fusion
  191.3 0.3 copy.26
  191.6 0.3 compare_reduce_fusion.1
  191.9 4.3 %select_reduce_fusion = f32[1536]{0:T(1024)S(1)} fusion(bf16[1536,768]{1,0:T(8,128)(2,1)S(1)} %bitcast.26, bf16[1536,768]{1,0:T(8,128)(2,1)S(1)} %bitcast.30, pred[1536]{0:T(1024)(128)(4,1)S(1)} %compare_reduce_fusion), kind=kOutput, calls=%fused_computation.4 | convolution fusion | flops 3630955008 | bytes 4726272 | tf_op jit(solution)/shard_map/dot_general | solution.py:84
  196.3 0.7 convert_reduce_fusion.2
  197.0 5.6 %select_reduce_fusion.1 = f32[1536]{0:T(1024)S(1)} fusion(bf16[1536,768]{1,0:T(8,128)(2,1)S(1)} %bitcast.27, pred[1536]{0:T(1024)(128)(4,1)S(1)} %compare_reduce_fusion.1), kind=kOutput, calls=%fused_computation.5 | convolution fusion | flops 3635673600 | bytes 2366976 | tf_op jit(solution)/shard_map/dot_general | solution.py:81
  202.6 0.4 convolution_reduce_fusion
  203.0 0.0 copy-start.1
  203.1 0.6 multiply_reduce_fusion.2
  204.4 0.5 multiply_reduce_fusion
  204.9 1.3 add_log_fusion
  206.3 0.2 log.8
  206.5 0.1 copy.20
  206.6 0.2 mul.111
  206.8 0.1 copy.21
  207.0 0.8 copy.22
  207.7 6.8 %all-to-all-start.1 = ((f32[256,1,12]{2,1,0:T(1,128)}), f32[256,1,12]{2,1,0:T(1,128)S(1)}, u32[]{:S(2)}, u32[]{:S(2)}) async-start(f32[256,1,12]{2,1,0:T(1,128)} %copy.22), calls=%async_computation.1 | async-start | bytes 262144 | tf_op jit(solution)/shard_map/all_to_all | solution.py:99
  214.5 0.0 copy-done.1
  214.6 12.9 %all-to-all-done.1 = f32[256,1,12]{2,1,0:T(1,128)S(1)} async-done(((f32[256,1,12]{2,1,0:T(1,128)}), f32[256,1,12]{2,1,0:T(1,128)S(1)}, u32[]{:S(2)}, u32[]{:S(2)}) %all-to-all-start.1) | async-done | bytes 12320 | tf_op jit(solution)/shard_map/all_to_all | solution.py:99
  227.5 0.1 copy.23
  227.6 0.1 copy.24
  227.8 0.1 broadcast_in_dim.102
  227.9 0.1 copy.25
  228.1 0.1 broadcast_in_dim.105
  228.2 2.2 select_reduce_fusion.2
  (16 shorter events, 0.2 us)
Async XLA Ops:
  0.6 4.2 %copy-start.2 = (s32[256]{0:T(256)S(1)}, s32[256]{0:T(256)}, u32[]{:S(2)}) copy-start(s32[256]{0:T(256)} %param.5) | copy-start | bytes 3076
  24.4 19.5 %copy-start = (f32[768,768]{1,0:T(8,128)S(1)}, f32[768,768]{1,0:T(8,128)}, u32[]{:S(2)}) copy-start(f32[768,768]{1,0:T(8,128)} %param.3) | copy-start | bytes 7077892
  203.0 11.5 %copy-start.1 = (s32[768,1]{0,1:T(1,128)S(1)}, s32[768,1]{0,1:T(1,128)}, u32[]{:S(2)}) copy-start(s32[768,1]{0,1:T(1,128)} %param.4) | copy-start | bytes 9220
  207.7 19.8 %all-to-all-start.1 = ((f32[256,1,12]{2,1,0:T(1,128)}), f32[256,1,12]{2,1,0:T(1,128)S(1)}, u32[]{:S(2)}, u32[]{:S(2)}) async-start(f32[256,1,12]{2,1,0:T(1,128)} %copy.22), calls=%async_computation.1 | async-start | bytes 262144 | tf_op jit(solution)/shard_map/all_to_all | solution.py:99

commit v4 on v3

--- a/solution.py
+++ b/solution.py
@@ -44,15 +44,19 @@
 
     within = row_slot % PIECE
     half = row_slot // PIECE
-    member_pos = (row_label * PIECE + within) * pieces + half
-    near_pos = (near_label * PIECE + within) * pieces + halves + half
+    member_pos = half * piece_rows + row_label * PIECE + within
+    near_pos = (halves + half) * piece_rows + near_label * PIECE + within
     slot_ids = jnp.arange(pieces * piece_rows, dtype=jnp.int32)
     chosen = (member_pos[None, :] == slot_ids[:, None]) | (near_pos[None, :] == slot_ids[:, None])
-    slot_piece = slot_ids % pieces
-    slot_rank = (slot_piece % halves) * PIECE + (slot_ids // pieces) % PIECE
-    slot_cluster = slot_ids // (pieces * PIECE)
-    have = jnp.where(slot_piece < halves, local_count[slot_cluster], near_count[slot_cluster])
-    present = have > slot_rank
+    shape3 = (pieces, clusters, PIECE)
+    piece_at = lax.broadcasted_iota(jnp.int32, shape3, 0)
+    k_at = lax.broadcasted_iota(jnp.int32, shape3, 2)
+    have = jnp.where(
+        piece_at < halves,
+        jnp.broadcast_to(local_count[None, :, None], shape3),
+        jnp.broadcast_to(near_count[None, :, None], shape3),
+    )
+    present = (have > (piece_at % halves) * PIECE + k_at).reshape(-1)
     picked = lax.dot_general(
         chosen.astype(jnp.bfloat16),
         unit_embed,
@@ -61,7 +65,7 @@
     )
     first = jnp.arange(feature_width, dtype=jnp.int32)[None, :] == 0
     send = jnp.where(first & ~present[:, None], EMPTY, picked).astype(jnp.bfloat16)
-    send = send.reshape(piece_rows, pieces, feature_width).transpose(1, 0, 2)
+    send = send.reshape(pieces, piece_rows, feature_width)
     arrived = lax.all_to_all(send, axes, split_axis=1, concat_axis=1, tiled=True)
     cluster_span = halves * piece_rows
     members = arrived[:halves].reshape(cluster_span, feature_width)

time: 231 us -> 187 us (0.81)
  local copies, waits for them, and re-layouts: 56.9 us -> 13 us
    gather x2 -> x0, local copies, waits for them, and re-layouts: 38.9 us -> none  [the longest x1 19.4 us: body(): local_count[slot_cluster]]
    reshape x1, local copies, waits for them, and re-layouts: 8.97 us -> 3.64 us  [body(): send = send.reshape(pieces, piece_rows, feature_width)]
where the time goes in v4:
time: 187 us; the launch traced here: 186 us
  blocking collectives  124 us (66%)
  matrix products  16.3 us (9%)
  local copies, waits for them, and re-layouts  13 us (7%)
  waiting for transfers between devices  12.9 us (7%)
  other arithmetic  11.2 us (6%)
  starting transfers between devices  6.79 us (4%)
    all_to_all x1, blocking collectives, body(): lax.all_to_all(send, axes, split_axis=1, concat_axis=1, tiled=True)  124 us
    all_to_all x1, waiting for transfers between devices, body(): lax.all_to_all(payload, axes, split_axis=0, concat_axis=0, tiled=True)  12.9 us
    all_to_all x1, starting transfers between devices, body(): lax.all_to_all(payload, axes, split_axis=0, concat_axis=0, tiled=True)  6.79 us
    dot_general x1, matrix products, body(): lax.dot_general(chosen.astype(jnp.bfloat16), unit_embed, (((1,), (0,)), (...  5.89 us
    dot_general x1, matrix products, body(): lax.dot_general(members, members, (((1,), (1,)), ((), ())), preferred_ele...  5.65 us
    slice x1, local copies, waits for them, and re-layouts, body(): others = arrived[halves:].reshape(cluster_span, feature_width)  4.67 us
    dot_general x1, matrix products, body(): lax.dot_general(members, others, (((1,), (1,)), ((), ())), preferred_elem...  4.34 us
  transfers between devices with their start and end apart: 1, of which 1 were waited for; matrix products, arithmetic and copies ran while one was open for 0% of the time, Pallas kernels for 0%

profile of v4, /device:TPU:1, one launch (start us, length us, event | category | flops | bytes accessed | tf_op | source)
XLA Modules:
  0.0 186.2 jit_solution(16653055522597537022)
XLA Ops:
  0.6 0.0 copy-start.2
  0.6 0.0 copy-start
  0.7 0.9 select_reduce_fusion.5
  1.6 0.7 reduce.3
  2.3 0.4 convert_reduce_fusion
  2.7 1.9 %multiply_reduce_fusion.1 = f32[768]{0:T(1024)S(1)} fusion(f32[768,768]{1,0:T(8,128)} %param.3), kind=kLoop, calls=%fused_computation.18 | loop fusion | flops 1178880 | bytes 2362368 | tf_op jit(solution)/shard_map/reduce_sum | solution.py:17
  4.6 0.3 select_reduce_fusion.4
  4.9 0.0 copy-done.2
  4.9 0.2 select_reduce_fusion.6
  5.1 0.2 fusion.10
  5.3 0.3 reshape.185
  5.7 0.0 copy-done
  5.7 5.9 %select_convert_fusion = bf16[3072,768]{1,0:T(8,128)(2,1)S(1)} fusion(pred[768]{0:T(1024)(128)(4,1)S(1)} %iota_compare_fusion.9, pred[3072]{0:T(1024)(128)(4,1)S(1)} %reshape.185, s32[768]{0:T(1024)S(1)} %get-tuple-element.11, s32[768]{0:T(1024)S(1)} %get-tuple-element.10, f32[768,768]{1,0:T(8,128)S(1)} %copy-done, f32[768]{0:T(1024)S(1)} %add_rsqrt_fusion), kind=kOutput, calls=%fused_computation.4 | convolution fusion | flops 3639214080 | bytes 7090944 | tf_op jit(solution)/shard_map/dot_general | solution.py:60
  11.6 3.6 %copy.27 = bf16[4,768,768]{2,0,1:T(4,128)(2,1)S(1)} copy(bf16[4,768,768]{2,1,0:T(8,128)(2,1)S(1)} %bitcast.27) | data formatting | bytes 9437184 | tf_op jit(solution)/shard_map/reshape | solution.py:68
  15.2 124.4 %all_to_all.14 = bf16[4,768,768]{2,0,1:T(4,128)(2,1)S(1)} all-to-all(bf16[4,768,768]{2,0,1:T(4,128)(2,1)S(1)} %copy.27), channel_id=1, replica_groups=mesh['corpus'=32,'group'=8] {'corpus','group'}, dimensions={1} | all-to-all | bytes 9437184 | tf_op jit(solution)/shard_map/all_to_all | solution.py:69
  139.6 4.7 %fusion.12 = (bf16[2,768,768]{2,0,1:T(2,128)(2,1)}, bf16[2,768,768]{2,0,1:T(2,128)(2,1)S(1)}) fusion(bf16[4,768,768]{2,0,1:T(4,128)(2,1)S(1)} %all_to_all.14), kind=kLoop, calls=%fused_computation.56 | loop fusion | bytes 9437184 | tf_op jit(solution)/shard_map/slice | solution.py:72
  144.3 2.0 %copy.37 = bf16[2,768,768]{2,1,0:T(8,128)(2,1)S(1)} copy(bf16[2,768,768]{2,0,1:T(2,128)(2,1)} %get-tuple-element.6) | data formatting | bytes 4718592
  146.2 0.3 compare_reduce_fusion
  146.5 0.6 convert_reduce_fusion.2
  147.1 0.3 copy.36
  147.4 4.3 %select_reduce_fusion = f32[1536]{0:T(1024)S(1)} fusion(bf16[1536,768]{1,0:T(8,128)(2,1)S(1)} %bitcast.23, bf16[1536,768]{1,0:T(8,128)(2,1)S(1)} %bitcast.29, pred[1536]{0:T(1024)(128)(4,1)S(1)} %compare_reduce_fusion), kind=kOutput, calls=%fused_computation.2 | convolution fusion | flops 3630955008 | bytes 4726272 | tf_op jit(solution)/shard_map/dot_general | solution.py:88
  151.8 0.3 compare_reduce_fusion.1
  152.1 0.7 convert_reduce_fusion.3
  152.8 5.6 %select_reduce_fusion.1 = f32[1536]{0:T(1024)S(1)} fusion(bf16[1536,768]{1,0:T(8,128)(2,1)S(1)} %bitcast.25, pred[1536]{0:T(1024)(128)(4,1)S(1)} %compare_reduce_fusion.1), kind=kOutput, calls=%fused_computation.3 | convolution fusion | flops 3635673600 | bytes 2366976 | tf_op jit(solution)/shard_map/dot_general | solution.py:85
  158.4 0.4 convolution_reduce_fusion
  158.9 0.0 copy-start.1
  158.9 0.6 multiply_reduce_fusion.2
  160.2 0.5 multiply_reduce_fusion
  160.7 1.3 add_log_fusion
  162.1 0.2 log.8
  162.3 0.1 copy.30
  162.4 0.2 mul.116
  162.7 0.1 copy.31
  162.8 0.8 copy.32
  163.6 6.8 %all-to-all-start.1 = ((f32[256,1,12]{2,1,0:T(1,128)}), f32[256,1,12]{2,1,0:T(1,128)S(1)}, u32[]{:S(2)}, u32[]{:S(2)}) async-start(f32[256,1,12]{2,1,0:T(1,128)} %copy.32), calls=%async_computation.1 | async-start | bytes 262144 | tf_op jit(solution)/shard_map/all_to_all | solution.py:103
  170.4 0.0 copy-done.1
  170.4 12.9 %all-to-all-done.1 = f32[256,1,12]{2,1,0:T(1,128)S(1)} async-done(((f32[256,1,12]{2,1,0:T(1,128)}), f32[256,1,12]{2,1,0:T(1,128)S(1)}, u32[]{:S(2)}, u32[]{:S(2)}) %all-to-all-start.1) | async-done | bytes 12320 | tf_op jit(solution)/shard_map/all_to_all | solution.py:103
  183.3 0.1 copy.33
  183.4 0.1 copy.34
  183.6 0.1 broadcast_in_dim.113
  183.7 0.1 copy.35
  183.9 0.1 broadcast_in_dim.116
  184.0 2.2 %select_reduce_fusion.2 = (f32[768]{0:T(1024)}, f32[768]{0:T(1024)}) fusion(f32[1536]{0:T(1024)S(1)} %broadcast_in_dim.116, s32[768]{0:T(1024)S(1)} %add_reduce_fusion, f32[1536]{0:T(1024)S(1)} %broadcast_in_dim.113), kind=kLoop, calls=%fused_computation.11 | loop fusion | flops 5896704 | bytes 21504 | tf_op jit(solution)/shard_map/reduce_sum | solution.py:107
  (15 shorter events, 0.1 us)
Async XLA Ops:
  0.6 4.3 %copy-start.2 = (s32[256]{0:T(256)S(1)}, s32[256]{0:T(256)}, u32[]{:S(2)}) copy-start(s32[256]{0:T(256)} %param.5) | copy-start | bytes 3076
  0.6 5.0 %copy-start = (f32[768,768]{1,0:T(8,128)S(1)}, f32[768,768]{1,0:T(8,128)}, u32[]{:S(2)}) copy-start(f32[768,768]{1,0:T(8,128)} %param.3) | copy-start | bytes 7077892
  158.9 11.5 %copy-start.1 = (s32[768,1]{0,1:T(1,128)S(1)}, s32[768,1]{0,1:T(1,128)}, u32[]{:S(2)}) copy-start(s32[768,1]{0,1:T(1,128)} %param.4) | copy-start | bytes 9220
  163.6 19.8 %all-to-all-start.1 = ((f32[256,1,12]{2,1,0:T(1,128)}), f32[256,1,12]{2,1,0:T(1,128)S(1)}, u32[]{:S(2)}, u32[]{:S(2)}) async-start(f32[256,1,12]{2,1,0:T(1,128)} %copy.32), calls=%async_computation.1 | async-start | bytes 262144 | tf_op jit(solution)/shard_map/all_to_all | solution.py:103

commit v5 on v4

--- a/solution.py
+++ b/solution.py
@@ -68,28 +68,30 @@
     send = send.reshape(pieces, piece_rows, feature_width)
     arrived = lax.all_to_all(send, axes, split_axis=1, concat_axis=1, tiled=True)
     cluster_span = halves * piece_rows
-    members = arrived[:halves].reshape(cluster_span, feature_width)
-    others = arrived[halves:].reshape(cluster_span, feature_width)
-    member_ok = members[:, 0] < 1.5
-    other_ok = others[:, 0] < 1.5
+    members = arrived[:halves]
+    others = arrived[halves:]
+    member_ok = members[:, :, 0] < 1.5
+    other_ok = others[:, :, 0] < 1.5
     count_own = jnp.sum(member_ok.astype(jnp.float32))
     count_near = jnp.sum(other_ok.astype(jnp.float32))
     sums = lax.dot_general(
-        member_ok.astype(jnp.bfloat16)[None, :],
+        member_ok.astype(jnp.bfloat16),
         members,
-        (((1,), (0,)), ((), ())),
+        (((0, 1), (0, 1)), ((), ())),
         preferred_element_type=jnp.float32,
     )
     centroid = normalize(sums)
-    typical = TYPICAL_SCALE * jnp.sum(members.astype(jnp.float32) * centroid, axis=1)
+    typical = TYPICAL_SCALE * jnp.sum(members.astype(jnp.float32) * centroid, axis=2).reshape(-1)
     g_own = lax.dot_general(
-        members, members, (((1,), (1,)), ((), ())), preferred_element_type=jnp.float32
-    )
+        members, members, (((2,), (2,)), ((), ())), preferred_element_type=jnp.float32
+    ).reshape(cluster_span, cluster_span)
     g_near = lax.dot_general(
-        members, others, (((1,), (1,)), ((), ())), preferred_element_type=jnp.float32
-    )
+        members, others, (((2,), (2,)), ((), ())), preferred_element_type=jnp.float32
+    ).reshape(cluster_span, cluster_span)
     ids = jnp.arange(cluster_span, dtype=jnp.int32)
     distinct = ids[:, None] != ids[None, :]
+    member_ok = member_ok.reshape(-1)
+    other_ok = other_ok.reshape(-1)
     w_own = jnp.where(distinct & member_ok[None, :], jnp.exp(SHARPNESS * g_own), 0.0)
     w_near = jnp.where(other_ok[None, :], jnp.exp(SHARPNESS * g_near), 0.0)
     own_sum = jnp.sum(w_own, axis=1)

time: 187 us -> 196 us (1.048)
  blocking collectives: 124 us -> 0 us
  waiting for transfers between devices: 12.9 us -> 121 us
  starting transfers between devices: 6.79 us -> 23.3 us
  local copies, waits for them, and re-layouts: 13 us -> 20.4 us
  matrix products: 16.3 us -> 18.4 us
    all_to_all x1 -> x0, blocking collectives: 124 us -> none  [body(): lax.all_to_all(send, axes, split_axis=1, concat_axis=1, tiled=True)]
    all_to_all x0 -> x1, waiting for transfers between devices: none -> 108 us  [body(): lax.all_to_all(send, axes, split_axis=1, concat_axis=1, tiled=True)]
    all_to_all x0 -> x1, starting transfers between devices: none -> 16.5 us  [body(): lax.all_to_all(send, axes, split_axis=1, concat_axis=1, tiled=True)]
    slice x1 -> x2, local copies, waits for them, and re-layouts: 4.67 us -> 11.5 us  [the longest x1 9.27 us: body(): others = arrived[halves:]]
    reshape x1, local copies, waits for them, and re-layouts: 3.64 us -> 5.81 us  [body(): send = send.reshape(pieces, piece_rows, feature_width)]
    dot_general x3, matrix products: 10.4 us -> 12.5 us  [the longest x1 6.24 us: body(): lax.dot_general(members, others, (((2,), (2,)), ((), ())), preferred_elem...]
  transfers between devices with their start and end apart: 1 -> 2, of which waited for: 1 -> 2; matrix products, arithmetic and copies ran while one was open for 0% -> 0% of each run, Pallas kernels for 0% -> 0%
where the time goes in v5:
time: 196 us; the launch traced here: 195 us
  waiting for transfers between devices  121 us (62%)
  starting transfers between devices  23.3 us (12%)
  local copies, waits for them, and re-layouts  20.4 us (10%)
  matrix products  18.4 us (9%)
  other arithmetic  10.6 us (5%)
    all_to_all x1, waiting for transfers between devices, body(): lax.all_to_all(send, axes, split_axis=1, concat_axis=1, tiled=True)  108 us
    all_to_all x1, starting transfers between devices, body(): lax.all_to_all(send, axes, split_axis=1, concat_axis=1, tiled=True)  16.5 us
    all_to_all x1, waiting for transfers between devices, body(): lax.all_to_all(payload, axes, split_axis=0, concat_axis=0, tiled=True)  12.9 us
    slice x1, local copies, waits for them, and re-layouts, body(): others = arrived[halves:]  9.27 us
    all_to_all x1, starting transfers between devices, body(): lax.all_to_all(payload, axes, split_axis=0, concat_axis=0, tiled=True)  6.79 us
    dot_general x1, matrix products, body(): lax.dot_general(members, others, (((2,), (2,)), ((), ())), preferred_elem...  6.24 us
    dot_general x1, matrix products, body(): lax.dot_general(chosen.astype(jnp.bfloat16), unit_embed, (((1,), (0,)), (...  5.9 us
    dot_general x1, matrix products, body(): lax.dot_general(members, members, (((2,), (2,)), ((), ())), preferred_ele...  5.88 us
  transfers between devices with their start and end apart: 2, of which 2 were waited for; matrix products, arithmetic and copies ran while one was open for 0% of the time, Pallas kernels for 0%

profile of v5, /device:TPU:1, one launch (start us, length us, event | category | flops | bytes accessed | tf_op | source)
XLA Modules:
  0.0 195.4 jit_solution(11725044335287983816)
XLA Ops:
  0.6 0.0 copy-start.2
  0.6 0.0 copy-start
  0.7 0.9 select_reduce_fusion.5
  1.6 0.7 reduce.2
  2.3 0.4 convert_reduce_fusion
  2.7 1.9 multiply_reduce_fusion.1
  4.6 0.3 select_reduce_fusion.4
  4.9 0.0 copy-done.2
  4.9 0.2 select_reduce_fusion.6
  5.1 0.2 fusion.19
  5.3 0.3 reshape.194
  5.7 0.0 copy-done
  5.7 5.9 %select_convert_fusion = bf16[3072,768]{1,0:T(8,128)(2,1)S(1)} fusion(pred[768]{0:T(1024)(128)(4,1)S(1)} %iota_compare_fusion.8, pred[3072]{0:T(1024)(128)(4,1)S(1)} %reshape.194, s32[768]{0:T(1024)S(1)} %get-tuple-element.13, s32[768]{0:T(1024)S(1)} %get-tuple-element.12, f32[768,768]{1,0:T(8,128)S(1)} %copy-done, f32[768]{0:T(1024)S(1)} %add_rsqrt_fusion), kind=kOutput, calls=%fused_computation.2 | convolution fusion | flops 3639214080 | bytes 7090944 | tf_op jit(solution)/shard_map/dot_general | solution.py:60
  11.6 5.8 %copy.31 = bf16[4,768,768]{2,0,1:T(4,128)(2,1)} copy(bf16[4,768,768]{2,1,0:T(8,128)(2,1)S(1)} %bitcast.34) | data formatting | bytes 9437184 | tf_op jit(solution)/shard_map/reshape | solution.py:68
  17.4 16.5 %all-to-all-start = ((bf16[4,768,768]{2,0,1:T(4,128)(2,1)}), bf16[4,768,768]{2,0,1:T(4,128)(2,1)}, u32[]{:S(2)}, u32[]{:S(2)}) async-start(bf16[4,768,768]{2,0,1:T(4,128)(2,1)} %copy.31), calls=%async_computation | async-start | bytes 9437184 | tf_op jit(solution)/shard_map/all_to_all | solution.py:69
  34.0 108.1 %all-to-all-done = bf16[4,768,768]{2,0,1:T(4,128)(2,1)} async-done(((bf16[4,768,768]{2,0,1:T(4,128)(2,1)}), bf16[4,768,768]{2,0,1:T(4,128)(2,1)}, u32[]{:S(2)}, u32[]{:S(2)}) %all-to-all-start) | async-done | bytes 4718624 | tf_op jit(solution)/shard_map/all_to_all | solution.py:69
  142.1 2.2 %fusion.25 = (bf16[2,768,1]{2,0,1:T(2,128)(2,1)S(1)}, bf16[2,768,1]{2,0,1:T(2,128)(2,1)S(1)}) fusion(bf16[4,768,768]{2,0,1:T(4,128)(2,1)} %all-to-all-done), kind=kLoop, calls=%fused_computation.65 | loop fusion | bytes 12288 | tf_op jit(solution)/shard_map/slice | solution.py:74
  144.3 0.3 copy.46
  144.6 0.6 convert_reduce_fusion.2
  145.3 0.3 copy.44
  145.6 0.6 convert_reduce_fusion.3
  146.2 9.3 %fusion.24 = (bf16[2,768,768]{2,0,1:T(2,128)(2,1)}, bf16[2,768,768]{2,0,1:T(2,128)(2,1)S(1)}) fusion(bf16[4,768,768]{2,0,1:T(4,128)(2,1)} %all-to-all-done), kind=kLoop, calls=%fused_computation.64 | loop fusion | bytes 9437184 | tf_op jit(solution)/shard_map/slice | solution.py:72
  155.5 0.4 fusion.16
  155.9 0.6 multiply_reduce_fusion.2
  157.2 0.5 multiply_reduce_fusion
  157.8 0.2 mul.115
  158.0 0.1 copy.37
  158.1 6.2 %select_reduce_fusion = f32[2,768]{1,0:T(2,128)S(1)} fusion(pred[2,768]{1,0:T(4,128)(4,1)S(1)} %compare_bitcast_fusion, bf16[2,768,768]{2,0,1:T(2,128)(2,1)} %get-tuple-element.6, bf16[2,768,768]{2,0,1:T(2,128)(2,1)S(1)} %get-tuple-element.7), kind=kOutput, calls=%fused_computation | convolution fusion | flops 3630955008 | bytes 4726272 | tf_op jit(solution)/shard_map/dot_general | solution.py:88
  164.4 0.0 copy-start.1
  164.4 5.9 %select_reduce_fusion.1 = f32[2,768]{1,0:T(2,128)S(1)} fusion(s32[2,768]{1,0:T(2,128)S(1)} %multiply_add_fusion, pred[2,768]{1,0:T(4,128)(4,1)S(1)} %get-tuple-element.14, bf16[2,768,768]{2,0,1:T(2,128)(2,1)S(1)} %get-tuple-element.7), kind=kOutput, calls=%fused_computation.1 | convolution fusion | flops 3635673600 | bytes 2373120 | tf_op jit(solution)/shard_map/dot_general | solution.py:85
  170.3 1.3 fusion.21
  171.6 0.2 log.8
  171.8 0.1 copy.36
  172.0 0.8 copy.38
  172.7 6.8 %all-to-all-start.1 = ((f32[256,1,12]{2,1,0:T(1,128)}), f32[256,1,12]{2,1,0:T(1,128)S(1)}, u32[]{:S(2)}, u32[]{:S(2)}) async-start(f32[256,1,12]{2,1,0:T(1,128)} %copy.38), calls=%async_computation.1 | async-start | bytes 262144 | tf_op jit(solution)/shard_map/all_to_all | solution.py:105
  179.5 0.0 copy-done.1
  179.6 12.9 %all-to-all-done.1 = f32[256,1,12]{2,1,0:T(1,128)S(1)} async-done(((f32[256,1,12]{2,1,0:T(1,128)}), f32[256,1,12]{2,1,0:T(1,128)S(1)}, u32[]{:S(2)}, u32[]{:S(2)}) %all-to-all-start.1) | async-done | bytes 12320 | tf_op jit(solution)/shard_map/all_to_all | solution.py:105
  192.5 0.1 copy.39
  192.6 0.1 copy.40
  192.7 0.1 broadcast_in_dim.111
  192.9 0.1 copy.41
  193.0 0.1 broadcast_in_dim.114
  193.2 2.2 %select_reduce_fusion.2 = (f32[768]{0:T(1024)}, f32[768]{0:T(1024)}) fusion(f32[1536]{0:T(1024)S(1)} %broadcast_in_dim.114, s32[768]{0:T(1024)S(1)} %add_reduce_fusion, f32[1536]{0:T(1024)S(1)} %broadcast_in_dim.111), kind=kLoop, calls=%fused_computation.7 | loop fusion | flops 5896704 | bytes 21504 | tf_op jit(solution)/shard_map/reduce_sum | solution.py:109
  (17 shorter events, 0.1 us)
Async XLA Ops:
  0.6 4.3 %copy-start.2 = (s32[256]{0:T(256)S(1)}, s32[256]{0:T(256)}, u32[]{:S(2)}) copy-start(s32[256]{0:T(256)} %param.5) | copy-start | bytes 3076
  0.6 5.0 %copy-start = (f32[768,768]{1,0:T(8,128)S(1)}, f32[768,768]{1,0:T(8,128)}, u32[]{:S(2)}) copy-start(f32[768,768]{1,0:T(8,128)} %param.3) | copy-start | bytes 7077892
  17.4 124.7 %all-to-all-start = ((bf16[4,768,768]{2,0,1:T(4,128)(2,1)}), bf16[4,768,768]{2,0,1:T(4,128)(2,1)}, u32[]{:S(2)}, u32[]{:S(2)}) async-start(bf16[4,768,768]{2,0,1:T(4,128)(2,1)} %copy.31), calls=%async_computation | async-start | bytes 9437184 | tf_op jit(solution)/shard_map/all_to_all | solution.py:69
  164.4 15.1 %copy-start.1 = (s32[768,1]{0,1:T(1,128)S(1)}, s32[768,1]{0,1:T(1,128)}, u32[]{:S(2)}) copy-start(s32[768,1]{0,1:T(1,128)} %param.4) | copy-start | bytes 9220
  172.7 19.8 %all-to-all-start.1 = ((f32[256,1,12]{2,1,0:T(1,128)}), f32[256,1,12]{2,1,0:T(1,128)S(1)}, u32[]{:S(2)}, u32[]{:S(2)}) async-start(f32[256,1,12]{2,1,0:T(1,128)} %copy.38), calls=%async_computation.1 | async-start | bytes 262144 | tf_op jit(solution)/shard_map/all_to_all | solution.py:105

commit v6 on v4

--- a/solution.py
+++ b/solution.py
@@ -1,6 +1,9 @@
+import functools
+
 import jax
 import jax.numpy as jnp
 from jax import lax
+from jax.experimental import pallas as pl
 from jax.sharding import PartitionSpec as P
 
 MOST = 6
@@ -15,6 +18,60 @@
 
 def normalize(values):
     return values * lax.rsqrt(jnp.sum(values * values, axis=-1, keepdims=True) + EPSILON)
+
+
+def pair_kernel(rows_ref, ok_ref, centroid_ref, score_ref, typical_ref, *, halves, block):
+    piece_rows = rows_ref.shape[1]
+    step = pl.program_id(0)
+    per_piece = piece_rows // block
+    first_row = (step % per_piece) * block
+    queries = rows_ref[step // per_piece, pl.ds(first_row, block), :]
+    row_at = (step // per_piece) * piece_rows + first_row + lax.broadcasted_iota(
+        jnp.int32, (block, piece_rows), 0
+    )
+    col_at = lax.broadcasted_iota(jnp.int32, (block, piece_rows), 1)
+    own = jnp.zeros((block, 1), jnp.float32)
+    near = jnp.zeros((block, 1), jnp.float32)
+    for piece in range(halves):
+        cols = slice(piece * piece_rows, (piece + 1) * piece_rows)
+        g_own = lax.dot_general(
+            queries, rows_ref[piece], (((1,), (1,)), ((), ())), preferred_element_type=jnp.float32
+        )
+        keep = (ok_ref[0:1, cols] > 0.5) & (col_at + piece * piece_rows != row_at)
+        own = own + jnp.sum(jnp.where(keep, jnp.exp(SHARPNESS * g_own), 0.0), axis=1, keepdims=True)
+        g_near = lax.dot_general(
+            queries,
+            rows_ref[halves + piece],
+            (((1,), (1,)), ((), ())),
+            preferred_element_type=jnp.float32,
+        )
+        keep = ok_ref[1:2, cols] > 0.5
+        near = near + jnp.sum(jnp.where(keep, jnp.exp(SHARPNESS * g_near), 0.0), axis=1, keepdims=True)
+    count_own = jnp.sum(ok_ref[0:1, :], axis=1, keepdims=True)
+    count_near = jnp.sum(ok_ref[1:2, :], axis=1, keepdims=True)
+    score_ref[...] = jnp.log(1.0 + own / count_own + near / count_near)
+    typical_ref[...] = TYPICAL_SCALE * jnp.sum(
+        queries.astype(jnp.float32) * centroid_ref[...], axis=1, keepdims=True
+    )
+
+
+def pair_scores(arrived, member_ok, other_ok, centroid, halves, block=256):
+    pieces, piece_rows, feature_width = arrived.shape
+    span = halves * piece_rows
+    oks = jnp.stack([member_ok, other_ok]).astype(jnp.float32)
+    out = jax.ShapeDtypeStruct((span, 1), jnp.float32)
+    score, typical = pl.pallas_call(
+        functools.partial(pair_kernel, halves=halves, block=block),
+        grid=(span // block,),
+        in_specs=[
+            pl.BlockSpec((pieces, piece_rows, feature_width), lambda i: (0, 0, 0)),
+            pl.BlockSpec((2, span), lambda i: (0, 0)),
+            pl.BlockSpec((1, feature_width), lambda i: (0, 0)),
+        ],
+        out_specs=[pl.BlockSpec((block, 1), lambda i: (i, 0))] * 2,
+        out_shape=[out, out],
+    )(arrived, oks, centroid.reshape(1, feature_width))
+    return score[:, 0], typical[:, 0]
 
 
 def body(embeddings, labels, neighbours):
@@ -68,12 +125,9 @@
     send = send.reshape(pieces, piece_rows, feature_width)
     arrived = lax.all_to_all(send, axes, split_axis=1, concat_axis=1, tiled=True)
     cluster_span = halves * piece_rows
+    member_ok = (arrived[:halves, :, 0] < 1.5).reshape(-1)
+    other_ok = (arrived[halves:, :, 0] < 1.5).reshape(-1)
     members = arrived[:halves].reshape(cluster_span, feature_width)
-    others = arrived[halves:].reshape(cluster_span, feature_width)
-    member_ok = members[:, 0] < 1.5
-    other_ok = others[:, 0] < 1.5
-    count_own = jnp.sum(member_ok.astype(jnp.float32))
-    count_near = jnp.sum(other_ok.astype(jnp.float32))
     sums = lax.dot_general(
         member_ok.astype(jnp.bfloat16)[None, :],
         members,
@@ -81,20 +135,8 @@
         preferred_element_type=jnp.float32,
     )
     centroid = normalize(sums)
-    typical = TYPICAL_SCALE * jnp.sum(members.astype(jnp.float32) * centroid, axis=1)
-    g_own = lax.dot_general(
-        members, members, (((1,), (1,)), ((), ())), preferred_element_type=jnp.float32
-    )
-    g_near = lax.dot_general(
-        members, others, (((1,), (1,)), ((), ())), preferred_element_type=jnp.float32
-    )
+    score, typical = pair_scores(arrived, member_ok, other_ok, centroid, halves)
     ids = jnp.arange(cluster_span, dtype=jnp.int32)
-    distinct = ids[:, None] != ids[None, :]
-    w_own = jnp.where(distinct & member_ok[None, :], jnp.exp(SHARPNESS * g_own), 0.0)
-    w_near = jnp.where(other_ok[None, :], jnp.exp(SHARPNESS * g_near), 0.0)
-    own_sum = jnp.sum(w_own, axis=1)
-    near_sum = jnp.sum(w_near, axis=1)
-    score = jnp.log(1.0 + own_sum / count_own + near_sum / count_near)
 
     def by_source(values):
         return values.reshape(halves, clusters, PIECE).transpose(1, 0, 2).reshape(clusters, MOST)

time: 187 us -> 193 us (1.032)
  Pallas kernels: 0 us -> 12.7 us
  matrix products: 16.3 us -> 6.32 us
  local copies, waits for them, and re-layouts: 13 us -> 16.8 us
    pallas_call x0 -> x1, Pallas kernels: none -> 12.7 us  [pair_scores(): pl.pallas_call(functools.partial(pair_kernel, halves=halves, block=block)...]
    dot_general x2 -> x0, matrix products: 9.99 us -> none  [the longest x1 5.65 us: body(): lax.dot_general(members, members, (((1,), (1,)), ((), ())), preferred_ele...]
    all_to_all x0 -> x1, local copies, waits for them, and re-layouts: none -> 5.06 us  [body(): lax.all_to_all(send, axes, split_axis=1, concat_axis=1, tiled=True)]
    pallas_call x0 -> x2, other arithmetic: none -> 2.82 us  [pair_scores(): pl.pallas_call(functools.partial(pair_kernel, halves=halves, block=block)...]
    slice x1 -> x3, local copies, waits for them, and re-layouts: 4.67 us -> 2.21 us  [the longest x2 1.66 us: body(): members = arrived[:halves].reshape(cluster_span, feature_width)]
where the time goes in v6:
time: 193 us; the launch traced here: 192 us
  blocking collectives  124 us (64%)
  local copies, waits for them, and re-layouts  16.8 us (9%)
  waiting for transfers between devices  12.9 us (7%)
  Pallas kernels  12.7 us (7%)
  other arithmetic  10.9 us (6%)
  starting transfers between devices  6.79 us (4%)
  matrix products  6.32 us (3%)
    all_to_all x1, blocking collectives, body(): lax.all_to_all(send, axes, split_axis=1, concat_axis=1, tiled=True)  124 us
    all_to_all x1, waiting for transfers between devices, body(): lax.all_to_all(payload, axes, split_axis=0, concat_axis=0, tiled=True)  12.9 us
    pallas_call x1, Pallas kernels, pair_scores(): pl.pallas_call(functools.partial(pair_kernel, halves=halves, block=block)...  12.7 us
    all_to_all x1, starting transfers between devices, body(): lax.all_to_all(payload, axes, split_axis=0, concat_axis=0, tiled=True)  6.79 us
    dot_general x1, matrix products, body(): lax.dot_general(chosen.astype(jnp.bfloat16), unit_embed, (((1,), (0,)), (...  5.89 us
    all_to_all x1, local copies, waits for them, and re-layouts, body(): lax.all_to_all(send, axes, split_axis=1, concat_axis=1, tiled=True)  5.06 us
  transfers between devices with their start and end apart: 1, of which 1 were waited for; matrix products, arithmetic and copies ran while one was open for 0% of the time, Pallas kernels for 0%

profile of v6, /device:TPU:1, one launch (start us, length us, event | category | flops | bytes accessed | tf_op | source)
XLA Modules:
  0.0 192.3 jit_solution(11924052817515637552)
XLA Ops:
  0.6 0.0 copy-start.3
  0.6 0.0 copy-start.1
  0.7 0.9 select_reduce_fusion.3
  1.6 0.7 reduce.2
  2.3 0.4 convert_reduce_fusion
  2.7 1.9 multiply_reduce_fusion
  4.6 0.3 select_reduce_fusion.2
  4.9 0.0 copy-done.3
  4.9 0.2 select_reduce_fusion.4
  5.1 0.2 fusion.14
  5.3 0.3 reshape.167
  5.7 0.0 copy-done.1
  5.7 5.9 %select_convert_fusion = bf16[3072,768]{1,0:T(8,128)(2,1)S(1)} fusion(pred[768]{0:T(1024)(128)(4,1)S(1)} %iota_compare_fusion.8, pred[3072]{0:T(1024)(128)(4,1)S(1)} %reshape.167, s32[768]{0:T(1024)S(1)} %get-tuple-element.15, s32[768]{0:T(1024)S(1)} %get-tuple-element.14, f32[768,768]{1,0:T(8,128)S(1)} %copy-done.1, f32[768]{0:T(1024)S(1)} %add_rsqrt_fusion), kind=kOutput, calls=%fused_computation | convolution fusion | flops 3639214080 | bytes 7090944 | tf_op jit(solution)/shard_map/dot_general | solution.py:117
  11.6 3.6 %copy.31 = bf16[4,768,768]{2,0,1:T(4,128)(2,1)S(1)} copy(bf16[4,768,768]{2,1,0:T(8,128)(2,1)S(1)} %bitcast.24) | data formatting | bytes 9437184 | tf_op jit(solution)/shard_map/reshape | solution.py:125
  15.2 124.4 %all_to_all.14 = bf16[4,768,768]{2,0,1:T(4,128)(2,1)S(1)} all-to-all(bf16[4,768,768]{2,0,1:T(4,128)(2,1)S(1)} %copy.31), channel_id=1, replica_groups=mesh['corpus'=32,'group'=8] {'corpus','group'}, dimensions={1} | all-to-all | bytes 9437184 | tf_op jit(solution)/shard_map/all_to_all | solution.py:126
  139.6 0.0 copy-start
  139.6 2.2 %copy-done = bf16[4,768,768]{2,0,1:T(4,128)(2,1)} copy-done((bf16[4,768,768]{2,0,1:T(4,128)(2,1)}, bf16[4,768,768]{2,0,1:T(4,128)(2,1)S(1)}, u32[]{:S(2)}) %copy-start) | copy-done | bytes 4718616
  141.8 0.5 fusion.18
  142.3 0.3 copy.43
  142.6 0.3 copy.44
  143.1 0.0 slice-start
  143.1 1.7 slice-done
  144.7 0.4 fusion.11
  145.2 0.6 multiply_reduce_fusion.1
  146.5 0.6 mul.86.centroid_ref
  147.0 0.6 add_convert_fusion.ok_ref
  147.7 5.1 %copy.34.rows_ref = bf16[4,768,768]{2,1,0:T(8,128)(2,1)} copy(bf16[4,768,768]{2,0,1:T(4,128)(2,1)} %copy-done) | data formatting | bytes 9437184 | tf_op jit(solution)/shard_map/all_to_all | solution.py:126
  152.7 12.7 %shard_map.50 = (f32[1536,1]{1,0:T(8,128)}, f32[1536,1]{1,0:T(8,128)}) custom-call(bf16[4,768,768]{2,1,0:T(8,128)(2,1)} %copy.34.rows_ref, f32[2,1536]{1,0:T(2,128)} %add_convert_fusion.ok_ref, f32[1,768]{1,0:T(1,128)} %mul.86.centroid_ref), custom_call_target="tpu_custom_call" | custom-call | tf_op jit(solution)/shard_map/pallas_call | solution.py:63
  165.4 0.0 copy-start.2
  165.4 1.4 reduce.5
  166.8 1.4 reduce.6
  168.2 0.2 reshape_squeeze.7
  168.4 0.1 copy.36
  168.5 0.2 reshape_squeeze.6
  168.8 0.1 copy.35
  168.9 0.8 copy.37
  169.7 6.8 %all-to-all-start.1 = ((f32[256,1,12]{2,1,0:T(1,128)}), f32[256,1,12]{2,1,0:T(1,128)S(1)}, u32[]{:S(2)}, u32[]{:S(2)}) async-start(f32[256,1,12]{2,1,0:T(1,128)} %copy.37), calls=%async_computation.1 | async-start | bytes 262144 | tf_op jit(solution)/shard_map/all_to_all | solution.py:145
  176.5 0.0 copy-done.2
  176.5 12.9 %all-to-all-done.1 = f32[256,1,12]{2,1,0:T(1,128)S(1)} async-done(((f32[256,1,12]{2,1,0:T(1,128)}), f32[256,1,12]{2,1,0:T(1,128)S(1)}, u32[]{:S(2)}, u32[]{:S(2)}) %all-to-all-start.1) | async-done | bytes 12320 | tf_op jit(solution)/shard_map/all_to_all | solution.py:145
  189.4 0.1 copy.38
  189.5 0.1 copy.39
  189.7 0.1 broadcast_in_dim.93
  189.8 0.1 copy.40
  190.0 0.1 broadcast_in_dim.96
  190.1 2.2 %select_reduce_fusion = (f32[768]{0:T(1024)}, f32[768]{0:T(1024)}) fusion(f32[1536]{0:T(1024)S(1)} %broadcast_in_dim.96, s32[768]{0:T(1024)S(1)} %add_reduce_fusion, f32[1536]{0:T(1024)S(1)} %broadcast_in_dim.93), kind=kLoop, calls=%fused_computation.5 | loop fusion | flops 5896704 | bytes 21504 | tf_op jit(solution)/shard_map/reduce_sum | solution.py:149
  (17 shorter events, 0.2 us)
Async XLA Ops:
  0.6 4.3 %copy-start.3 = (s32[256]{0:T(256)S(1)}, s32[256]{0:T(256)}, u32[]{:S(2)}) copy-start(s32[256]{0:T(256)} %param.5) | copy-start | bytes 3076
  0.6 5.0 %copy-start.1 = (f32[768,768]{1,0:T(8,128)S(1)}, f32[768,768]{1,0:T(8,128)}, u32[]{:S(2)}) copy-start(f32[768,768]{1,0:T(8,128)} %param.3) | copy-start | bytes 7077892
  139.6 2.2 %copy-start = (bf16[4,768,768]{2,0,1:T(4,128)(2,1)}, bf16[4,768,768]{2,0,1:T(4,128)(2,1)S(1)}, u32[]{:S(2)}) copy-start(bf16[4,768,768]{2,0,1:T(4,128)(2,1)S(1)} %all_to_all.14) | copy-start | bytes 14155780
  143.1 1.7 slice-start
  165.4 11.1 %copy-start.2 = (s32[768,1]{0,1:T(1,128)S(1)}, s32[768,1]{0,1:T(1,128)}, u32[]{:S(2)}) copy-start(s32[768,1]{0,1:T(1,128)} %param.4) | copy-start | bytes 9220
  169.7 19.8 %all-to-all-start.1 = ((f32[256,1,12]{2,1,0:T(1,128)}), f32[256,1,12]{2,1,0:T(1,128)S(1)}, u32[]{:S(2)}, u32[]{:S(2)}) async-start(f32[256,1,12]{2,1,0:T(1,128)} %copy.37), calls=%async_computation.1 | async-start | bytes 262144 | tf_op jit(solution)/shard_map/all_to_all | solution.py:145

commit v7 on v4

--- a/solution.py
+++ b/solution.py
@@ -29,34 +29,22 @@
     unit_embed = normalize(embeddings).astype(jnp.bfloat16)
     row_label = labels[:, 0]
     cluster_ids = jnp.arange(clusters, dtype=jnp.int32)
-    previous = jnp.sum(
-        jnp.where(neighbours[None, :] == cluster_ids[:, None], cluster_ids[None, :], 0), axis=1
-    )
     row_ids = jnp.arange(row_count, dtype=jnp.int32)
     before = (row_label[None, :] == row_label[:, None]) & (row_ids[None, :] < row_ids[:, None])
     row_slot = jnp.sum(before.astype(jnp.int32), axis=1)
     label_hot = row_label[:, None] == cluster_ids[None, :]
-    near_label = jnp.sum(jnp.where(label_hot, previous[None, :], 0), axis=1)
     local_count = jnp.sum(label_hot.astype(jnp.int32), axis=0)
-    near_count = jnp.sum(
-        jnp.where(neighbours[:, None] == cluster_ids[None, :], local_count[None, :], 0), axis=1
-    )
 
     within = row_slot % PIECE
     half = row_slot // PIECE
     member_pos = half * piece_rows + row_label * PIECE + within
-    near_pos = (halves + half) * piece_rows + near_label * PIECE + within
-    slot_ids = jnp.arange(pieces * piece_rows, dtype=jnp.int32)
-    chosen = (member_pos[None, :] == slot_ids[:, None]) | (near_pos[None, :] == slot_ids[:, None])
-    shape3 = (pieces, clusters, PIECE)
-    piece_at = lax.broadcasted_iota(jnp.int32, shape3, 0)
+    slot_ids = jnp.arange(halves * piece_rows, dtype=jnp.int32)
+    chosen = member_pos[None, :] == slot_ids[:, None]
+    shape3 = (halves, clusters, PIECE)
+    half_at = lax.broadcasted_iota(jnp.int32, shape3, 0)
     k_at = lax.broadcasted_iota(jnp.int32, shape3, 2)
-    have = jnp.where(
-        piece_at < halves,
-        jnp.broadcast_to(local_count[None, :, None], shape3),
-        jnp.broadcast_to(near_count[None, :, None], shape3),
-    )
-    present = (have > (piece_at % halves) * PIECE + k_at).reshape(-1)
+    have = jnp.broadcast_to(local_count[None, :, None], shape3)
+    present = (have > half_at * PIECE + k_at).reshape(-1)
     picked = lax.dot_general(
         chosen.astype(jnp.bfloat16),
         unit_embed,
@@ -64,7 +52,14 @@
         preferred_element_type=jnp.float32,
     )
     first = jnp.arange(feature_width, dtype=jnp.int32)[None, :] == 0
-    send = jnp.where(first & ~present[:, None], EMPTY, picked).astype(jnp.bfloat16)
+    member_send = jnp.where(first & ~present[:, None], EMPTY, picked).astype(jnp.bfloat16)
+    member_send = member_send.reshape(halves, clusters, PIECE * feature_width)
+    follow = (neighbours[:, None] == cluster_ids[None, :]).astype(jnp.bfloat16)
+    near_send = lax.dot_general(
+        follow, member_send, (((1,), (1,)), ((), ())), preferred_element_type=jnp.float32
+    ).astype(jnp.bfloat16)
+    near_send = near_send.transpose(1, 0, 2)
+    send = jnp.concatenate([member_send, near_send], axis=0)
     send = send.reshape(pieces, piece_rows, feature_width)
     arrived = lax.all_to_all(send, axes, split_axis=1, concat_axis=1, tiled=True)
     cluster_span = halves * piece_rows

time: 187 us -> 202 us (1.080)
  local copies, waits for them, and re-layouts: 13 us -> 24.7 us
  other arithmetic: 11.2 us -> 14.3 us
    concatenate x0 -> x3, local copies, waits for them, and re-layouts: none -> 11.8 us  [body(): send = jnp.concatenate([member_send, near_send], axis=0)]
    concatenate x0 -> x1, other arithmetic: none -> 4.86 us  [body(): send = jnp.concatenate([member_send, near_send], axis=0)]
    dot_general x0 -> x1, matrix products: none -> 2.21 us  [body(): lax.dot_general(follow, member_send, (((1,), (1,)), ((), ())), preferred_...]
    dot_general x1, matrix products: 5.89 us -> 3.82 us  [body(): lax.dot_general(chosen.astype(jnp.bfloat16), unit_embed, (((1,), (0,)), (...]
where the time goes in v7:
time: 202 us; the launch traced here: 201 us
  blocking collectives  124 us (61%)
  local copies, waits for them, and re-layouts  24.7 us (12%)
  matrix products  16.4 us (8%)
  other arithmetic  14.3 us (7%)
  waiting for transfers between devices  12.9 us (6%)
  starting transfers between devices  6.79 us (3%)
    all_to_all x1, blocking collectives, body(): lax.all_to_all(send, axes, split_axis=1, concat_axis=1, tiled=True)  124 us
    all_to_all x1, waiting for transfers between devices, body(): lax.all_to_all(payload, axes, split_axis=0, concat_axis=0, tiled=True)  12.9 us
    concatenate x3, local copies, waits for them, and re-layouts, body(): send = jnp.concatenate([member_send, near_send], axis=0)  11.8 us
    all_to_all x1, starting transfers between devices, body(): lax.all_to_all(payload, axes, split_axis=0, concat_axis=0, tiled=True)  6.79 us
    dot_general x1, matrix products, body(): lax.dot_general(members, members, (((1,), (1,)), ((), ())), preferred_ele...  5.65 us
    concatenate x1, other arithmetic, body(): send = jnp.concatenate([member_send, near_send], axis=0)  4.86 us
    slice x1, local copies, waits for them, and re-layouts, body(): others = arrived[halves:].reshape(cluster_span, feature_width)  4.67 us
    dot_general x1, matrix products, body(): lax.dot_general(members, others, (((1,), (1,)), ((), ())), preferred_elem...  4.34 us
  transfers between devices with their start and end apart: 1, of which 1 were waited for; matrix products, arithmetic and copies ran while one was open for 0% of the time, Pallas kernels for 0%

profile of v7, /device:TPU:1, one launch (start us, length us, event | category | flops | bytes accessed | tf_op | source)
XLA Modules:
  0.0 201.1 jit_solution(3760415464621720746)
XLA Ops:
  0.6 0.0 copy-start.1
  0.7 0.8 reduce.3
  1.5 0.2 convert_reduce_fusion.1
  1.7 0.4 convert_reduce_fusion
  2.1 1.9 multiply_reduce_fusion.1
  4.0 0.1 fusion.6
  4.1 0.2 not.12
  4.3 0.0 copy-done.1
  4.3 3.8 %select_convert_fusion = bf16[1536,768]{1,0:T(8,128)(2,1)} fusion(s32[768]{0:T(1024)S(1)} %fusion.12, pred[768]{0:T(1024)(128)(4,1)S(1)} %iota_compare_fusion.9, pred[1536]{0:T(1024)(128)(4,1)S(1)} %not.12, f32[768,768]{1,0:T(8,128)S(1)} %copy-done.1, f32[768]{0:T(1024)S(1)} %add_rsqrt_fusion), kind=kOutput, calls=%fused_computation.10 | convolution fusion | flops 1817837568 | bytes 4727040 | tf_op jit(solution)/shard_map/dot_general | solution.py:48
  8.2 3.7 %reshape.139 = bf16[2,256,2304]{2,1,0:T(8,128)(2,1)S(1)} reshape(bf16[1536,768]{1,0:T(8,128)(2,1)} %select_convert_fusion) | data formatting | bytes 4718592 | tf_op jit(solution)/shard_map/reshape | solution.py:56
  11.8 0.0 copy-start.3
  11.8 5.5 %copy.29 = bf16[2,768,768]{2,0,1:T(2,128)(2,1)} copy(bf16[2,768,768]{2,1,0:T(8,128)(2,1)} %bitcast.33) | data formatting | bytes 4718592 | tf_op jit(solution)/shard_map/concatenate | solution.py:62
  17.4 0.0 copy-done.3
  17.4 2.2 %fusion.2 = bf16[2,256,2304]{2,1,0:T(8,128)(2,1)} fusion(bf16[2,256,2304]{2,1,0:T(8,128)(2,1)S(1)} %reshape.139, s32[256]{0:T(256)S(1)} %copy-done.3), kind=kOutput, calls=%fused_computation.15 | convolution fusion | flops 605224960 | bytes 4719616 | tf_op jit(solution)/shard_map/dot_general | solution.py:58
  19.6 3.8 %concatenate.9 = bf16[2,768,768]{2,1,0:T(8,128)(2,1)S(1)} reshape(bf16[2,256,2304]{2,1,0:T(8,128)(2,1)} %fusion.2) | data formatting | bytes 4718592 | tf_op jit(solution)/shard_map/concatenate | solution.py:62
  23.4 0.0 copy-start
  23.4 2.4 %copy.30 = bf16[2,768,768]{2,0,1:T(2,128)(2,1)S(1)} copy(bf16[2,768,768]{2,1,0:T(8,128)(2,1)S(1)} %concatenate.9) | data formatting | bytes 4718592 | tf_op jit(solution)/shard_map/concatenate | solution.py:62
  25.9 0.0 copy-done
  25.9 4.9 %pad_maximum_fusion = bf16[4,768,768]{2,0,1:T(4,128)(2,1)S(1)} fusion(bf16[2,768,768]{2,0,1:T(2,128)(2,1)S(1)} %copy.30, bf16[2,768,768]{2,0,1:T(2,128)(2,1)S(1)} %copy-done), kind=kLoop, calls=%fused_computation.6 | loop fusion | flops 9437184 | bytes 9437184 | tf_op jit(solution)/shard_map/concatenate | solution.py:62
  30.7 124.4 %all_to_all.14 = bf16[4,768,768]{2,0,1:T(4,128)(2,1)S(1)} all-to-all(bf16[4,768,768]{2,0,1:T(4,128)(2,1)S(1)} %pad_maximum_fusion), channel_id=1, replica_groups=mesh['corpus'=32,'group'=8] {'corpus','group'}, dimensions={1} | all-to-all | bytes 9437184 | tf_op jit(solution)/shard_map/all_to_all | solution.py:64
  155.1 4.7 %fusion.14 = (bf16[2,768,768]{2,0,1:T(2,128)(2,1)}, bf16[2,768,768]{2,0,1:T(2,128)(2,1)S(1)}) fusion(bf16[4,768,768]{2,0,1:T(4,128)(2,1)S(1)} %all_to_all.14), kind=kLoop, calls=%fused_computation.52 | loop fusion | bytes 9437184 | tf_op jit(solution)/shard_map/slice | solution.py:67
  159.8 2.0 copy.40
  161.7 0.3 compare_reduce_fusion
  162.0 0.3 copy.39
  162.3 0.3 compare_reduce_fusion.1
  162.6 4.3 %select_reduce_fusion = f32[1536]{0:T(1024)S(1)} fusion(bf16[1536,768]{1,0:T(8,128)(2,1)S(1)} %bitcast.30, bf16[1536,768]{1,0:T(8,128)(2,1)S(1)} %bitcast.35, pred[1536]{0:T(1024)(128)(4,1)S(1)} %compare_reduce_fusion), kind=kOutput, calls=%fused_computation.2 | convolution fusion | flops 3630955008 | bytes 4726272 | tf_op jit(solution)/shard_map/dot_general | solution.py:83
  167.0 0.7 convert_reduce_fusion.2
  167.7 5.6 %select_reduce_fusion.1 = f32[1536]{0:T(1024)S(1)} fusion(bf16[1536,768]{1,0:T(8,128)(2,1)S(1)} %bitcast.31, pred[1536]{0:T(1024)(128)(4,1)S(1)} %compare_reduce_fusion.1), kind=kOutput, calls=%fused_computation.3 | convolution fusion | flops 3635673600 | bytes 2366976 | tf_op jit(solution)/shard_map/dot_general | solution.py:80
  173.3 0.4 convolution_reduce_fusion
  173.7 0.0 copy-start.2
  173.8 0.6 multiply_reduce_fusion.2
  175.1 0.5 multiply_reduce_fusion
  175.6 1.3 add_log_fusion
  177.0 0.2 log.8
  177.2 0.1 copy.33
  177.3 0.2 mul.100
  177.5 0.1 copy.34
  177.7 0.8 copy.35
  178.4 6.8 %all-to-all-start.1 = ((f32[256,1,12]{2,1,0:T(1,128)}), f32[256,1,12]{2,1,0:T(1,128)S(1)}, u32[]{:S(2)}, u32[]{:S(2)}) async-start(f32[256,1,12]{2,1,0:T(1,128)} %copy.35), calls=%async_computation.1 | async-start | bytes 262144 | tf_op jit(solution)/shard_map/all_to_all | solution.py:98
  185.3 0.0 copy-done.2
  185.3 12.9 %all-to-all-done.1 = f32[256,1,12]{2,1,0:T(1,128)S(1)} async-done(((f32[256,1,12]{2,1,0:T(1,128)}), f32[256,1,12]{2,1,0:T(1,128)S(1)}, u32[]{:S(2)}, u32[]{:S(2)}) %all-to-all-start.1) | async-done | bytes 12320 | tf_op jit(solution)/shard_map/all_to_all | solution.py:98
  198.2 0.1 copy.36
  198.3 0.1 copy.37
  198.5 0.1 broadcast_in_dim.67
  198.6 0.1 copy.38
  198.8 0.1 broadcast_in_dim.70
  198.9 2.2 %select_reduce_fusion.2 = (f32[768]{0:T(1024)}, f32[768]{0:T(1024)}) fusion(f32[1536]{0:T(1024)S(1)} %broadcast_in_dim.70, s32[768]{0:T(1024)S(1)} %add_reduce_fusion, f32[1536]{0:T(1024)S(1)} %broadcast_in_dim.67), kind=kLoop, calls=%fused_computation.7 | loop fusion | flops 5896704 | bytes 21504 | tf_op jit(solution)/shard_map/reduce_sum | solution.py:102
  (14 shorter events, 0.1 us)
Async XLA Ops:
  0.6 3.7 %copy-start.1 = (f32[768,768]{1,0:T(8,128)S(1)}, f32[768,768]{1,0:T(8,128)}, u32[]{:S(2)}) copy-start(f32[768,768]{1,0:T(8,128)} %param.3) | copy-start | bytes 7077892
  11.8 5.5 %copy-start.3 = (s32[256]{0:T(256)S(1)}, s32[256]{0:T(256)}, u32[]{:S(2)}) copy-start(s32[256]{0:T(256)} %param.5) | copy-start | bytes 3076
  23.4 2.4 %copy-start = (bf16[2,768,768]{2,0,1:T(2,128)(2,1)S(1)}, bf16[2,768,768]{2,0,1:T(2,128)(2,1)}, u32[]{:S(2)}) copy-start(bf16[2,768,768]{2,0,1:T(2,128)(2,1)} %copy.29) | copy-start | bytes 7077892
  173.7 11.5 %copy-start.2 = (s32[768,1]{0,1:T(1,128)S(1)}, s32[768,1]{0,1:T(1,128)}, u32[]{:S(2)}) copy-start(s32[768,1]{0,1:T(1,128)} %param.4) | copy-start | bytes 9220
  178.4 19.8 %all-to-all-start.1 = ((f32[256,1,12]{2,1,0:T(1,128)}), f32[256,1,12]{2,1,0:T(1,128)S(1)}, u32[]{:S(2)}, u32[]{:S(2)}) async-start(f32[256,1,12]{2,1,0:T(1,128)} %copy.35), calls=%async_computation.1 | async-start | bytes 262144 | tf_op jit(solution)/shard_map/all_to_all | solution.py:98

commit v8 on v4

--- a/solution.py
+++ b/solution.py
@@ -68,32 +68,48 @@
     send = send.reshape(pieces, piece_rows, feature_width)
     arrived = lax.all_to_all(send, axes, split_axis=1, concat_axis=1, tiled=True)
     cluster_span = halves * piece_rows
-    members = arrived[:halves].reshape(cluster_span, feature_width)
-    others = arrived[halves:].reshape(cluster_span, feature_width)
-    member_ok = members[:, 0] < 1.5
-    other_ok = others[:, 0] < 1.5
+    parts = [arrived[p] for p in range(pieces)]
+    oks = [part[:, 0] < 1.5 for part in parts]
+    member_ok = jnp.concatenate(oks[:halves])
+    other_ok = jnp.concatenate(oks[halves:])
     count_own = jnp.sum(member_ok.astype(jnp.float32))
     count_near = jnp.sum(other_ok.astype(jnp.float32))
-    sums = lax.dot_general(
-        member_ok.astype(jnp.bfloat16)[None, :],
-        members,
-        (((1,), (0,)), ((), ())),
-        preferred_element_type=jnp.float32,
+    sums = sum(
+        lax.dot_general(
+            oks[h].astype(jnp.bfloat16)[None, :],
+            parts[h],
+            (((1,), (0,)), ((), ())),
+            preferred_element_type=jnp.float32,
+        )
+        for h in range(halves)
     )
     centroid = normalize(sums)
-    typical = TYPICAL_SCALE * jnp.sum(members.astype(jnp.float32) * centroid, axis=1)
-    g_own = lax.dot_general(
-        members, members, (((1,), (1,)), ((), ())), preferred_element_type=jnp.float32
-    )
-    g_near = lax.dot_general(
-        members, others, (((1,), (1,)), ((), ())), preferred_element_type=jnp.float32
+    typical = jnp.concatenate(
+        [TYPICAL_SCALE * jnp.sum(parts[h].astype(jnp.float32) * centroid, axis=1) for h in range(halves)]
     )
     ids = jnp.arange(cluster_span, dtype=jnp.int32)
-    distinct = ids[:, None] != ids[None, :]
-    w_own = jnp.where(distinct & member_ok[None, :], jnp.exp(SHARPNESS * g_own), 0.0)
-    w_near = jnp.where(other_ok[None, :], jnp.exp(SHARPNESS * g_near), 0.0)
-    own_sum = jnp.sum(w_own, axis=1)
-    near_sum = jnp.sum(w_near, axis=1)
+    local = jnp.arange(piece_rows, dtype=jnp.int32)
+    same = local[:, None] == local[None, :]
+
+    def weights(queries, keys, ok, mask_self):
+        g = lax.dot_general(
+            queries, keys, (((1,), (1,)), ((), ())), preferred_element_type=jnp.float32
+        )
+        keep = ok[None, :] & ~same if mask_self else jnp.broadcast_to(ok[None, :], g.shape)
+        return jnp.sum(jnp.where(keep, jnp.exp(SHARPNESS * g), 0.0), axis=1)
+
+    own_sum = jnp.concatenate(
+        [
+            sum(weights(parts[h], parts[j], oks[j], h == j) for j in range(halves))
+            for h in range(halves)
+        ]
+    )
+    near_sum = jnp.concatenate(
+        [
+            sum(weights(parts[h], parts[halves + j], oks[halves + j], False) for j in range(halves))
+            for h in range(halves)
+        ]
+    )
     score = jnp.log(1.0 + own_sum / count_own + near_sum / count_near)
 
     def by_source(values):

time: 187 us -> 195 us (1.043)
  local copies, waits for them, and re-layouts: 13 us -> 16.4 us
  matrix products: 16.3 us -> 19.6 us
    dot_general x3 -> x10, matrix products: 10.4 us -> 13.7 us  [the longest x8 13.2 us: weights(): lax.dot_general(queries, keys, (((1,), (1,)), ((), ())), preferred_elemen...]
    add x0 -> x8, local copies, waits for them, and re-layouts: none -> 2.64 us  [the longest x4 2.1 us: body(): sum((weights(parts[h], parts[halves + j], oks[halves + j], False) for j i...]
    slice x1, local copies, waits for them, and re-layouts: 4.67 us -> 7.02 us  [body(): parts = [arrived[p] for p in range(pieces)]]
where the time goes in v8:
time: 195 us
  blocking collectives  124 us (64%)
  matrix products  19.6 us (10%)
  local copies, waits for them, and re-layouts  16.4 us (8%)
  other arithmetic  13 us (7%)
  waiting for transfers between devices  12.9 us (7%)
  starting transfers between devices  6.77 us (3%)
    all_to_all x1, blocking collectives, body(): lax.all_to_all(send, axes, split_axis=1, concat_axis=1, tiled=True)  124 us
    dot_general x8, matrix products, weights(): lax.dot_general(queries, keys, (((1,), (1,)), ((), ())), preferred_elemen...  13.2 us
    all_to_all x1, waiting for transfers between devices, body(): lax.all_to_all(payload, axes, split_axis=0, concat_axis=0, tiled=True)  12.9 us
    slice x1, local copies, waits for them, and re-layouts, body(): parts = [arrived[p] for p in range(pieces)]  7.02 us
    all_to_all x1, starting transfers between devices, body(): lax.all_to_all(payload, axes, split_axis=0, concat_axis=0, tiled=True)  6.77 us
    dot_general x1, matrix products, body(): lax.dot_general(chosen.astype(jnp.bfloat16), unit_embed, (((1,), (0,)), (...  5.9 us
  transfers between devices with their start and end apart: 1, of which 1 were waited for; matrix products, arithmetic and copies ran while one was open for 0% of the time, Pallas kernels for 0%

profile of v8, /device:TPU:1, one launch (start us, length us, event | category | flops | bytes accessed | tf_op | source)
XLA Modules:
  0.0 194.8 jit_solution(9851100709715182048)
XLA Ops:
  0.7 0.9 select_reduce_fusion.11
  1.6 0.7 reduce.2
  2.3 0.4 convert_reduce_fusion
  2.7 1.9 multiply_reduce_fusion.2
  4.6 0.3 select_reduce_fusion.10
  4.9 0.2 select_reduce_fusion.12
  5.1 0.2 fusion.12
  5.3 0.3 reshape.257
  5.7 5.9 %select_convert_fusion = bf16[3072,768]{1,0:T(8,128)(2,1)S(1)} fusion(pred[768]{0:T(1024)(128)(4,1)S(1)} %iota_compare_fusion.9, pred[3072]{0:T(1024)(128)(4,1)S(1)} %reshape.257, s32[768]{0:T(1024)S(1)} %get-tuple-element.17, s32[768]{0:T(1024)S(1)} %get-tuple-element.16, f32[768,768]{1,0:T(8,128)S(1)} %copy-done.1, f32[768]{0:T(1024)S(1)} %add_rsqrt_fusion), kind=kOutput, calls=%fused_computation | convolution fusion | flops 3639214080 | bytes 7090944 | tf_op jit(solution)/shard_map/dot_general | solution.py:60
  11.6 3.6 %copy.43 = bf16[4,768,768]{2,0,1:T(4,128)(2,1)S(1)} copy(bf16[4,768,768]{2,1,0:T(8,128)(2,1)S(1)} %bitcast.67) | data formatting | bytes 9437184 | tf_op jit(solution)/shard_map/reshape | solution.py:68
  15.3 124.3 %all_to_all.14 = bf16[4,768,768]{2,0,1:T(4,128)(2,1)S(1)} all-to-all(bf16[4,768,768]{2,0,1:T(4,128)(2,1)S(1)} %copy.43), channel_id=1, replica_groups=mesh['corpus'=32,'group'=8] {'corpus','group'}, dimensions={1} | all-to-all | bytes 9437184 | tf_op jit(solution)/shard_map/all_to_all | solution.py:69
  139.6 7.0 %fusion.15 = (bf16[1,768,768]{2,0,1:T(2,128)(2,1)S(1)}, bf16[1,768,768]{2,0,1:T(2,128)(2,1)S(1)}, bf16[1,768,768]{2,0,1:T(2,128)(2,1)S(1)}, bf16[1,768,768]{2,0,1:T(2,128)(2,1)S(1)}) fusion(bf16[4,768,768]{2,0,1:T(4,128)(2,1)S(1)} %all_to_all.14), kind=kLoop, calls=%fused_computation.75 | loop fusion | bytes 9437184 | tf_op jit(solution)/shard_map/slice | solution.py:71
  146.6 0.2 copy.74
  146.8 0.2 compare_reduce_fusion.2
  147.0 1.8 select_reduce_fusion.6
  148.9 0.2 copy.72
  149.0 0.2 compare_reduce_fusion
  149.2 0.2 copy.73
  149.4 0.2 compare_reduce_fusion.1
  149.6 1.2 select_reduce_fusion.2
  150.8 0.6 convert_reduce_fusion.2
  151.4 1.2 select_reduce_fusion.3
  152.7 0.2 copy.75
  152.8 1.8 select_reduce_fusion.4
  154.6 1.8 select_reduce_fusion.5
  156.4 0.2 compare_reduce_fusion.3
  156.6 1.8 select_reduce_fusion.8
  158.4 0.6 convert_reduce_fusion.3
  159.0 1.8 select_reduce_fusion.7
  160.8 1.8 select_reduce_fusion.9
  162.6 0.3 convolution_reduce_fusion
  162.9 0.8 add.177
  163.7 1.0 copy.51
  164.7 0.3 convolution_reduce_fusion.1
  165.0 0.6 multiply_reduce_fusion.3
  166.3 2.2 %multiply_reduce_fusion.1 = (f32[768]{0:T(1024)S(1)}, f32[768]{0:T(1024)S(1)}) fusion(f32[768]{0:T(1024)S(1)} %broadcast_multiply_fusion.2, bf16[1,768,768]{2,0,1:T(2,128)(2,1)S(1)} %get-tuple-element.12, bf16[1,768,768]{2,0,1:T(2,128)(2,1)} %copy-done), kind=kLoop, calls=%fused_computation.11 | loop fusion | flops 3537408 | bytes 2368512 | tf_op jit(solution)/shard_map/reduce_sum | solution.py:88
  168.6 0.2 mul.163
  168.8 0.2 mul.160
  169.2 0.2 add.169
  169.5 0.2 add.171
  169.8 0.2 add.175
  170.1 1.3 log_bitcast_fusion
  171.4 0.8 copy.56
  172.2 6.8 %all-to-all-start.1 = ((f32[256,1,12]{2,1,0:T(1,128)}), f32[256,1,12]{2,1,0:T(1,128)S(1)}, u32[]{:S(2)}, u32[]{:S(2)}) async-start(f32[256,1,12]{2,1,0:T(1,128)} %copy.56), calls=%async_computation.1 | async-start | bytes 262144 | tf_op jit(solution)/shard_map/all_to_all | solution.py:119
  179.0 12.9 %all-to-all-done.1 = f32[256,1,12]{2,1,0:T(1,128)S(1)} async-done(((f32[256,1,12]{2,1,0:T(1,128)}), f32[256,1,12]{2,1,0:T(1,128)S(1)}, u32[]{:S(2)}, u32[]{:S(2)}) %all-to-all-start.1) | async-done | bytes 12320 | tf_op jit(solution)/shard_map/all_to_all | solution.py:119
  192.0 0.1 copy.58
  192.2 0.1 broadcast_in_dim.143
  192.6 2.2 %select_reduce_fusion = (f32[768]{0:T(1024)}, f32[768]{0:T(1024)}) fusion(f32[1536]{0:T(1024)S(1)} %broadcast_in_dim.146, s32[768]{0:T(1024)S(1)} %add_reduce_fusion, f32[1536]{0:T(1024)S(1)} %broadcast_in_dim.143), kind=kLoop, calls=%fused_computation.5 | loop fusion | flops 5896704 | bytes 21504 | tf_op jit(solution)/shard_map/reduce_sum | solution.py:123
  (52 shorter events, 0.9 us)
Async XLA Ops:
  0.6 4.3 %copy-start.9 = (s32[256]{0:T(256)S(1)}, s32[256]{0:T(256)}, u32[]{:S(2)}) copy-start(s32[256]{0:T(256)} %param.5) | copy-start | bytes 3076
  0.6 5.0 %copy-start.1 = (f32[768,768]{1,0:T(8,128)S(1)}, f32[768,768]{1,0:T(8,128)}, u32[]{:S(2)}) copy-start(f32[768,768]{1,0:T(8,128)} %param.3) | copy-start | bytes 7077892
  146.6 6.0 %copy-start = (bf16[1,768,768]{2,0,1:T(2,128)(2,1)}, bf16[1,768,768]{2,0,1:T(2,128)(2,1)S(1)}, u32[]{:S(2)}) copy-start(bf16[1,768,768]{2,0,1:T(2,128)(2,1)S(1)} %get-tuple-element.13) | copy-start | bytes 3538948
  166.2 2.9 %copy-start.7 = (f32[768]{0:T(1024)S(1)}, f32[768]{0:T(1024)}, u32[]{:S(2)}) copy-start(f32[768]{0:T(1024)} %select_reduce_fusion.8) | copy-start | bytes 9220
  166.2 2.9 %copy-start.8 = (f32[768]{0:T(1024)S(1)}, f32[768]{0:T(1024)}, u32[]{:S(2)}) copy-start(f32[768]{0:T(1024)} %select_reduce_fusion.9) | copy-start | bytes 9220
  166.3 3.2 %copy-start.3 = (f32[768]{0:T(1024)S(1)}, f32[768]{0:T(1024)}, u32[]{:S(2)}) copy-start(f32[768]{0:T(1024)} %select_reduce_fusion.6) | copy-start | bytes 9220
  166.3 3.2 %copy-start.6 = (f32[768]{0:T(1024)S(1)}, f32[768]{0:T(1024)}, u32[]{:S(2)}) copy-start(f32[768]{0:T(1024)} %select_reduce_fusion.7) | copy-start | bytes 9220
  166.3 3.5 %copy-start.4 = (f32[768]{0:T(1024)S(1)}, f32[768]{0:T(1024)}, u32[]{:S(2)}) copy-start(f32[768]{0:T(1024)} %select_reduce_fusion.4) | copy-start | bytes 9220
  166.3 3.5 %copy-start.5 = (f32[768]{0:T(1024)S(1)}, f32[768]{0:T(1024)}, u32[]{:S(2)}) copy-start(f32[768]{0:T(1024)} %select_reduce_fusion.5) | copy-start | bytes 9220
  166.3 12.7 %copy-start.2 = (s32[768,1]{0,1:T(1,128)S(1)}, s32[768,1]{0,1:T(1,128)}, u32[]{:S(2)}) copy-start(s32[768,1]{0,1:T(1,128)} %param.4) | copy-start | bytes 9220
  172.2 19.8 %all-to-all-start.1 = ((f32[256,1,12]{2,1,0:T(1,128)}), f32[256,1,12]{2,1,0:T(1,128)S(1)}, u32[]{:S(2)}, u32[]{:S(2)}) async-start(f32[256,1,12]{2,1,0:T(1,128)} %copy.56), calls=%async_computation.1 | async-start | bytes 262144 | tf_op jit(solution)/shard_map/all_to_all | solution.py:119

commit v9 on v4

--- a/solution.py
+++ b/solution.py
@@ -1,6 +1,7 @@
 import jax
 import jax.numpy as jnp
 from jax import lax
+from jax.experimental.layout import Layout, with_layout_constraint
 from jax.sharding import PartitionSpec as P
 
 MOST = 6
@@ -46,8 +47,10 @@
     half = row_slot // PIECE
     member_pos = half * piece_rows + row_label * PIECE + within
     near_pos = (halves + half) * piece_rows + near_label * PIECE + within
-    slot_ids = jnp.arange(pieces * piece_rows, dtype=jnp.int32)
-    chosen = (member_pos[None, :] == slot_ids[:, None]) | (near_pos[None, :] == slot_ids[:, None])
+    slot_ids = jnp.arange(pieces * piece_rows, dtype=jnp.int32).reshape(pieces, piece_rows)
+    chosen = (member_pos[None, None, :] == slot_ids[:, :, None]) | (
+        near_pos[None, None, :] == slot_ids[:, :, None]
+    )
     shape3 = (pieces, clusters, PIECE)
     piece_at = lax.broadcasted_iota(jnp.int32, shape3, 0)
     k_at = lax.broadcasted_iota(jnp.int32, shape3, 2)
@@ -56,16 +59,16 @@
         jnp.broadcast_to(local_count[None, :, None], shape3),
         jnp.broadcast_to(near_count[None, :, None], shape3),
     )
-    present = (have > (piece_at % halves) * PIECE + k_at).reshape(-1)
+    present = (have > (piece_at % halves) * PIECE + k_at).reshape(pieces, piece_rows)
     picked = lax.dot_general(
         chosen.astype(jnp.bfloat16),
         unit_embed,
-        (((1,), (0,)), ((), ())),
+        (((2,), (0,)), ((), ())),
         preferred_element_type=jnp.float32,
     )
-    first = jnp.arange(feature_width, dtype=jnp.int32)[None, :] == 0
-    send = jnp.where(first & ~present[:, None], EMPTY, picked).astype(jnp.bfloat16)
-    send = send.reshape(pieces, piece_rows, feature_width)
+    first = jnp.arange(feature_width, dtype=jnp.int32)[None, None, :] == 0
+    send = jnp.where(first & ~present[:, :, None], EMPTY, picked).astype(jnp.bfloat16)
+    send = with_layout_constraint(send, Layout(major_to_minor=(1, 0, 2)))
     arrived = lax.all_to_all(send, axes, split_axis=1, concat_axis=1, tiled=True)
     cluster_span = halves * piece_rows
     members = arrived[:halves].reshape(cluster_span, feature_width)

time: 187 us -> 197 us (1.053)
  other arithmetic: 11.2 us -> 24.2 us
    convert_element_type x0 -> x1, other arithmetic: none -> 8.91 us  [body(): jnp.where(first & ~present[:, :, None], EMPTY, picked).astype(jnp.bfloat16)]
    reduce_sum x1, other arithmetic: 0.55 us -> 4.86 us  [body(): jnp.sum(members.astype(jnp.float32) * centroid, axis=1)]
    reshape x1 -> x0, local copies, waits for them, and re-layouts: 3.64 us -> none  [body(): send = send.reshape(pieces, piece_rows, feature_width)]
    unnamed x8 -> x11, local copies, waits for them, and re-layouts: 2.28 us -> 0.17 us
    slice x1 -> x2, local copies, waits for them, and re-layouts: 4.67 us -> 5.79 us  [body(): others = arrived[halves:].reshape(cluster_span, feature_width)]
where the time goes in v9:
time: 197 us; the launch traced here: 196 us
  blocking collectives  124 us (63%)
  other arithmetic  24.2 us (12%)
  matrix products  15.5 us (8%)
  waiting for transfers between devices  12.9 us (7%)
  local copies, waits for them, and re-layouts  11.1 us (6%)
  starting transfers between devices  6.79 us (3%)
    all_to_all x1, blocking collectives, body(): lax.all_to_all(send, axes, split_axis=1, concat_axis=1, tiled=True)  124 us
    all_to_all x1, waiting for transfers between devices, body(): lax.all_to_all(payload, axes, split_axis=0, concat_axis=0, tiled=True)  12.9 us
    convert_element_type x1, other arithmetic, body(): jnp.where(first & ~present[:, :, None], EMPTY, picked).astype(jnp.bfloat16)  8.91 us
    all_to_all x1, starting transfers between devices, body(): lax.all_to_all(payload, axes, split_axis=0, concat_axis=0, tiled=True)  6.79 us
    slice x2, local copies, waits for them, and re-layouts, body(): others = arrived[halves:].reshape(cluster_span, feature_width)  5.79 us
    dot_general x1, matrix products, body(): lax.dot_general(members, members, (((1,), (1,)), ((), ())), preferred_ele...  5.65 us
    reduce_sum x1, other arithmetic, body(): jnp.sum(members.astype(jnp.float32) * centroid, axis=1)  4.86 us
    dot_general x1, matrix products, body(): lax.dot_general(chosen.astype(jnp.bfloat16), unit_embed, (((2,), (0,)), (...  4.81 us
  transfers between devices with their start and end apart: 1, of which 1 were waited for; matrix products, arithmetic and copies ran while one was open for 0% of the time, Pallas kernels for 0%

profile of v9, /device:TPU:1, one launch (start us, length us, event | category | flops | bytes accessed | tf_op | source)
XLA Modules:
  0.0 196.5 jit_solution(7724931046286897833)
XLA Ops:
  0.6 0.0 copy-start.4
  0.6 0.0 copy-start.2
  0.7 0.9 select_reduce_fusion.5
  1.7 0.7 reduce.3
  2.4 0.4 convert_reduce_fusion
  2.7 0.3 convert_reduce_fusion.1
  3.0 1.9 multiply_reduce_fusion.1
  4.9 0.0 copy-done.4
  5.0 0.2 select_reduce_fusion.6
  5.1 0.1 broadcast_in_dim.115
  5.2 0.2 broadcast_in_dim.116
  5.5 0.1 broadcast_in_dim.110
  5.5 0.2 broadcast_in_dim.111
  5.8 0.2 iota.74
  6.0 0.1 fusion.13
  6.1 0.2 copy.33
  6.3 0.0 copy-done.2
  6.3 4.8 %fusion.2 = bf16[4,768,768]{2,1,0:T(8,128)(2,1)S(1)} fusion(s32[768]{0:T(1024)S(1)} %get-tuple-element.11, s32[4,768]{1,0:T(4,128)S(1)} %multiply_add_fusion, s32[768]{0:T(1024)S(1)} %get-tuple-element.10, f32[768,768]{1,0:T(8,128)S(1)} %copy-done.2, f32[768]{0:T(1024)S(1)} %add_rsqrt_fusion), kind=kOutput, calls=%fused_computation.8 | convolution fusion | flops 3632136192 | bytes 7099392 | tf_op jit(solution)/shard_map/dot_general | solution.py:63
  11.2 8.9 %fusion = bf16[4,768,768]{2,0,1:T(4,128)(2,1)S(1)} fusion(bf16[4,768,768]{2,1,0:T(8,128)(2,1)S(1)} %fusion.2, pred[4,768]{0,1:T(8,128)(4,1)S(1)} %copy.33, pred[768]{0:T(1024)(128)(4,1)S(1)} %iota_compare_fusion.6), kind=kLoop, calls=%fused_computation.3 | loop fusion | flops 4718592 | bytes 9441024 | tf_op jit(solution)/shard_map/convert_element_type | solution.py:70
  20.1 124.4 %all_to_all.14 = bf16[4,768,768]{2,0,1:T(4,128)(2,1)S(1)} all-to-all(bf16[4,768,768]{2,0,1:T(4,128)(2,1)S(1)} %fusion), channel_id=1, replica_groups=mesh['corpus'=32,'group'=8] {'corpus','group'}, dimensions={1} | all-to-all | bytes 9437184 | tf_op jit(solution)/shard_map/all_to_all | solution.py:72
  144.4 5.5 %fusion.15 = (bf16[2,768,768]{2,0,1:T(2,128)(2,1)}, bf16[2,768,768]{2,0,1:T(2,128)(2,1)}) fusion(bf16[4,768,768]{2,0,1:T(4,128)(2,1)S(1)} %all_to_all.14), kind=kLoop, calls=%fused_computation.60 | loop fusion | bytes 9437184 | tf_op jit(solution)/shard_map/slice | solution.py:75
  149.9 2.0 copy.35
  151.9 0.3 compare_reduce_fusion.1
  152.2 5.7 %select_reduce_fusion.1 = f32[1536]{0:T(1024)S(1)} fusion(bf16[1536,768]{1,0:T(8,128)(2,1)S(1)} %bitcast.26, pred[1536]{0:T(1024)(128)(4,1)S(1)} %compare_reduce_fusion.1), kind=kOutput, calls=%fused_computation.5 | convolution fusion | flops 3635673600 | bytes 2366976 | tf_op jit(solution)/shard_map/dot_general | solution.py:88
  157.9 0.6 convert_reduce_fusion.3
  158.5 0.3 copy.36
  158.8 0.3 compare_reduce_fusion
  159.0 4.6 %select_reduce_fusion = f32[1536]{0:T(1024)S(1)} fusion(bf16[1536,768]{1,0:T(8,128)(2,1)S(1)} %bitcast.27, bf16[1536,768]{1,0:T(8,128)(2,1)S(1)} %bitcast.30, pred[1536]{0:T(1024)(128)(4,1)S(1)} %compare_reduce_fusion), kind=kOutput, calls=%fused_computation.4 | convolution fusion | flops 3630955008 | bytes 4726272 | tf_op jit(solution)/shard_map/dot_general | solution.py:91
  163.6 0.6 convert_reduce_fusion.2
  164.2 1.3 add_log_fusion
  165.5 0.2 log.8
  165.8 0.1 copy.37
  165.9 0.4 convolution_reduce_fusion
  166.3 0.6 multiply_reduce_fusion.2
  167.6 0.0 copy-start.3
  167.6 4.9 %multiply_reduce_fusion = f32[2,768]{0,1:T(8,128)S(1)} fusion(f32[768]{0:T(1024)S(1)} %broadcast_multiply_fusion.1, bf16[4,768,768]{2,0,1:T(4,128)(2,1)} %copy-done), kind=kLoop, calls=%fused_computation.14 | loop fusion | flops 3537408 | bytes 2368512 | tf_op jit(solution)/shard_map/reduce_sum | solution.py:87
  172.5 0.1 copy.44
  172.7 0.2 mul.115
  172.9 0.1 copy.39
  173.1 0.8 copy.40
  173.8 6.8 %all-to-all-start.1 = ((f32[256,1,12]{2,1,0:T(1,128)}), f32[256,1,12]{2,1,0:T(1,128)S(1)}, u32[]{:S(2)}, u32[]{:S(2)}) async-start(f32[256,1,12]{2,1,0:T(1,128)} %copy.40), calls=%async_computation.1 | async-start | bytes 262144 | tf_op jit(solution)/shard_map/all_to_all | solution.py:106
  180.7 12.9 %all-to-all-done.1 = f32[256,1,12]{2,1,0:T(1,128)S(1)} async-done(((f32[256,1,12]{2,1,0:T(1,128)}), f32[256,1,12]{2,1,0:T(1,128)S(1)}, u32[]{:S(2)}, u32[]{:S(2)}) %all-to-all-start.1) | async-done | bytes 12320 | tf_op jit(solution)/shard_map/all_to_all | solution.py:106
  193.6 0.1 copy.41
  193.7 0.1 copy.42
  193.8 0.1 broadcast_in_dim.123
  194.0 0.1 copy.43
  194.1 0.1 broadcast_in_dim.126
  194.3 2.2 %select_reduce_fusion.2 = (f32[768]{0:T(1024)}, f32[768]{0:T(1024)}) fusion(f32[1536]{0:T(1024)S(1)} %broadcast_in_dim.126, s32[768]{0:T(1024)S(1)} %add_reduce_fusion, f32[1536]{0:T(1024)S(1)} %broadcast_in_dim.123), kind=kLoop, calls=%fused_computation.12 | loop fusion | flops 5896704 | bytes 21504 | tf_op jit(solution)/shard_map/reduce_sum | solution.py:110
  (22 shorter events, 0.2 us)
Async XLA Ops:
  0.6 4.3 %copy-start.4 = (s32[256]{0:T(256)S(1)}, s32[256]{0:T(256)}, u32[]{:S(2)}) copy-start(s32[256]{0:T(256)} %param.5) | copy-start | bytes 3076
  0.6 5.7 %copy-start.2 = (f32[768,768]{1,0:T(8,128)S(1)}, f32[768,768]{1,0:T(8,128)}, u32[]{:S(2)}) copy-start(f32[768,768]{1,0:T(8,128)} %param.3) | copy-start | bytes 7077892
  144.4 5.5 %copy-start = (bf16[4,768,768]{2,0,1:T(4,128)(2,1)}, bf16[4,768,768]{2,0,1:T(4,128)(2,1)S(1)}, u32[]{:S(2)}) copy-start(bf16[4,768,768]{2,0,1:T(4,128)(2,1)S(1)} %all_to_all.14) | copy-start | bytes 14155780
  152.2 6.3 %copy-start.1 = (bf16[2,768,768]{2,0,1:T(2,128)(2,1)S(1)}, bf16[2,768,768]{2,0,1:T(2,128)(2,1)}, u32[]{:S(2)}) copy-start(bf16[2,768,768]{2,0,1:T(2,128)(2,1)} %get-tuple-element.6) | copy-start | bytes 7077892
  167.6 13.0 %copy-start.3 = (s32[768,1]{0,1:T(1,128)S(1)}, s32[768,1]{0,1:T(1,128)}, u32[]{:S(2)}) copy-start(s32[768,1]{0,1:T(1,128)} %param.4) | copy-start | bytes 9220
  173.8 19.8 %all-to-all-start.1 = ((f32[256,1,12]{2,1,0:T(1,128)}), f32[256,1,12]{2,1,0:T(1,128)S(1)}, u32[]{:S(2)}, u32[]{:S(2)}) async-start(f32[256,1,12]{2,1,0:T(1,128)} %copy.40), calls=%async_computation.1 | async-start | bytes 262144 | tf_op jit(solution)/shard_map/all_to_all | solution.py:106

commit v10 on v4

--- a/solution.py
+++ b/solution.py
@@ -10,7 +10,7 @@
 TYPICAL_SCALE = 8.0
 EPSILON = 1e-06
 EMPTY = 2.0
-PIECE = 3
+PIECE = 6
 
 
 def normalize(values):

time: 187 us -> 217 us (1.16)
  local copies, waits for them, and re-layouts: 13 us -> 43.3 us
    reshape x1, local copies, waits for them, and re-layouts: 3.64 us -> 33.8 us  [body(): send = send.reshape(pieces, piece_rows, feature_width)]
    unnamed x8 -> x6, local copies, waits for them, and re-layouts: 2.28 us -> 0.02 us
where the time goes in v10:
time: 217 us; the launch traced here: 216 us
  blocking collectives  124 us (57%)
  local copies, waits for them, and re-layouts  43.3 us (20%)
  matrix products  16.3 us (8%)
  waiting for transfers between devices  12.9 us (6%)
  other arithmetic  11.2 us (5%)
  starting transfers between devices  6.79 us (3%)
    all_to_all x1, blocking collectives, body(): lax.all_to_all(send, axes, split_axis=1, concat_axis=1, tiled=True)  124 us
    reshape x1, local copies, waits for them, and re-layouts, body(): send = send.reshape(pieces, piece_rows, feature_width)  33.8 us
    all_to_all x1, waiting for transfers between devices, body(): lax.all_to_all(payload, axes, split_axis=0, concat_axis=0, tiled=True)  12.9 us
    all_to_all x1, starting transfers between devices, body(): lax.all_to_all(payload, axes, split_axis=0, concat_axis=0, tiled=True)  6.79 us
    slice x1, local copies, waits for them, and re-layouts, body(): others = arrived[halves:].reshape(cluster_span, feature_width)  6.68 us
    dot_general x1, matrix products, body(): lax.dot_general(chosen.astype(jnp.bfloat16), unit_embed, (((1,), (0,)), (...  5.89 us
    dot_general x1, matrix products, body(): lax.dot_general(members, members, (((1,), (1,)), ((), ())), preferred_ele...  5.64 us
    dot_general x1, matrix products, body(): lax.dot_general(members, others, (((1,), (1,)), ((), ())), preferred_elem...  4.36 us
  transfers between devices with their start and end apart: 1, of which 1 were waited for; matrix products, arithmetic and copies ran while one was open for 0% of the time, Pallas kernels for 0%

profile of v10, /device:TPU:1, one launch (start us, length us, event | category | flops | bytes accessed | tf_op | source)
XLA Modules:
  0.0 216.4 jit_solution(8035599352689006764)
XLA Ops:
  0.6 0.0 copy-start.2
  0.6 0.0 copy-start
  0.7 0.9 select_reduce_fusion.5
  1.6 0.7 reduce.2
  2.3 0.4 convert_reduce_fusion
  2.7 1.9 multiply_reduce_fusion.1
  4.6 0.3 select_reduce_fusion.4
  4.9 0.0 copy-done.2
  4.9 0.2 select_reduce_fusion.6
  5.1 0.1 fusion.10
  5.3 0.2 not.12
  5.5 0.0 copy-done
  5.5 5.9 %select_convert_fusion = bf16[3072,768]{1,0:T(8,128)(2,1)S(1)} fusion(pred[768]{0:T(1024)(128)(4,1)S(1)} %iota_compare_fusion.10, pred[3072]{0:T(1024)(128)(4,1)S(1)} %not.12, s32[768]{0:T(1024)S(1)} %get-tuple-element.11, s32[768]{0:T(1024)S(1)} %get-tuple-element.10, f32[768,768]{1,0:T(8,128)S(1)} %copy-done, f32[768]{0:T(1024)S(1)} %add_rsqrt_fusion), kind=kOutput, calls=%fused_computation.4 | convolution fusion | flops 3639214080 | bytes 7090944 | tf_op jit(solution)/shard_map/dot_general | solution.py:60
  11.4 33.8 %copy.28 = bf16[2,1536,768]{2,0,1:T(2,128)(2,1)S(1)} copy(bf16[2,1536,768]{2,1,0:T(8,128)(2,1)S(1)} %bitcast.19) | data formatting | bytes 9437184 | tf_op jit(solution)/shard_map/reshape | solution.py:68
  45.2 124.3 %all_to_all.14 = bf16[2,1536,768]{2,0,1:T(2,128)(2,1)S(1)} all-to-all(bf16[2,1536,768]{2,0,1:T(2,128)(2,1)S(1)} %copy.28), channel_id=1, replica_groups=mesh['corpus'=32,'group'=8] {'corpus','group'}, dimensions={1} | all-to-all | bytes 9437184 | tf_op jit(solution)/shard_map/all_to_all | solution.py:69
  169.5 6.7 %fusion.12 = (bf16[1,1536,768]{2,0,1:T(2,128)(2,1)S(1)}, bf16[1,1536,768]{2,0,1:T(2,128)(2,1)S(1)}) fusion(bf16[2,1536,768]{2,0,1:T(2,128)(2,1)S(1)} %all_to_all.14), kind=kLoop, calls=%fused_computation.55 | loop fusion | bytes 9437184 | tf_op jit(solution)/shard_map/slice | solution.py:72
  176.2 0.8 copy_bitcast_fusion
  177.0 0.3 compare_reduce_fusion.1
  177.3 0.3 compare_reduce_fusion
  177.6 0.6 convert_reduce_fusion.2
  178.2 4.4 %select_reduce_fusion = f32[1536]{0:T(1024)S(1)} fusion(bf16[1536,768]{1,0:T(8,128)(2,1)S(1)} %get-tuple-element.13, bf16[1536,768]{1,0:T(8,128)(2,1)S(1)} %get-tuple-element.12, pred[1536]{0:T(1024)(128)(4,1)S(1)} %compare_reduce_fusion), kind=kOutput, calls=%fused_computation.2 | convolution fusion | flops 3630955008 | bytes 4726272 | tf_op jit(solution)/shard_map/dot_general | solution.py:88
  182.6 0.7 convert_reduce_fusion.3
  183.3 5.6 %select_reduce_fusion.1 = f32[1536]{0:T(1024)S(1)} fusion(bf16[1536,768]{1,0:T(8,128)(2,1)S(1)} %get-tuple-element.13, pred[1536]{0:T(1024)(128)(4,1)S(1)} %compare_reduce_fusion.1), kind=kOutput, calls=%fused_computation.3 | convolution fusion | flops 3635673600 | bytes 2366976 | tf_op jit(solution)/shard_map/dot_general | solution.py:85
  188.9 0.4 convolution_reduce_fusion
  189.4 0.0 copy-start.1
  189.4 0.6 multiply_reduce_fusion.2
  190.7 0.5 multiply_reduce_fusion
  191.2 0.1 mul.108
  191.4 1.3 add_log_fusion
  192.7 0.1 log.14
  192.9 0.1 copy.31
  193.0 0.8 copy.32
  193.8 6.8 %all-to-all-start.1 = ((f32[256,1,12]{2,1,0:T(1,128)}), f32[256,1,12]{2,1,0:T(1,128)S(1)}, u32[]{:S(2)}, u32[]{:S(2)}) async-start(f32[256,1,12]{2,1,0:T(1,128)} %copy.32), calls=%async_computation.1 | async-start | bytes 262144 | tf_op jit(solution)/shard_map/all_to_all | solution.py:103
  200.6 0.0 copy-done.1
  200.6 12.9 %all-to-all-done.1 = f32[256,1,12]{2,1,0:T(1,128)S(1)} async-done(((f32[256,1,12]{2,1,0:T(1,128)}), f32[256,1,12]{2,1,0:T(1,128)S(1)}, u32[]{:S(2)}, u32[]{:S(2)}) %all-to-all-start.1) | async-done | bytes 12320 | tf_op jit(solution)/shard_map/all_to_all | solution.py:103
  213.6 0.1 copy.33
  213.6 0.1 copy.34
  213.8 0.1 broadcast_in_dim.113
  213.9 0.1 copy.35
  214.1 0.1 broadcast_in_dim.116
  214.2 2.2 %select_reduce_fusion.2 = (f32[768]{0:T(1024)}, f32[768]{0:T(1024)}) fusion(f32[1536]{0:T(1024)S(1)} %broadcast_in_dim.116, s32[768]{0:T(1024)S(1)} %add_reduce_fusion, f32[1536]{0:T(1024)S(1)} %broadcast_in_dim.113), kind=kLoop, calls=%fused_computation.11 | loop fusion | flops 5896704 | bytes 21504 | tf_op jit(solution)/shard_map/reduce_sum | solution.py:107
  (12 shorter events, 0.1 us)
Async XLA Ops:
  0.6 4.3 %copy-start.2 = (s32[256]{0:T(256)S(1)}, s32[256]{0:T(256)}, u32[]{:S(2)}) copy-start(s32[256]{0:T(256)} %param.5) | copy-start | bytes 3076
  0.6 4.8 %copy-start = (f32[768,768]{1,0:T(8,128)S(1)}, f32[768,768]{1,0:T(8,128)}, u32[]{:S(2)}) copy-start(f32[768,768]{1,0:T(8,128)} %param.3) | copy-start | bytes 7077892
  189.4 11.2 %copy-start.1 = (s32[768,1]{0,1:T(1,128)S(1)}, s32[768,1]{0,1:T(1,128)}, u32[]{:S(2)}) copy-start(s32[768,1]{0,1:T(1,128)} %param.4) | copy-start | bytes 9220
  193.8 19.8 %all-to-all-start.1 = ((f32[256,1,12]{2,1,0:T(1,128)}), f32[256,1,12]{2,1,0:T(1,128)S(1)}, u32[]{:S(2)}, u32[]{:S(2)}) async-start(f32[256,1,12]{2,1,0:T(1,128)} %copy.32), calls=%async_computation.1 | async-start | bytes 262144 | tf_op jit(solution)/shard_map/all_to_all | solution.py:103

commit v11 on v4

--- a/solution.py
+++ b/solution.py
@@ -68,12 +68,12 @@
     send = send.reshape(pieces, piece_rows, feature_width)
     arrived = lax.all_to_all(send, axes, split_axis=1, concat_axis=1, tiled=True)
     cluster_span = halves * piece_rows
-    members = arrived[:halves].reshape(cluster_span, feature_width)
-    others = arrived[halves:].reshape(cluster_span, feature_width)
-    member_ok = members[:, 0] < 1.5
-    other_ok = others[:, 0] < 1.5
+    keys = arrived.reshape(pieces * piece_rows, feature_width)
+    members = keys[:cluster_span]
+    key_ok = keys[:, 0] < 1.5
+    member_ok = key_ok[:cluster_span]
     count_own = jnp.sum(member_ok.astype(jnp.float32))
-    count_near = jnp.sum(other_ok.astype(jnp.float32))
+    count_near = jnp.sum(key_ok[cluster_span:].astype(jnp.float32))
     sums = lax.dot_general(
         member_ok.astype(jnp.bfloat16)[None, :],
         members,
@@ -82,18 +82,16 @@
     )
     centroid = normalize(sums)
     typical = TYPICAL_SCALE * jnp.sum(members.astype(jnp.float32) * centroid, axis=1)
-    g_own = lax.dot_general(
-        members, members, (((1,), (1,)), ((), ())), preferred_element_type=jnp.float32
-    )
-    g_near = lax.dot_general(
-        members, others, (((1,), (1,)), ((), ())), preferred_element_type=jnp.float32
+    g = lax.dot_general(
+        members, keys, (((1,), (1,)), ((), ())), preferred_element_type=jnp.float32
     )
     ids = jnp.arange(cluster_span, dtype=jnp.int32)
-    distinct = ids[:, None] != ids[None, :]
-    w_own = jnp.where(distinct & member_ok[None, :], jnp.exp(SHARPNESS * g_own), 0.0)
-    w_near = jnp.where(other_ok[None, :], jnp.exp(SHARPNESS * g_near), 0.0)
-    own_sum = jnp.sum(w_own, axis=1)
-    near_sum = jnp.sum(w_near, axis=1)
+    col_ids = jnp.arange(pieces * piece_rows, dtype=jnp.int32)
+    weights = jnp.exp(SHARPNESS * g)
+    own_keep = (col_ids[None, :] < cluster_span) & (col_ids[None, :] != ids[:, None]) & key_ok[None, :]
+    near_keep = (col_ids[None, :] >= cluster_span) & key_ok[None, :]
+    own_sum = jnp.sum(jnp.where(own_keep, weights, 0.0), axis=1)
+    near_sum = jnp.sum(jnp.where(near_keep, weights, 0.0), axis=1)
     score = jnp.log(1.0 + own_sum / count_own + near_sum / count_near)
 
     def by_source(values):

time: 187 us -> 192 us (1.027)
  blocking collectives: 124 us -> 0 us
  waiting for transfers between devices: 12.9 us -> 121 us
  starting transfers between devices: 6.79 us -> 23.4 us
  matrix products: 16.3 us -> 20.7 us
  other arithmetic: 11.2 us -> 13.7 us
    all_to_all x1 -> x0, blocking collectives: 124 us -> none  [body(): lax.all_to_all(send, axes, split_axis=1, concat_axis=1, tiled=True)]
    all_to_all x0 -> x1, waiting for transfers between devices: none -> 108 us  [body(): lax.all_to_all(send, axes, split_axis=1, concat_axis=1, tiled=True)]
    all_to_all x0 -> x1, starting transfers between devices: none -> 16.5 us  [body(): lax.all_to_all(send, axes, split_axis=1, concat_axis=1, tiled=True)]
    slice x1 -> x3, local copies, waits for them, and re-layouts: 4.67 us -> 0.45 us  [the longest x2 0.29 us: body(): member_ok = key_ok[:cluster_span]]
    all_to_all x0 -> x1, local copies, waits for them, and re-layouts: none -> 2.94 us  [body(): lax.all_to_all(send, axes, split_axis=1, concat_axis=1, tiled=True)]
    dot_general x2 -> x1, matrix products: 9.99 us -> 12.7 us  [body(): lax.dot_general(members, keys, (((1,), (1,)), ((), ())), preferred_elemen...]
    unnamed x8 -> x4, local copies, waits for them, and re-layouts: 2.28 us -> 0.01 us
    reshape x1, local copies, waits for them, and re-layouts: 3.64 us -> 5.81 us  [body(): send = send.reshape(pieces, piece_rows, feature_width)]
  transfers between devices with their start and end apart: 1 -> 2, of which waited for: 1 -> 2; matrix products, arithmetic and copies ran while one was open for 0% -> 0% of each run, Pallas kernels for 0% -> 0%
where the time goes in v11:
time: 192 us
  waiting for transfers between devices  121 us (63%)
  starting transfers between devices  23.4 us (12%)
  matrix products  20.7 us (11%)
  other arithmetic  13.7 us (7%)
  local copies, waits for them, and re-layouts  11.6 us (6%)
    all_to_all x1, waiting for transfers between devices, body(): lax.all_to_all(send, axes, split_axis=1, concat_axis=1, tiled=True)  108 us
    all_to_all x1, starting transfers between devices, body(): lax.all_to_all(send, axes, split_axis=1, concat_axis=1, tiled=True)  16.5 us
    all_to_all x1, waiting for transfers between devices, body(): lax.all_to_all(payload, axes, split_axis=0, concat_axis=0, tiled=True)  12.9 us
    dot_general x1, matrix products, body(): lax.dot_general(members, keys, (((1,), (1,)), ((), ())), preferred_elemen...  12.7 us
    dot_general x1, matrix products, body(): lax.dot_general(chosen.astype(jnp.bfloat16), unit_embed, (((1,), (0,)), (...  7.57 us
    all_to_all x1, starting transfers between devices, body(): lax.all_to_all(payload, axes, split_axis=0, concat_axis=0, tiled=True)  6.84 us
    reshape x1, local copies, waits for them, and re-layouts, body(): send = send.reshape(pieces, piece_rows, feature_width)  5.81 us
  transfers between devices with their start and end apart: 2, of which 2 were waited for; matrix products, arithmetic and copies ran while one was open for 0% of the time, Pallas kernels for 0%

profile of v11, /device:TPU:1, one launch (start us, length us, event | category | flops | bytes accessed | tf_op | source)
XLA Modules:
  0.0 192.1 jit_solution(9874803340465522303)
XLA Ops:
  0.7 0.8 select_reduce_fusion.5
  1.5 0.7 reduce.4
  2.2 0.4 convert_reduce_fusion
  2.5 0.3 select_reduce_fusion.4
  2.8 0.9 select_reduce_fusion.6
  3.7 0.2 fusion.11
  3.9 0.3 reshape.191
  4.3 1.9 multiply_reduce_fusion.1
  6.2 7.6 %select_convert_fusion = bf16[3072,768]{1,0:T(8,128)(2,1)S(1)} fusion(pred[768]{0:T(1024)(128)(4,1)S(1)} %iota_compare_fusion.11, pred[3072]{0:T(1024)(128)(4,1)S(1)} %reshape.191, s32[768]{0:T(1024)S(1)} %get-tuple-element.13, s32[768]{0:T(1024)S(1)} %get-tuple-element.12, f32[768,768]{1,0:T(8,128)} %param.3, f32[768]{0:T(1024)S(1)} %add_rsqrt_fusion), kind=kOutput, calls=%fused_computation.6 | convolution fusion | flops 3639214080 | bytes 7090944 | tf_op jit(solution)/shard_map/dot_general | solution.py:60
  13.8 5.8 %copy.26 = bf16[4,768,768]{2,0,1:T(4,128)(2,1)} copy(bf16[4,768,768]{2,1,0:T(8,128)(2,1)S(1)} %bitcast.25) | data formatting | bytes 9437184 | tf_op jit(solution)/shard_map/reshape | solution.py:68
  19.6 16.5 %all-to-all-start = ((bf16[4,768,768]{2,0,1:T(4,128)(2,1)}), bf16[4,768,768]{2,0,1:T(4,128)(2,1)}, u32[]{:S(2)}, u32[]{:S(2)}) async-start(bf16[4,768,768]{2,0,1:T(4,128)(2,1)} %copy.26), calls=%async_computation | async-start | bytes 9437184 | tf_op jit(solution)/shard_map/all_to_all | solution.py:69
  36.1 108.1 %all-to-all-done = bf16[4,768,768]{2,0,1:T(4,128)(2,1)} async-done(((bf16[4,768,768]{2,0,1:T(4,128)(2,1)}), bf16[4,768,768]{2,0,1:T(4,128)(2,1)}, u32[]{:S(2)}, u32[]{:S(2)}) %all-to-all-start) | async-done | bytes 4718624 | tf_op jit(solution)/shard_map/all_to_all | solution.py:69
  144.2 2.9 %copy.27 = bf16[4,768,768]{2,1,0:T(8,128)(2,1)S(1)} copy(bf16[4,768,768]{2,0,1:T(4,128)(2,1)} %all-to-all-done) | data formatting | bytes 9437184 | tf_op jit(solution)/shard_map/all_to_all | solution.py:69
  147.2 0.0 copy-start
  147.2 0.2 slice.34
  147.3 0.5 fusion.14
  147.8 0.3 slice_reduce_fusion
  148.1 1.1 convert_reduce_fusion.1
  149.2 0.6 convert_reduce_fusion.3
  149.9 12.7 %select_reduce_fusion.1 = (f32[1536]{0:T(1024)S(1)}, f32[1536]{0:T(1024)S(1)}) fusion(pred[3072]{0:T(1024)(128)(4,1)S(1)} %get-tuple-element.8, pred[3072]{0:T(1024)(128)(4,1)S(1)} %iota_compare_fusion.10, pred[3072]{0:T(1024)(128)(4,1)S(1)} %fusion.12, bf16[1536,768]{1,0:T(8,128)(2,1)S(1)} %bitcast.23, bf16[3072,768]{1,0:T(8,128)(2,1)S(1)} %bitcast.22), kind=kOutput, calls=%fused_computation.1 | convolution fusion | flops 7285502976 | bytes 7099392 | tf_op jit(solution)/shard_map/dot_general | solution.py:85
  162.6 0.0 copy-done
  162.6 0.0 copy-start.1
  162.6 1.3 add_log_fusion
  163.9 0.2 log.8
  164.1 0.1 copy.29
  164.3 0.4 convolution_reduce_fusion
  164.7 0.6 multiply_reduce_fusion.2
  166.0 2.2 %multiply_reduce_fusion = f32[2,768]{1,0:T(2,128)S(1)} fusion(f32[768]{0:T(1024)S(1)} %broadcast_multiply_fusion.1, bf16[4,768,768]{2,1,0:T(8,128)(2,1)} %copy-done), kind=kLoop, calls=%fused_computation.13 | loop fusion | flops 3537408 | bytes 2368512 | tf_op jit(solution)/shard_map/reduce_sum | solution.py:84
  168.2 0.2 mul.116
  168.4 0.1 copy.30
  168.6 0.8 copy.31
  169.3 6.8 %all-to-all-start.1 = ((f32[256,1,12]{2,1,0:T(1,128)}), f32[256,1,12]{2,1,0:T(1,128)S(1)}, u32[]{:S(2)}, u32[]{:S(2)}) async-start(f32[256,1,12]{2,1,0:T(1,128)} %copy.31), calls=%async_computation.1 | async-start | bytes 262144 | tf_op jit(solution)/shard_map/all_to_all | solution.py:101
  176.2 0.0 copy-done.1
  176.2 12.9 %all-to-all-done.1 = f32[256,1,12]{2,1,0:T(1,128)S(1)} async-done(((f32[256,1,12]{2,1,0:T(1,128)}), f32[256,1,12]{2,1,0:T(1,128)S(1)}, u32[]{:S(2)}, u32[]{:S(2)}) %all-to-all-start.1) | async-done | bytes 12320 | tf_op jit(solution)/shard_map/all_to_all | solution.py:101
  189.2 0.1 copy.32
  189.2 0.1 copy.33
  189.4 0.1 broadcast_in_dim.115
  189.6 0.1 copy.34
  189.7 0.1 broadcast_in_dim.118
  189.8 2.2 %select_reduce_fusion.2 = (f32[768]{0:T(1024)}, f32[768]{0:T(1024)}) fusion(f32[1536]{0:T(1024)S(1)} %broadcast_in_dim.118, s32[768]{0:T(1024)S(1)} %add_reduce_fusion, f32[1536]{0:T(1024)S(1)} %broadcast_in_dim.115), kind=kLoop, calls=%fused_computation.11 | loop fusion | flops 5896704 | bytes 21504 | tf_op jit(solution)/shard_map/reduce_sum | solution.py:105
  (17 shorter events, 0.1 us)
Async XLA Ops:
  19.6 124.7 %all-to-all-start = ((bf16[4,768,768]{2,0,1:T(4,128)(2,1)}), bf16[4,768,768]{2,0,1:T(4,128)(2,1)}, u32[]{:S(2)}, u32[]{:S(2)}) async-start(bf16[4,768,768]{2,0,1:T(4,128)(2,1)} %copy.26), calls=%async_computation | async-start | bytes 9437184 | tf_op jit(solution)/shard_map/all_to_all | solution.py:69
  147.2 15.4 %copy-start = (bf16[4,768,768]{2,1,0:T(8,128)(2,1)}, bf16[4,768,768]{2,1,0:T(8,128)(2,1)S(1)}, u32[]{:S(2)}) copy-start(bf16[4,768,768]{2,1,0:T(8,128)(2,1)S(1)} %copy.27) | copy-start | bytes 14155780
  162.6 13.6 %copy-start.1 = (s32[768,1]{0,1:T(1,128)S(1)}, s32[768,1]{0,1:T(1,128)}, u32[]{:S(2)}) copy-start(s32[768,1]{0,1:T(1,128)} %param.4) | copy-start | bytes 9220
  169.3 19.8 %all-to-all-start.1 = ((f32[256,1,12]{2,1,0:T(1,128)}), f32[256,1,12]{2,1,0:T(1,128)S(1)}, u32[]{:S(2)}, u32[]{:S(2)}) async-start(f32[256,1,12]{2,1,0:T(1,128)} %copy.31), calls=%async_computation.1 | async-start | bytes 262144 | tf_op jit(solution)/shard_map/all_to_all | solution.py:101

commit v12 on v4

--- a/solution.py
+++ b/solution.py
@@ -65,8 +65,12 @@
     )
     first = jnp.arange(feature_width, dtype=jnp.int32)[None, :] == 0
     send = jnp.where(first & ~present[:, None], EMPTY, picked).astype(jnp.bfloat16)
-    send = send.reshape(pieces, piece_rows, feature_width)
+    split_width = feature_width // 2
+    send = send.reshape(pieces, piece_rows, 2, split_width).transpose(0, 2, 1, 3)
+    send = send.reshape(2 * pieces, piece_rows, split_width)
     arrived = lax.all_to_all(send, axes, split_axis=1, concat_axis=1, tiled=True)
+    arrived = arrived.reshape(pieces, 2, piece_rows, split_width).transpose(0, 2, 1, 3)
+    arrived = arrived.reshape(pieces, piece_rows, feature_width)
     cluster_span = halves * piece_rows
     members = arrived[:halves].reshape(cluster_span, feature_width)
     others = arrived[halves:].reshape(cluster_span, feature_width)

time: 187 us -> 224 us (1.20)
  local copies, waits for them, and re-layouts: 13 us -> 43.1 us
  other arithmetic: 11.2 us -> 17.3 us
    reshape x1 -> x5, local copies, waits for them, and re-layouts: 3.64 us -> 34.1 us  [the longest x2 18.1 us: body(): arrived.reshape(pieces, 2, piece_rows, split_width).transpose(0, 2, 1, 3)]
    reduce_sum x1, other arithmetic: 0.55 us -> 6.57 us  [body(): jnp.sum(members.astype(jnp.float32) * centroid, axis=1)]
where the time goes in v12:
time: 224 us
  blocking collectives  124 us (55%)
  local copies, waits for them, and re-layouts  43.1 us (19%)
  matrix products  17.4 us (8%)
  other arithmetic  17.3 us (8%)
  waiting for transfers between devices  12.9 us (6%)
  starting transfers between devices  6.79 us (3%)
    all_to_all x1, blocking collectives, body(): lax.all_to_all(send, axes, split_axis=1, concat_axis=1, tiled=True)  124 us
    reshape x2, local copies, waits for them, and re-layouts, body(): arrived.reshape(pieces, 2, piece_rows, split_width).transpose(0, 2, 1, 3)  18.1 us
    reshape x2, local copies, waits for them, and re-layouts, body(): send.reshape(pieces, piece_rows, 2, split_width).transpose(0, 2, 1, 3)  13.1 us
    all_to_all x1, waiting for transfers between devices, body(): lax.all_to_all(payload, axes, split_axis=0, concat_axis=0, tiled=True)  12.9 us
    dot_general x1, matrix products, body(): lax.dot_general(chosen.astype(jnp.bfloat16), unit_embed, (((1,), (0,)), (...  6.82 us
    all_to_all x1, starting transfers between devices, body(): lax.all_to_all(payload, axes, split_axis=0, concat_axis=0, tiled=True)  6.79 us
    reduce_sum x1, other arithmetic, body(): jnp.sum(members.astype(jnp.float32) * centroid, axis=1)  6.57 us
    dot_general x1, matrix products, body(): lax.dot_general(members, members, (((1,), (1,)), ((), ())), preferred_ele...  5.85 us
  transfers between devices with their start and end apart: 1, of which 1 were waited for; matrix products, arithmetic and copies ran while one was open for 0% of the time, Pallas kernels for 0%

profile of v12, /device:TPU:1, one launch (start us, length us, event | category | flops | bytes accessed | tf_op | source)
XLA Modules:
  0.0 223.6 jit_solution(2405369054601351825)
XLA Ops:
  0.6 0.0 copy-start.2
  0.6 0.0 copy-start
  0.7 0.9 select_reduce_fusion.5
  1.6 0.7 reduce.3
  2.3 0.4 convert_reduce_fusion
  2.7 1.9 multiply_reduce_fusion.1
  4.6 0.3 select_reduce_fusion.4
  4.9 0.0 copy-done.2
  4.9 0.2 select_reduce_fusion.6
  5.1 0.2 fusion.10
  5.3 0.3 reshape.198
  5.7 0.0 copy-done
  5.7 6.8 %select_convert_fusion = bf16[3072,768]{1,0:T(8,128)(2,1)} fusion(pred[768]{0:T(1024)(128)(4,1)S(1)} %iota_compare_fusion.9, pred[3072]{0:T(1024)(128)(4,1)S(1)} %reshape.198, s32[768]{0:T(1024)S(1)} %get-tuple-element.11, s32[768]{0:T(1024)S(1)} %get-tuple-element.10, f32[768,768]{1,0:T(8,128)S(1)} %copy-done, f32[768]{0:T(1024)S(1)} %add_rsqrt_fusion), kind=kOutput, calls=%fused_computation.4 | convolution fusion | flops 3639214080 | bytes 7090944 | tf_op jit(solution)/shard_map/dot_general | solution.py:60
  12.5 10.1 %reshape.191 = bf16[4,768,2,384]{3,2,1,0:T(2,128)(2,1)} reshape(bf16[3072,768]{1,0:T(8,128)(2,1)} %select_convert_fusion) | data formatting | bytes 9437184 | tf_op jit(solution)/shard_map/reshape | solution.py:69
  22.7 3.0 %copy.20 = bf16[4,768,2,384]{3,1,2,0:T(8,128)(2,1)S(1)} copy(bf16[4,768,2,384]{3,2,1,0:T(2,128)(2,1)} %reshape.191) | data formatting | bytes 9437184 | tf_op jit(solution)/shard_map/reshape | solution.py:69
  25.7 2.8 %copy.21 = bf16[8,768,384]{2,0,1:T(8,128)(2,1)S(1)} copy(bf16[8,768,384]{2,1,0:T(8,128)(2,1)S(1)} %bitcast.36) | data formatting | bytes 9437184 | tf_op jit(solution)/shard_map/reshape | solution.py:70
  28.5 124.5 %all_to_all.14 = bf16[8,768,384]{2,0,1:T(8,128)(2,1)} all-to-all(bf16[8,768,384]{2,0,1:T(8,128)(2,1)S(1)} %copy.21), channel_id=1, replica_groups=mesh['corpus'=32,'group'=8] {'corpus','group'}, dimensions={1} | all-to-all | bytes 9437184 | tf_op jit(solution)/shard_map/all_to_all | solution.py:71
  152.9 10.4 %reshape.193 = bf16[4,2,768,384]{3,1,0,2:T(2,128)(2,1)} reshape(bf16[8,768,384]{2,0,1:T(8,128)(2,1)} %all_to_all.14) | data formatting | bytes 9437184 | tf_op jit(solution)/shard_map/reshape | solution.py:72
  163.3 7.7 %copy.32 = bf16[4,2,768,384]{3,1,2,0:T(2,128)(2,1)} copy(bf16[4,2,768,384]{3,1,0,2:T(2,128)(2,1)} %reshape.193) | data formatting | bytes 9437184 | tf_op jit(solution)/shard_map/reshape | solution.py:72
  171.1 5.6 %fusion.12 = (bf16[2,768,2,384]{3,2,1,0:T(2,128)(2,1)S(1)}, bf16[2,768,2,384]{3,2,1,0:T(2,128)(2,1)S(1)}) fusion(bf16[4,768,2,384]{3,2,1,0:T(2,128)(2,1)} %bitcast.34), kind=kLoop, calls=%fused_computation.57 | loop fusion | bytes 9437184 | tf_op jit(solution)/shard_map/slice | solution.py:76
  176.7 0.5 copy.30
  177.2 0.5 copy.29
  177.7 0.3 compare_reduce_fusion.1
  178.0 0.3 compare_reduce_fusion
  178.2 0.6 convert_reduce_fusion.2
  178.9 4.3 %select_reduce_fusion = f32[1536]{0:T(1024)S(1)} fusion(bf16[1536,768]{1,0:T(8,128)(2,1)S(1)} %bitcast.38, bf16[1536,768]{1,0:T(8,128)(2,1)S(1)} %bitcast.44, pred[1536]{0:T(1024)(128)(4,1)S(1)} %compare_reduce_fusion), kind=kOutput, calls=%fused_computation.2 | convolution fusion | flops 3630955008 | bytes 4726272 | tf_op jit(solution)/shard_map/dot_general | solution.py:92
  183.2 0.7 convert_reduce_fusion.3
  183.9 5.8 %select_reduce_fusion.1 = f32[1536]{0:T(1024)S(1)} fusion(bf16[1536,768]{1,0:T(8,128)(2,1)S(1)} %bitcast.39, pred[1536]{0:T(1024)(128)(4,1)S(1)} %compare_reduce_fusion.1), kind=kOutput, calls=%fused_computation.3 | convolution fusion | flops 3635673600 | bytes 2366976 | tf_op jit(solution)/shard_map/dot_general | solution.py:89
  189.7 0.4 convolution_reduce_fusion
  190.2 0.0 copy-start.1
  190.2 0.6 multiply_reduce_fusion.2
  191.5 6.6 %multiply_reduce_fusion = f32[2,768]{1,0:T(2,128)S(1)} fusion(f32[2,384]{1,0:T(2,128)S(1)} %mul.114, bf16[4,768,2,384]{3,2,1,0:T(2,128)(2,1)} %bitcast.35), kind=kLoop, calls=%fused_computation.14 | loop fusion | flops 3537408 | bytes 2368512 | tf_op jit(solution)/shard_map/reduce_sum | solution.py:88
  198.1 1.3 add_log_fusion
  199.4 0.2 log.8
  199.7 0.1 copy.23
  199.8 0.2 mul.119
  200.0 0.1 copy.24
  200.2 0.8 copy.25
  200.9 6.8 %all-to-all-start.1 = ((f32[256,1,12]{2,1,0:T(1,128)}), f32[256,1,12]{2,1,0:T(1,128)S(1)}, u32[]{:S(2)}, u32[]{:S(2)}) async-start(f32[256,1,12]{2,1,0:T(1,128)} %copy.25), calls=%async_computation.1 | async-start | bytes 262144 | tf_op jit(solution)/shard_map/all_to_all | solution.py:107
  207.7 0.0 copy-done.1
  207.8 12.9 %all-to-all-done.1 = f32[256,1,12]{2,1,0:T(1,128)S(1)} async-done(((f32[256,1,12]{2,1,0:T(1,128)}), f32[256,1,12]{2,1,0:T(1,128)S(1)}, u32[]{:S(2)}, u32[]{:S(2)}) %all-to-all-start.1) | async-done | bytes 12320 | tf_op jit(solution)/shard_map/all_to_all | solution.py:107
  220.7 0.1 copy.26
  220.8 0.1 copy.27
  220.9 0.1 broadcast_in_dim.113
  221.1 0.1 copy.28
  221.2 0.1 broadcast_in_dim.116
  221.4 2.2 select_reduce_fusion.2
  (16 shorter events, 0.1 us)
Async XLA Ops:
  0.6 4.3 %copy-start.2 = (s32[256]{0:T(256)S(1)}, s32[256]{0:T(256)}, u32[]{:S(2)}) copy-start(s32[256]{0:T(256)} %param.5) | copy-start | bytes 3076
  0.6 5.0 %copy-start = (f32[768,768]{1,0:T(8,128)S(1)}, f32[768,768]{1,0:T(8,128)}, u32[]{:S(2)}) copy-start(f32[768,768]{1,0:T(8,128)} %param.3) | copy-start | bytes 7077892
  190.2 17.5 %copy-start.1 = (s32[768,1]{0,1:T(1,128)S(1)}, s32[768,1]{0,1:T(1,128)}, u32[]{:S(2)}) copy-start(s32[768,1]{0,1:T(1,128)} %param.4) | copy-start | bytes 9220
  200.9 19.8 %all-to-all-start.1 = ((f32[256,1,12]{2,1,0:T(1,128)}), f32[256,1,12]{2,1,0:T(1,128)S(1)}, u32[]{:S(2)}, u32[]{:S(2)}) async-start(f32[256,1,12]{2,1,0:T(1,128)} %copy.25), calls=%async_computation.1 | async-start | bytes 262144 | tf_op jit(solution)/shard_map/all_to_all | solution.py:107

commit v13 on v4

--- a/solution.py
+++ b/solution.py
@@ -65,8 +65,9 @@
     )
     first = jnp.arange(feature_width, dtype=jnp.int32)[None, :] == 0
     send = jnp.where(first & ~present[:, None], EMPTY, picked).astype(jnp.bfloat16)
-    send = send.reshape(pieces, piece_rows, feature_width)
-    arrived = lax.all_to_all(send, axes, split_axis=1, concat_axis=1, tiled=True)
+    send = send.reshape(pieces, piece_rows, feature_width).transpose(1, 0, 2)
+    arrived = lax.all_to_all(send, axes, split_axis=0, concat_axis=0, tiled=True)
+    arrived = arrived.transpose(1, 0, 2)
     cluster_span = halves * piece_rows
     members = arrived[:halves].reshape(cluster_span, feature_width)
     others = arrived[halves:].reshape(cluster_span, feature_width)

time: 187 us -> 185 us (0.989)
  local copies, waits for them, and re-layouts: 13 us -> 8.78 us
  other arithmetic: 11.2 us -> 13.4 us
    slice x1, local copies, waits for them, and re-layouts: 4.67 us -> 0.31 us  [body(): others = arrived[halves:].reshape(cluster_span, feature_width)]
where the time goes in v13:
time: 185 us; the launch traced here: 184 us
  blocking collectives  124 us (67%)
  matrix products  16.4 us (9%)
  other arithmetic  13.4 us (7%)
  waiting for transfers between devices  12.9 us (7%)
  local copies, waits for them, and re-layouts  8.78 us (5%)
  starting transfers between devices  6.79 us (4%)
    all_to_all x1, blocking collectives, body(): lax.all_to_all(send, axes, split_axis=0, concat_axis=0, tiled=True)  124 us
    all_to_all x1, waiting for transfers between devices, body(): lax.all_to_all(payload, axes, split_axis=0, concat_axis=0, tiled=True)  12.9 us
    all_to_all x1, starting transfers between devices, body(): lax.all_to_all(payload, axes, split_axis=0, concat_axis=0, tiled=True)  6.79 us
    dot_general x1, matrix products, body(): lax.dot_general(chosen.astype(jnp.bfloat16), unit_embed, (((1,), (0,)), (...  5.92 us
    dot_general x1, matrix products, body(): lax.dot_general(members, members, (((1,), (1,)), ((), ())), preferred_ele...  5.64 us
    dot_general x1, matrix products, body(): lax.dot_general(members, others, (((1,), (1,)), ((), ())), preferred_elem...  4.39 us
  transfers between devices with their start and end apart: 1, of which 1 were waited for; matrix products, arithmetic and copies ran while one was open for 0% of the time, Pallas kernels for 0%

profile of v13, /device:TPU:1, one launch (start us, length us, event | category | flops | bytes accessed | tf_op | source)
XLA Modules:
  0.0 184.3 jit_solution(12115013025248522482)
XLA Ops:
  0.6 0.0 copy-start.1
  0.7 0.9 select_reduce_fusion.5
  1.6 0.7 reduce.3
  2.3 0.4 convert_reduce_fusion
  2.7 0.3 select_reduce_fusion.4
  3.0 0.9 select_reduce_fusion.6
  3.9 0.2 fusion.10
  4.1 0.3 reshape.185
  4.4 1.9 %multiply_reduce_fusion.1 = f32[768]{0:T(1024)S(1)} fusion(f32[768,768]{1,0:T(8,128)} %param.3), kind=kLoop, calls=%fused_computation.20 | loop fusion | flops 1178880 | bytes 2362368 | tf_op jit(solution)/shard_map/reduce_sum | solution.py:17
  6.3 0.0 copy-done.1
  6.4 5.9 %select_convert_fusion = bf16[3072,768]{1,0:T(8,128)(2,1)S(1)} fusion(pred[768]{0:T(1024)(128)(4,1)S(1)} %iota_compare_fusion.9, pred[3072]{0:T(1024)(128)(4,1)S(1)} %reshape.185, s32[768]{0:T(1024)S(1)} %get-tuple-element.11, s32[768]{0:T(1024)S(1)} %get-tuple-element.10, f32[768,768]{1,0:T(8,128)S(1)} %copy-done.1, f32[768]{0:T(1024)S(1)} %add_rsqrt_fusion), kind=kOutput, calls=%fused_computation.4 | convolution fusion | flops 3639214080 | bytes 7090944 | tf_op jit(solution)/shard_map/dot_general | solution.py:60
  12.3 3.6 %copy.37 = bf16[4,768,768]{2,0,1:T(4,128)(2,1)S(1)} copy(bf16[4,768,768]{2,1,0:T(8,128)(2,1)S(1)} %bitcast.36) | data formatting | bytes 9437184 | tf_op jit(solution)/shard_map/reshape | solution.py:68
  15.9 124.4 %all_to_all.14 = bf16[768,4,768]{2,1,0:T(4,128)(2,1)S(1)} all-to-all(bf16[768,4,768]{2,1,0:T(4,128)(2,1)S(1)} %bitcast.31), channel_id=1, replica_groups=mesh['corpus'=32,'group'=8] {'corpus','group'}, dimensions={0} | all-to-all | bytes 9437184 | tf_op jit(solution)/shard_map/all_to_all | solution.py:69
  140.3 0.6 copy.36
  140.9 0.0 copy-start
  140.9 0.3 fusion.12
  141.2 1.8 copy-done
  143.0 0.3 compare_reduce_fusion.1
  143.3 5.6 %select_reduce_fusion.1 = f32[1536]{0:T(1024)S(1)} fusion(bf16[1536,768]{1,0:T(8,128)(2,1)S(1)} %bitcast.33, pred[1536]{0:T(1024)(128)(4,1)S(1)} %compare_reduce_fusion.1), kind=kOutput, calls=%fused_computation.3 | convolution fusion | flops 3635673600 | bytes 2366976 | tf_op jit(solution)/shard_map/dot_general | solution.py:86
  148.9 0.6 convert_reduce_fusion.3
  149.5 0.3 compare_reduce_fusion
  149.8 4.4 %select_reduce_fusion = f32[1536]{0:T(1024)S(1)} fusion(bf16[1536,768]{1,0:T(8,128)(2,1)S(1)} %bitcast.34, bf16[1536,768]{1,0:T(8,128)(2,1)S(1)} %bitcast.38, pred[1536]{0:T(1024)(128)(4,1)S(1)} %compare_reduce_fusion), kind=kOutput, calls=%fused_computation.2 | convolution fusion | flops 3630955008 | bytes 4726272 | tf_op jit(solution)/shard_map/dot_general | solution.py:89
  154.2 0.6 convert_reduce_fusion.2
  154.9 1.3 add_log_fusion
  156.2 0.2 log.8
  156.4 0.1 copy.28
  156.5 0.0 copy-start.2
  156.5 0.4 convolution_reduce_fusion
  156.9 0.6 multiply_reduce_fusion.2
  158.2 2.2 %multiply_reduce_fusion = f32[2,768]{1,0:T(2,128)S(1)} fusion(f32[768]{0:T(1024)S(1)} %broadcast_multiply_fusion.1, bf16[4,768,768]{2,1,0:T(8,128)(2,1)} %bitcast.30), kind=kLoop, calls=%fused_computation.15 | loop fusion | flops 3537408 | bytes 2368512 | tf_op jit(solution)/shard_map/reduce_sum | solution.py:85
  160.5 0.2 mul.116
  160.7 0.1 copy.29
  160.8 0.8 copy.30
  161.6 6.8 %all-to-all-start.1 = ((f32[256,1,12]{2,1,0:T(1,128)}), f32[256,1,12]{2,1,0:T(1,128)S(1)}, u32[]{:S(2)}, u32[]{:S(2)}) async-start(f32[256,1,12]{2,1,0:T(1,128)} %copy.30), calls=%async_computation.1 | async-start | bytes 262144 | tf_op jit(solution)/shard_map/all_to_all | solution.py:104
  168.4 0.0 copy-done.2
  168.4 12.9 %all-to-all-done.1 = f32[256,1,12]{2,1,0:T(1,128)S(1)} async-done(((f32[256,1,12]{2,1,0:T(1,128)}), f32[256,1,12]{2,1,0:T(1,128)S(1)}, u32[]{:S(2)}, u32[]{:S(2)}) %all-to-all-start.1) | async-done | bytes 12320 | tf_op jit(solution)/shard_map/all_to_all | solution.py:104
  181.4 0.1 copy.31
  181.5 0.1 copy.32
  181.6 0.1 broadcast_in_dim.113
  181.8 0.1 copy.33
  181.9 0.1 broadcast_in_dim.116
  182.0 2.2 %select_reduce_fusion.2 = (f32[768]{0:T(1024)}, f32[768]{0:T(1024)}) fusion(f32[1536]{0:T(1024)S(1)} %broadcast_in_dim.116, s32[768]{0:T(1024)S(1)} %add_reduce_fusion, f32[1536]{0:T(1024)S(1)} %broadcast_in_dim.113), kind=kLoop, calls=%fused_computation.13 | loop fusion | flops 5896704 | bytes 21504 | tf_op jit(solution)/shard_map/reduce_sum | solution.py:108
  (15 shorter events, 0.1 us)
Async XLA Ops:
  0.6 5.7 %copy-start.1 = (f32[768,768]{1,0:T(8,128)S(1)}, f32[768,768]{1,0:T(8,128)}, u32[]{:S(2)}) copy-start(f32[768,768]{1,0:T(8,128)} %param.3) | copy-start | bytes 7077892
  140.9 2.1 %copy-start = (bf16[768,4,768]{2,0,1:T(8,128)(2,1)}, bf16[768,4,768]{2,0,1:T(8,128)(2,1)S(1)}, u32[]{:S(2)}) copy-start(bf16[768,4,768]{2,0,1:T(8,128)(2,1)S(1)} %copy.36) | copy-start | bytes 14155780
  156.5 11.9 %copy-start.2 = (s32[768,1]{0,1:T(1,128)S(1)}, s32[768,1]{0,1:T(1,128)}, u32[]{:S(2)}) copy-start(s32[768,1]{0,1:T(1,128)} %param.4) | copy-start | bytes 9220
  161.6 19.8 %all-to-all-start.1 = ((f32[256,1,12]{2,1,0:T(1,128)}), f32[256,1,12]{2,1,0:T(1,128)S(1)}, u32[]{:S(2)}, u32[]{:S(2)}) async-start(f32[256,1,12]{2,1,0:T(1,128)} %copy.30), calls=%async_computation.1 | async-start | bytes 262144 | tf_op jit(solution)/shard_map/all_to_all | solution.py:104

commit v14 on v9

--- a/solution.py
+++ b/solution.py
@@ -1,7 +1,6 @@
 import jax
 import jax.numpy as jnp
 from jax import lax
-from jax.experimental.layout import Layout, with_layout_constraint
 from jax.sharding import PartitionSpec as P
 
 MOST = 6
@@ -47,19 +46,22 @@
     half = row_slot // PIECE
     member_pos = half * piece_rows + row_label * PIECE + within
     near_pos = (halves + half) * piece_rows + near_label * PIECE + within
-    slot_ids = jnp.arange(pieces * piece_rows, dtype=jnp.int32).reshape(pieces, piece_rows)
+    slot_ids = (
+        lax.broadcasted_iota(jnp.int32, (piece_rows, pieces), 1) * piece_rows
+        + lax.broadcasted_iota(jnp.int32, (piece_rows, pieces), 0)
+    )
     chosen = (member_pos[None, None, :] == slot_ids[:, :, None]) | (
         near_pos[None, None, :] == slot_ids[:, :, None]
     )
-    shape3 = (pieces, clusters, PIECE)
-    piece_at = lax.broadcasted_iota(jnp.int32, shape3, 0)
-    k_at = lax.broadcasted_iota(jnp.int32, shape3, 2)
+    shape3 = (clusters, PIECE, pieces)
+    piece_at = lax.broadcasted_iota(jnp.int32, shape3, 2)
+    k_at = lax.broadcasted_iota(jnp.int32, shape3, 1)
     have = jnp.where(
         piece_at < halves,
-        jnp.broadcast_to(local_count[None, :, None], shape3),
-        jnp.broadcast_to(near_count[None, :, None], shape3),
+        jnp.broadcast_to(local_count[:, None, None], shape3),
+        jnp.broadcast_to(near_count[:, None, None], shape3),
     )
-    present = (have > (piece_at % halves) * PIECE + k_at).reshape(pieces, piece_rows)
+    present = (have > (piece_at % halves) * PIECE + k_at).reshape(piece_rows, pieces)
     picked = lax.dot_general(
         chosen.astype(jnp.bfloat16),
         unit_embed,
@@ -68,8 +70,8 @@
     )
     first = jnp.arange(feature_width, dtype=jnp.int32)[None, None, :] == 0
     send = jnp.where(first & ~present[:, :, None], EMPTY, picked).astype(jnp.bfloat16)
-    send = with_layout_constraint(send, Layout(major_to_minor=(1, 0, 2)))
-    arrived = lax.all_to_all(send, axes, split_axis=1, concat_axis=1, tiled=True)
+    arrived = lax.all_to_all(send, axes, split_axis=0, concat_axis=0, tiled=True)
+    arrived = arrived.transpose(1, 0, 2)
     cluster_span = halves * piece_rows
     members = arrived[:halves].reshape(cluster_span, feature_width)
     others = arrived[halves:].reshape(cluster_span, feature_width)

time: 197 us -> 184 us (0.934)
  other arithmetic: 24.2 us -> 13.4 us
    convert_element_type x1 -> x0, other arithmetic: 8.91 us -> none  [body(): jnp.where(first & ~present[:, :, None], EMPTY, picked).astype(jnp.bfloat16)]
    slice x2 -> x1, local copies, waits for them, and re-layouts: 5.79 us -> 0.31 us  [body(): others = arrived[halves:].reshape(cluster_span, feature_width)]
    convert_element_type x0 -> x1, local copies, waits for them, and re-layouts: none -> 3.64 us  [body(): jnp.where(first & ~present[:, :, None], EMPTY, picked).astype(jnp.bfloat16)]
    reduce_sum x1, other arithmetic: 4.86 us -> 2.21 us  [body(): jnp.sum(members.astype(jnp.float32) * centroid, axis=1)]
where the time goes in v14:
time: 184 us
  blocking collectives  124 us (67%)
  matrix products  15.6 us (8%)
  other arithmetic  13.4 us (7%)
  waiting for transfers between devices  12.9 us (7%)
  local copies, waits for them, and re-layouts  9.25 us (5%)
  starting transfers between devices  6.82 us (4%)
    all_to_all x1, blocking collectives, body(): lax.all_to_all(send, axes, split_axis=0, concat_axis=0, tiled=True)  124 us
    all_to_all x1, waiting for transfers between devices, body(): lax.all_to_all(payload, axes, split_axis=0, concat_axis=0, tiled=True)  12.9 us
    all_to_all x1, starting transfers between devices, body(): lax.all_to_all(payload, axes, split_axis=0, concat_axis=0, tiled=True)  6.82 us
    dot_general x1, matrix products, body(): lax.dot_general(members, members, (((1,), (1,)), ((), ())), preferred_ele...  5.64 us
    dot_general x1, matrix products, body(): lax.dot_general(chosen.astype(jnp.bfloat16), unit_embed, (((2,), (0,)), (...  5.14 us
    dot_general x1, matrix products, body(): lax.dot_general(members, others, (((1,), (1,)), ((), ())), preferred_elem...  4.38 us
  transfers between devices with their start and end apart: 1, of which 1 were waited for; matrix products, arithmetic and copies ran while one was open for 0% of the time, Pallas kernels for 0%

profile of v14, /device:TPU:1, one launch (start us, length us, event | category | flops | bytes accessed | tf_op | source)
XLA Modules:
  0.0 184.0 jit_solution(10015241888198335848)
XLA Ops:
  0.6 0.0 copy-start.1
  0.7 0.9 select_reduce_fusion.5
  1.6 0.7 reduce.3
  2.3 0.4 convert_reduce_fusion
  2.7 0.3 select_reduce_fusion.4
  3.0 0.9 select_reduce_fusion.6
  3.9 0.1 broadcast_in_dim.117
  4.0 0.2 broadcast_in_dim.118
  4.2 0.1 broadcast_in_dim.112
  4.3 0.2 broadcast_in_dim.113
  4.5 0.2 iota.80
  4.7 0.1 iota_add_fusion
  4.8 1.9 %multiply_reduce_fusion.1 = f32[768]{0:T(1024)S(1)} fusion(f32[768,768]{1,0:T(8,128)} %param.3), kind=kLoop, calls=%fused_computation.20 | loop fusion | flops 1178880 | bytes 2362368 | tf_op jit(solution)/shard_map/reduce_sum | solution.py:17
  6.7 0.1 fusion.14
  6.8 0.0 copy-done.1
  6.8 5.1 %select_convert_fusion = bf16[768,4,768]{2,0,1:T(8,128)(2,1)S(1)} fusion(pred[768,4]{0,1:T(4,128)(4,1)S(1)} %fusion.14, pred[768]{0:T(1024)(128)(4,1)S(1)} %iota_compare_fusion.6, s32[768]{0:T(1024)S(1)} %get-tuple-element.11, s32[768,4]{0,1:T(4,128)S(1)} %iota_add_fusion, s32[768]{0:T(1024)S(1)} %get-tuple-element.10, f32[768,768]{1,0:T(8,128)S(1)} %copy-done.1, ...), kind=kOutput, calls=%fused_computation.4 | convolution fusion | flops 3639214080 | bytes 7103232 | tf_op jit(solution)/shard_map/dot_general | solution.py:65
  12.0 3.6 %copy.26 = bf16[768,4,768]{2,1,0:T(4,128)(2,1)S(1)} copy(bf16[768,4,768]{2,0,1:T(8,128)(2,1)S(1)} %select_convert_fusion) | data formatting | bytes 9437184 | tf_op jit(solution)/shard_map/convert_element_type | solution.py:72
  15.6 124.4 %all_to_all.14 = bf16[768,4,768]{2,1,0:T(4,128)(2,1)S(1)} all-to-all(bf16[768,4,768]{2,1,0:T(4,128)(2,1)S(1)} %copy.26), channel_id=1, replica_groups=mesh['corpus'=32,'group'=8] {'corpus','group'}, dimensions={0} | all-to-all | bytes 9437184 | tf_op jit(solution)/shard_map/all_to_all | solution.py:73
  140.0 0.6 copy.35
  140.6 0.0 copy-start
  140.6 0.3 fusion.16
  140.9 1.8 copy-done
  142.7 0.3 compare_reduce_fusion.1
  143.0 5.6 %select_reduce_fusion.1 = f32[1536]{0:T(1024)S(1)} fusion(bf16[1536,768]{1,0:T(8,128)(2,1)S(1)} %bitcast.31, pred[1536]{0:T(1024)(128)(4,1)S(1)} %compare_reduce_fusion.1), kind=kOutput, calls=%fused_computation.3 | convolution fusion | flops 3635673600 | bytes 2366976 | tf_op jit(solution)/shard_map/dot_general | solution.py:90
  148.6 0.6 convert_reduce_fusion.3
  149.2 0.3 compare_reduce_fusion
  149.5 4.4 %select_reduce_fusion = f32[1536]{0:T(1024)S(1)} fusion(bf16[1536,768]{1,0:T(8,128)(2,1)S(1)} %bitcast.32, bf16[1536,768]{1,0:T(8,128)(2,1)S(1)} %bitcast.35, pred[1536]{0:T(1024)(128)(4,1)S(1)} %compare_reduce_fusion), kind=kOutput, calls=%fused_computation.2 | convolution fusion | flops 3630955008 | bytes 4726272 | tf_op jit(solution)/shard_map/dot_general | solution.py:93
  153.9 0.6 convert_reduce_fusion.2
  154.5 1.3 add_log_fusion
  155.8 0.2 log.8
  156.0 0.1 copy.28
  156.2 0.0 copy-start.2
  156.2 0.4 convolution_reduce_fusion
  156.6 0.6 multiply_reduce_fusion.2
  157.9 2.2 %multiply_reduce_fusion = f32[2,768]{1,0:T(2,128)S(1)} fusion(f32[768]{0:T(1024)S(1)} %broadcast_multiply_fusion.1, bf16[4,768,768]{2,1,0:T(8,128)(2,1)} %bitcast.29), kind=kLoop, calls=%fused_computation.14 | loop fusion | flops 3537408 | bytes 2368512 | tf_op jit(solution)/shard_map/reduce_sum | solution.py:89
  160.1 0.2 mul.126
  160.4 0.1 copy.29
  160.5 0.8 copy.30
  161.3 6.8 %all-to-all-start.1 = ((f32[256,1,12]{2,1,0:T(1,128)}), f32[256,1,12]{2,1,0:T(1,128)S(1)}, u32[]{:S(2)}, u32[]{:S(2)}) async-start(f32[256,1,12]{2,1,0:T(1,128)} %copy.30), calls=%async_computation.1 | async-start | bytes 262144 | tf_op jit(solution)/shard_map/all_to_all | solution.py:108
  168.1 0.0 copy-done.2
  168.1 12.9 %all-to-all-done.1 = f32[256,1,12]{2,1,0:T(1,128)S(1)} async-done(((f32[256,1,12]{2,1,0:T(1,128)}), f32[256,1,12]{2,1,0:T(1,128)S(1)}, u32[]{:S(2)}, u32[]{:S(2)}) %all-to-all-start.1) | async-done | bytes 12320 | tf_op jit(solution)/shard_map/all_to_all | solution.py:108
  181.1 0.1 copy.31
  181.1 0.1 copy.32
  181.3 0.1 broadcast_in_dim.125
  181.5 0.1 copy.33
  181.6 0.1 broadcast_in_dim.128
  181.7 2.2 %select_reduce_fusion.2 = (f32[768]{0:T(1024)}, f32[768]{0:T(1024)}) fusion(f32[1536]{0:T(1024)S(1)} %broadcast_in_dim.128, s32[768]{0:T(1024)S(1)} %add_reduce_fusion, f32[1536]{0:T(1024)S(1)} %broadcast_in_dim.125), kind=kLoop, calls=%fused_computation.12 | loop fusion | flops 5896704 | bytes 21504 | tf_op jit(solution)/shard_map/reduce_sum | solution.py:112
  (17 shorter events, 0.1 us)
Async XLA Ops:
  0.6 6.2 %copy-start.1 = (f32[768,768]{1,0:T(8,128)S(1)}, f32[768,768]{1,0:T(8,128)}, u32[]{:S(2)}) copy-start(f32[768,768]{1,0:T(8,128)} %param.3) | copy-start | bytes 7077892
  140.6 2.1 %copy-start = (bf16[768,4,768]{2,0,1:T(8,128)(2,1)}, bf16[768,4,768]{2,0,1:T(8,128)(2,1)S(1)}, u32[]{:S(2)}) copy-start(bf16[768,4,768]{2,0,1:T(8,128)(2,1)S(1)} %copy.35) | copy-start | bytes 14155780
  156.2 11.9 %copy-start.2 = (s32[768,1]{0,1:T(1,128)S(1)}, s32[768,1]{0,1:T(1,128)}, u32[]{:S(2)}) copy-start(s32[768,1]{0,1:T(1,128)} %param.4) | copy-start | bytes 9220
  161.3 19.8 %all-to-all-start.1 = ((f32[256,1,12]{2,1,0:T(1,128)}), f32[256,1,12]{2,1,0:T(1,128)S(1)}, u32[]{:S(2)}, u32[]{:S(2)}) async-start(f32[256,1,12]{2,1,0:T(1,128)} %copy.30), calls=%async_computation.1 | async-start | bytes 262144 | tf_op jit(solution)/shard_map/all_to_all | solution.py:108

commit v15 on v14

--- a/solution.py
+++ b/solution.py
@@ -86,7 +86,13 @@
         preferred_element_type=jnp.float32,
     )
     centroid = normalize(sums)
-    typical = TYPICAL_SCALE * jnp.sum(members.astype(jnp.float32) * centroid, axis=1)
+    typical = TYPICAL_SCALE * lax.dot_general(
+        members.astype(jnp.float32),
+        centroid[0],
+        (((1,), (0,)), ((), ())),
+        precision=lax.Precision.HIGHEST,
+        preferred_element_type=jnp.float32,
+    )
     g_own = lax.dot_general(
         members, members, (((1,), (1,)), ((), ())), preferred_element_type=jnp.float32
     )

time: 184 us -> 182 us (0.989)
  other arithmetic: 13.4 us -> 10.7 us
  matrix products: 15.6 us -> 17.5 us
    reduce_sum x1 -> x0, other arithmetic: 2.21 us -> none  [body(): jnp.sum(members.astype(jnp.float32) * centroid, axis=1)]
    dot_general x0 -> x1, matrix products: none -> 1.94 us  [body(): lax.dot_general(members.astype(jnp.float32), centroid[0], (((1,), (0,)),...]
where the time goes in v15:
time: 182 us; the launch traced here: 181 us
  blocking collectives  124 us (68%)
  matrix products  17.5 us (10%)
  waiting for transfers between devices  12.9 us (7%)
  other arithmetic  10.7 us (6%)
  local copies, waits for them, and re-layouts  7.45 us (4%)
  starting transfers between devices  6.79 us (4%)
    all_to_all x1, blocking collectives, body(): lax.all_to_all(send, axes, split_axis=0, concat_axis=0, tiled=True)  124 us
    all_to_all x1, waiting for transfers between devices, body(): lax.all_to_all(payload, axes, split_axis=0, concat_axis=0, tiled=True)  12.9 us
    all_to_all x1, starting transfers between devices, body(): lax.all_to_all(payload, axes, split_axis=0, concat_axis=0, tiled=True)  6.79 us
    dot_general x1, matrix products, body(): lax.dot_general(members, members, (((1,), (1,)), ((), ())), preferred_ele...  5.64 us
    dot_general x1, matrix products, body(): lax.dot_general(chosen.astype(jnp.bfloat16), unit_embed, (((2,), (0,)), (...  5.13 us
    dot_general x1, matrix products, body(): lax.dot_general(members, others, (((1,), (1,)), ((), ())), preferred_elem...  4.37 us
    convert_element_type x1, local copies, waits for them, and re-layouts, body(): jnp.where(first & ~present[:, :, None], EMPTY, picked).astype(jnp.bfloat16)  3.64 us
  transfers between devices with their start and end apart: 1, of which 1 were waited for; matrix products, arithmetic and copies ran while one was open for 0% of the time, Pallas kernels for 0%

profile of v15, /device:TPU:1, one launch (start us, length us, event | category | flops | bytes accessed | tf_op | source)
XLA Modules:
  0.0 181.3 jit_solution(10989399365303626407)
XLA Ops:
  0.6 0.0 copy-start.2
  0.6 0.0 copy-start
  0.7 0.9 select_reduce_fusion.5
  1.6 0.7 reduce.2
  2.4 0.4 convert_reduce_fusion
  2.7 1.9 %multiply_reduce_fusion = f32[768]{0:T(1024)S(1)} fusion(f32[768,768]{1,0:T(8,128)} %param.3), kind=kLoop, calls=%fused_computation.19 | loop fusion | flops 1178880 | bytes 2362368 | tf_op jit(solution)/shard_map/reduce_sum | solution.py:17
  4.6 0.3 select_reduce_fusion.4
  4.9 0.0 copy-done.2
  4.9 0.2 select_reduce_fusion.6
  5.1 0.1 iota_add_fusion
  5.2 0.1 broadcast_in_dim.112
  5.3 0.2 broadcast_in_dim.113
  5.5 0.1 broadcast_in_dim.117
  5.6 0.2 broadcast_in_dim.118
  5.8 0.2 iota.80
  6.1 0.1 fusion.14
  6.1 0.0 copy-done
  6.2 5.1 %select_convert_fusion = bf16[768,4,768]{2,0,1:T(8,128)(2,1)S(1)} fusion(pred[768,4]{0,1:T(4,128)(4,1)S(1)} %fusion.14, pred[768]{0:T(1024)(128)(4,1)S(1)} %iota_compare_fusion.6, s32[768]{0:T(1024)S(1)} %get-tuple-element.11, s32[768,4]{0,1:T(4,128)S(1)} %iota_add_fusion, s32[768]{0:T(1024)S(1)} %get-tuple-element.10, f32[768,768]{1,0:T(8,128)S(1)} %copy-done, ...), kind=kOutput, calls=%fused_computation.4 | convolution fusion | flops 3639214080 | bytes 7103232 | tf_op jit(solution)/shard_map/dot_general | solution.py:65
  11.3 3.6 %copy.26 = bf16[768,4,768]{2,1,0:T(4,128)(2,1)S(1)} copy(bf16[768,4,768]{2,0,1:T(8,128)(2,1)S(1)} %select_convert_fusion) | data formatting | bytes 9437184 | tf_op jit(solution)/shard_map/convert_element_type | solution.py:72
  14.9 124.4 %all_to_all.14 = bf16[768,4,768]{2,1,0:T(4,128)(2,1)S(1)} all-to-all(bf16[768,4,768]{2,1,0:T(4,128)(2,1)S(1)} %copy.26), channel_id=1, replica_groups=mesh['corpus'=32,'group'=8] {'corpus','group'}, dimensions={0} | all-to-all | bytes 9437184 | tf_op jit(solution)/shard_map/all_to_all | solution.py:73
  139.3 0.6 copy.35
  139.9 0.3 fusion.16
  140.2 0.3 compare_reduce_fusion.1
  140.5 0.3 compare_reduce_fusion
  140.8 0.6 convert_reduce_fusion.2
  141.4 4.4 %select_reduce_fusion = f32[1536]{0:T(1024)S(1)} fusion(bf16[1536,768]{1,0:T(8,128)(2,1)S(1)} %bitcast.31, bf16[1536,768]{1,0:T(8,128)(2,1)S(1)} %bitcast.37, pred[1536]{0:T(1024)(128)(4,1)S(1)} %compare_reduce_fusion), kind=kOutput, calls=%fused_computation.2 | convolution fusion | flops 3630955008 | bytes 4726272 | tf_op jit(solution)/shard_map/dot_general | solution.py:99
  145.8 0.7 convert_reduce_fusion.3
  146.5 5.6 %select_reduce_fusion.1 = f32[1536]{0:T(1024)S(1)} fusion(bf16[1536,768]{1,0:T(8,128)(2,1)S(1)} %bitcast.32, pred[1536]{0:T(1024)(128)(4,1)S(1)} %compare_reduce_fusion.1), kind=kOutput, calls=%fused_computation.3 | convolution fusion | flops 3635673600 | bytes 2366976 | tf_op jit(solution)/shard_map/dot_general | solution.py:96
  152.1 0.4 convolution_reduce_fusion.1
  152.6 0.0 copy-start.1
  152.6 0.6 multiply_reduce_fusion.1
  153.9 1.9 %convolution_reduce_fusion = f32[1536]{0:T(1024)S(1)} fusion(bf16[1536,768]{1,0:T(8,128)(2,1)S(1)} %bitcast.34, f32[768,1]{0,1:T(1,128)S(1)} %reshape.236), kind=kOutput, calls=%fused_computation.25 | convolution fusion | flops 14155776 | bytes 2368512 | tf_op jit(solution)/shard_map/dot_general | solution.py:89
  155.8 0.2 reshape.231
  156.1 0.1 copy.29
  156.2 1.4 add_log_fusion
  157.5 0.2 log.8
  157.8 0.1 copy.28
  157.9 0.8 copy.30
  158.7 6.8 %all-to-all-start.1 = ((f32[256,1,12]{2,1,0:T(1,128)}), f32[256,1,12]{2,1,0:T(1,128)S(1)}, u32[]{:S(2)}, u32[]{:S(2)}) async-start(f32[256,1,12]{2,1,0:T(1,128)} %copy.30), calls=%async_computation.1 | async-start | bytes 262144 | tf_op jit(solution)/shard_map/all_to_all | solution.py:114
  165.5 0.0 copy-done.1
  165.5 12.9 %all-to-all-done.1 = f32[256,1,12]{2,1,0:T(1,128)S(1)} async-done(((f32[256,1,12]{2,1,0:T(1,128)}), f32[256,1,12]{2,1,0:T(1,128)S(1)}, u32[]{:S(2)}, u32[]{:S(2)}) %all-to-all-start.1) | async-done | bytes 12320 | tf_op jit(solution)/shard_map/all_to_all | solution.py:114
  178.4 0.1 copy.31
  178.5 0.1 copy.32
  178.7 0.1 broadcast_in_dim.125
  178.8 0.1 copy.33
  179.0 0.1 broadcast_in_dim.128
  179.1 2.2 %select_reduce_fusion.2 = (f32[768]{0:T(1024)}, f32[768]{0:T(1024)}) fusion(f32[1536]{0:T(1024)S(1)} %broadcast_in_dim.128, s32[768]{0:T(1024)S(1)} %add_reduce_fusion, f32[1536]{0:T(1024)S(1)} %broadcast_in_dim.125), kind=kLoop, calls=%fused_computation.12 | loop fusion | flops 5896704 | bytes 21504 | tf_op jit(solution)/shard_map/reduce_sum | solution.py:118
  (18 shorter events, 0.1 us)
Async XLA Ops:
  0.6 4.3 %copy-start.2 = (s32[256]{0:T(256)S(1)}, s32[256]{0:T(256)}, u32[]{:S(2)}) copy-start(s32[256]{0:T(256)} %param.5) | copy-start | bytes 3076
  0.6 5.5 %copy-start = (f32[768,768]{1,0:T(8,128)S(1)}, f32[768,768]{1,0:T(8,128)}, u32[]{:S(2)}) copy-start(f32[768,768]{1,0:T(8,128)} %param.3) | copy-start | bytes 7077892
  152.6 12.9 %copy-start.1 = (s32[768,1]{0,1:T(1,128)S(1)}, s32[768,1]{0,1:T(1,128)}, u32[]{:S(2)}) copy-start(s32[768,1]{0,1:T(1,128)} %param.4) | copy-start | bytes 9220
  158.7 19.8 %all-to-all-start.1 = ((f32[256,1,12]{2,1,0:T(1,128)}), f32[256,1,12]{2,1,0:T(1,128)S(1)}, u32[]{:S(2)}, u32[]{:S(2)}) async-start(f32[256,1,12]{2,1,0:T(1,128)} %copy.30), calls=%async_computation.1 | async-start | bytes 262144 | tf_op jit(solution)/shard_map/all_to_all | solution.py:114
